TPU v7x, 32 devices: a whole 2x2x4 slice. The times are simulated.
32 devices in a mesh: pool: 8 (over z, x), tp: 4 (over y, core).
Axes of the slice: x: 2, y: 2, z: 4, core: 2. Of those that a mesh axis runs over, the one named last changes fastest.
Arguments:
- draft_states: bfloat16 [1024, 8192], P(None, 'pool'), may hold values from -12 to 12
- w_qkv: bfloat16 [8192, 10240], P('pool', 'tp'), may hold values from -0.0625 to 0.0625
- w_out: bfloat16 [8192, 8192], P('tp', 'pool'), may hold values from -0.0625 to 0.0625
- kv_pool: bfloat16 [640, 128, 2048], P('pool', None, 'tp'), may hold values from -58 to 58
- resident_kv: bfloat16 [16, 8, 128, 2048], P('pool', None, None, 'tp'), may hold values from -58 to 58
- page_owner: int32 [16, 32], replicated, may hold values from 0 to 7, as said below
- page_slot: int32 [16, 32], replicated, may hold values from 0 to 79, as said below
- hist_len: int32 [16], replicated, may hold values from 3073 to 4096, as said below
- res_count: int32 [16], replicated, may hold values from 0 to 8, as said below
- parents: int32 [16, 64], replicated, may hold values from -1 to 62, as said below
Outputs:
- layer_out: bfloat16 [1024, 8192], P('tp', 'pool')
Inputs may be any that keep to these rules, and one draw needn't show every extreme that they name: `page_owner`: among the 64 entries of the users of one pool index, one owner is named 16 times, one owner is never named, and every other owner 16 / 2 times; each owner is the most named one for exactly one pool index. No pair (page_owner, page_slot) is named twice. `hist_len`: some user's history has exactly 4096 tokens. res_count[u] is at most the page count ceil(hist_len[u] / 128) of user u; some user has exactly 8. parents[u, i] lies between i - 4 and i - 1 and is -1 where that is negative; parents[u, 0] = -1 and parents[u, 63] = 62.
All inputs are finite; a program needn't handle non-finite values.
Results may differ from a plain program's by a relative error of at most 0.013.
The roundings to bfloat16 on the way count: a program that leaves them out, or rounds other values in their place, can miss the bound.
Values may be sent and summed in bfloat16 or wider, within the bound.
No kernel may reach another device: no remote copies, remote signals or barrier semaphores. Data moves between devices by JAX's collectives and lax.ppermute only.
A program may use at most 192 MiB of HBM per device.

v0:
```python
import math

import jax
import jax.numpy as jnp
from jax import lax
from jax.sharding import PartitionSpec as P

H = 64
KVH = 8
HD = 128
DRAFT = 64
PAGE = 128
MAXP = 32
MAXRES = 8
USER_DEV = 2


ROPE_BASE = 500000.0
NEG_FILL = -1e30


def ancestry_of(parents):
    users_count, draft_len = parents.shape

    def visit_token(step_index, ancestry):
        parent_ids = parents[:, step_index]
        parent_rows = ancestry[jnp.arange(users_count), jnp.maximum(parent_ids, 0)]
        own_row = (jnp.arange(draft_len) == step_index).astype(jnp.float32)
        new_row = own_row[None, :] + jnp.where((parent_ids >= 0)[:, None], parent_rows, 0.0)
        return ancestry.at[:, step_index, :].set(new_row)

    return lax.fori_loop(
        0, draft_len, visit_token, jnp.zeros((users_count, draft_len, draft_len), jnp.float32)
    )


def rotate(vectors, positions):
    half_size = vectors.shape[-1] // 2
    frequencies = jnp.exp(
        jnp.arange(half_size).astype(jnp.float32) * (-2.0 * math.log(ROPE_BASE) / vectors.shape[-1])
    )
    angles = positions[..., None] * frequencies
    cosines = jnp.cos(angles)
    sines = jnp.sin(angles)
    lower_half = vectors[..., :half_size]
    upper_half = vectors[..., half_size:]
    return jnp.concatenate(
        [lower_half * cosines - upper_half * sines, upper_half * cosines + lower_half * sines], -1
    )


def merge_block(running, scores, usable, value_rows):
    row_max, denominator, weighted = running
    new_max = jnp.maximum(row_max, jnp.max(jnp.where(usable, scores, NEG_FILL), axis=-1))
    shrink = jnp.exp(row_max - new_max)
    weight = jnp.where(usable, jnp.exp(scores - new_max[..., None]), 0.0)
    denominator = denominator * shrink + jnp.sum(weight, axis=-1)
    weighted = weighted * shrink[..., None] + jnp.einsum(
        "krs,skd->krd", weight.astype(jnp.bfloat16), value_rows, preferred_element_type=jnp.float32
    )
    return (new_max, denominator, weighted)


def attend(queries, source, page_index, page_number, page_usable, length, running):
    page_count = page_index.shape[0]
    page_size = source.shape[1]
    per_block = math.gcd(page_count, max(1, 512 // page_size))
    heads_kv = queries.shape[0]
    head_dim = queries.shape[2]
    score_scale = head_dim ** (-0.5)

    def visit_block(running, block_index):
        page_ids = lax.dynamic_slice_in_dim(page_index, block_index * per_block, per_block)
        numbers = lax.dynamic_slice_in_dim(page_number, block_index * per_block, per_block)
        allowed = lax.dynamic_slice_in_dim(page_usable, block_index * per_block, per_block)
        page_data = source[page_ids].reshape(per_block * page_size, heads_kv, 2, head_dim)
        scores = (
            jnp.einsum(
                "krd,skd->krs", queries, page_data[:, :, 0], preferred_element_type=jnp.float32
            )
            * score_scale
        )
        places = numbers[:, None] * page_size + jnp.arange(page_size)[None, :]
        usable = (allowed[:, None] & (places < length)).reshape(-1)
        return (merge_block(running, scores, usable[None, None, :], page_data[:, :, 1]), None)

    running, unused = lax.scan(visit_block, running, jnp.arange(page_count // per_block))
    return running


def add_draft(running, queries, draft_key, draft_value, visible):
    score_scale = queries.shape[2] ** (-0.5)
    scores = (
        jnp.einsum("krd,jkd->krj", queries, draft_key, preferred_element_type=jnp.float32)
        * score_scale
    )
    return merge_block(running, scores, visible[None], draft_value)


def finish(running, draft_len):
    row_max, denominator, weighted = running
    heads_kv, row_count, head_dim = weighted.shape
    result = weighted / denominator[..., None]
    result = result.reshape(heads_kv, draft_len, row_count // draft_len, head_dim).transpose(
        1, 0, 2, 3
    )
    return result.reshape(draft_len, heads_kv * row_count // draft_len * head_dim).astype(
        jnp.bfloat16
    )


def body(
    draft_states,
    w_qkv,
    w_out,
    kv_pool,
    resident_kv,
    page_owner,
    page_slot,
    hist_len,
    res_count,
    parents,
):
    pool_size = lax.axis_size("pool")
    my_index = lax.axis_index("pool")
    group_size = H // KVH
    local_cols = w_qkv.shape[1]
    heads_kv = local_cols // ((group_size + 2) * HD)
    projected = lax.psum_scatter(
        jnp.dot(draft_states, w_qkv, preferred_element_type=jnp.float32),
        "pool",
        scatter_dimension=0,
        tiled=True,
    )
    projected = projected.reshape(USER_DEV, DRAFT, heads_kv, group_size + 2, HD)
    first_user = my_index * USER_DEV
    my_lengths = lax.dynamic_slice_in_dim(hist_len, first_user, USER_DEV)
    my_resident = lax.dynamic_slice_in_dim(res_count, first_user, USER_DEV)
    my_parents = lax.dynamic_slice_in_dim(parents, first_user, USER_DEV, 0)
    ancestry = ancestry_of(my_parents)
    positions = my_lengths.astype(jnp.float32)[:, None] + jnp.sum(ancestry, -1) - 1.0
    queries = rotate(projected[:, :, :, :group_size], positions[:, :, None, None]).astype(
        jnp.bfloat16
    )
    draft_key = rotate(projected[:, :, :, group_size], positions[:, :, None]).astype(jnp.bfloat16)
    draft_value = projected[:, :, :, group_size + 1].astype(jnp.bfloat16)
    row_count = DRAFT * group_size
    query_rows = queries.transpose(0, 2, 1, 3, 4).reshape(USER_DEV, heads_kv, row_count, HD)
    visible = jnp.repeat(ancestry > 0.5, group_size, axis=1)
    block_rows = USER_DEV * MAXP
    capacity = 2 * block_rows // pool_size
    kv_cols = kv_pool.shape[2]
    owner_blocks = page_owner.reshape(pool_size, block_rows)
    slot_blocks = page_slot.reshape(pool_size, block_rows)
    one_hot = (owner_blocks[:, :, None] == jnp.arange(pool_size)[None, None, :]).astype(jnp.int32)
    slot_ranks = jnp.sum((jnp.cumsum(one_hot, axis=1) - one_hot) * one_hot, axis=2)
    targets = jnp.arange(pool_size)[:, None] * capacity + slot_ranks
    send_to = jnp.where(owner_blocks == my_index, targets, pool_size * capacity).reshape(-1)
    pack_index = (
        jnp.zeros((pool_size * capacity,), jnp.int32)
        .at[send_to]
        .set(slot_blocks.reshape(-1), mode="drop")
    )
    local_source = resident_kv.reshape(USER_DEV * MAXRES, PAGE, kv_cols)
    outputs = []
    packed = kv_pool[pack_index]
    arrived = lax.all_to_all(packed, "pool", split_axis=0, concat_axis=0, tiled=True)
    source = jnp.concatenate([local_source, arrived], 0)
    my_owner = lax.dynamic_index_in_dim(owner_blocks, my_index, 0, keepdims=False).reshape(
        USER_DEV, MAXP
    )
    my_rank = lax.dynamic_index_in_dim(slot_ranks, my_index, 0, keepdims=False).reshape(
        USER_DEV, MAXP
    )
    numbers = jnp.arange(MAXP)
    for local_user in range(USER_DEV):
        page_index = jnp.where(
            numbers < my_resident[local_user],
            local_user * MAXRES + jnp.minimum(numbers, MAXRES - 1),
            USER_DEV * MAXRES + my_owner[local_user] * capacity + my_rank[local_user],
        )
        running = attend(
            query_rows[local_user],
            source,
            page_index,
            numbers,
            jnp.ones((MAXP,), bool),
            my_lengths[local_user],
            (
                jnp.full((heads_kv, row_count), NEG_FILL, jnp.float32),
                jnp.zeros((heads_kv, row_count), jnp.float32),
                jnp.zeros((heads_kv, row_count, HD), jnp.float32),
            ),
        )
        running = add_draft(
            running,
            query_rows[local_user],
            draft_key[local_user],
            draft_value[local_user],
            visible[local_user],
        )
        outputs.append(finish(running, DRAFT))
    attention = jnp.concatenate(outputs, 0)
    partial_out = jnp.dot(
        lax.all_gather(attention, "pool", axis=0, tiled=True),
        w_out,
        preferred_element_type=jnp.float32,
    )
    return lax.psum_scatter(partial_out.astype(jnp.bfloat16), "tp", scatter_dimension=0, tiled=True)


def solution(mesh):
    in_specs = (
        P(None, "pool"),
        P("pool", "tp"),
        P("tp", "pool"),
        P("pool", None, "tp"),
        P("pool", None, None, "tp"),
        P(),
        P(),
        P(),
        P(),
        P(),
    )
    out_specs = P("tp", "pool")
    return jax.shard_map(body, mesh=mesh, in_specs=in_specs, out_specs=out_specs, check_vma=False)
```

profile of v0, /device:TPU:0, one launch (start us, length us, event | category | flops | bytes accessed | tf_op | source)
XLA Modules:
  0.0 875.3 jit_solution(8432410539029704304)
XLA Ops:
  13.2 12.0 %gather_fusion.3 = bf16[128,128,512]{2,1,0:T(8,128)(2,1)} fusion(bf16[80,128,512]{2,1,0:T(8,128)(2,1)} %param.21, s32[1024]{0:T(1024)S(1)} %pad_clamp_fusion.2), kind=kCustom, calls=%fused_computation.3 | custom fusion | bytes 33554944 | tf_op jit(solution)/shard_map/gather | solution.py:166
  25.2 7.3 all-to-all-start
  32.6 10.6 %fusion.66 = f32[1024,2560]{1,0:T(8,128)} fusion(bf16[1024,1024]{1,0:T(8,128)(2,1)S(1)} %copy-done, bf16[1024,2560]{1,0:T(8,128)(2,1)} %param.19), kind=kOutput, calls=%fused_computation.159 | convolution fusion | flops 5368709120 | bytes 17825792 | tf_op jit(solution)/shard_map/dot_general | solution.py:130
  44.2 138.5 %while.44 = (s32[]{:T(128)}, f32[2,64,64]{2,1,0:T(8,128)S(1)}, s32[2,64]{0,1:T(8,128)S(1)}, s32[]{:T(128)}, s32[3]{0:T(128)S(1)}, /*index=5*/s32[1]{0:T(128)}, s32[]{:T(128)}) while((s32[]{:T(128)}, f32[2,64,64]{2,1,0:T(8,128)S(1)}, s32[2,64]{0,1:T(8,128)S(1)}, s32[]{:T(128)}, s32[3]{0:T(128)S(1)}, /*index=5*/s32[1]{0:T(128)}, ...), condition=%wide.region_6.7_spmd, body=%wide.region_4.0_spmd.sunk | while | flops 545 | bytes 69803 | solution.py:32
  186.4 337.0 %reduce-scatter.3.cloned.1.call-done = f32[128,2560]{1,0:T(8,128)} async-done(((f32[1024,2560]{1,0:T(8,128)}), f32[128,2560]{1,0:T(8,128)}) %reduce-scatter.3.cloned.1.call-update) | async-done | bytes 1310736 | tf_op jit(solution)/shard_map/reduce_scatter | solution.py:129
  529.0 14.9 %pad_maximum_fusion = bf16[144,128,512]{2,1,0:T(8,128)(2,1)} fusion(bf16[128,128,512]{2,1,0:T(8,128)(2,1)} %all-to-all-done, bf16[16,128,512]{2,1,0:T(8,128)(2,1)} %bitcast.147), kind=kLoop, calls=%fused_computation.63 | loop fusion | flops 9437184 | bytes 37748736 | tf_op jit(solution)/shard_map/concatenate | solution.py:168
  543.9 102.9 %while.46 = (s32[]{:T(128)}, f32[2,512]{1,0:T(2,128)S(1)}, f32[2,512]{1,0:T(2,128)S(1)}, f32[2,512,128]{2,1,0:T(8,128)}, s32[8]{0:T(128)S(1)}, /*index=5*/s32[32...) while((s32[]{:T(128)}, f32[2,512]{1,0:T(2,128)S(1)}, ...), condition=%wide.region_17.18_spmd.clone, body=%wide.region_14.17_spmd.clone.sunk | while | flops 274603008 | bytes 15538563 | solution.py:87
  545.7 6.9 gather_fusion.2
  558.6 6.9 gather_fusion.2
  571.5 6.9 gather_fusion.2
  584.3 6.9 gather_fusion.2
  597.2 6.9 gather_fusion.2
  610.1 6.9 gather_fusion.2
  622.9 6.9 gather_fusion.2
  635.8 6.9 gather_fusion.2
  648.6 104.9 %while.45 = (s32[]{:T(128)}, f32[2,512]{1,0:T(2,128)S(1)}, f32[2,512]{1,0:T(2,128)S(1)}, f32[2,512,128]{2,1,0:T(8,128)}, s32[8]{0:T(128)S(1)}, /*index=5*/s32[32...) while((s32[]{:T(128)}, f32[2,512]{1,0:T(2,128)S(1)}, ...), condition=%wide.region_11.12_spmd.clone, body=%wide.region_8.11_spmd.clone.sunk | while | flops 274603008 | bytes 15538563 | solution.py:87
  650.7 6.9 gather_fusion.1
  663.8 6.9 gather_fusion.1
  690.0 6.9 gather_fusion.1
  716.3 6.9 gather_fusion.1
  729.4 6.9 gather_fusion.1
  757.4 72.0 %all-gather.2.cloned.1.call-done = bf16[1024,2048]{1,0:T(8,128)(2,1)} async-done(((bf16[128,2048]{1,0:T(8,128)(2,1)}), bf16[1024,2048]{1,0:T(8,128)(2,1)}) %all-gather.2.cloned.1.call-update) | async-done | bytes 4194320 | tf_op jit(solution)/shard_map/all_gather | solution.py:205
  829.4 9.4 %convolution_convert_fusion = bf16[1024,1024]{1,0:T(8,128)(2,1)} fusion(bf16[1024,2048]{1,0:T(8,128)(2,1)} %all-gather.2.cloned.1.call-done, bf16[2048,1024]{1,0:T(8,128)(2,1)} %param.20), kind=kOutput, calls=%fused_computation.64 | convolution fusion | flops 4296015872 | bytes 10485760 | tf_op jit(solution)/shard_map/dot_general | solution.py:204
  838.9 29.9 %reduce-scatter.5.cloned.1.call-done = bf16[256,1024]{1,0:T(8,128)(2,1)} async-done(((bf16[1024,1024]{1,0:T(8,128)(2,1)}), bf16[256,1024]{1,0:T(8,128)(2,1)}) %reduce-scatter.5.cloned.1.call-update) | async-done | bytes 524304 | tf_op jit(solution)/shard_map/reduce_scatter | solution.py:209
  (854 shorter events, 265.7 us)
Async XLA Ops:
  6.5 26.0 %copy-start = (bf16[1024,1024]{1,0:T(8,128)(2,1)S(1)}, bf16[1024,1024]{1,0:T(8,128)(2,1)}, u32[]{:S(2)}) copy-start(bf16[1024,1024]{1,0:T(8,128)(2,1)} %param.18) | copy-start | bytes 6291460
  25.2 503.8 %all-to-all-start = ((bf16[128,128,512]{2,1,0:T(8,128)(2,1)}), bf16[128,128,512]{2,1,0:T(8,128)(2,1)}, u32[]{:S(2)}, u32[]{:S(2)}) async-start(bf16[128,128,512]{2,1,0:T(8,128)(2,1)} %gather_fusion.3), calls=%async_computation | async-start | bytes 33554432 | tf_op jit(solution)/shard_map/all_to_all | solution.py:167
  32.5 491.0 %reduce-scatter.3.cloned.1.call-start = ((), (), s32[]{:S(2)}) async-start(), calls=%async_computation.3 | async-start | bytes 11796480 | tf_op jit(solution)/shard_map/reduce_scatter | solution.py:129
  43.1 1.1 copy-start.2
  43.1 139.6 %copy-start.4 = (s32[16]{0:T(128)S(1)}, s32[16]{0:T(128)}, u32[]{:S(2)}) copy-start(s32[16]{0:T(128)} %param.26) | copy-start | bytes 196
  43.1 140.4 %copy-start.3 = (s32[16]{0:T(128)S(1)}, s32[16]{0:T(128)}, u32[]{:S(2)}) copy-start(s32[16]{0:T(128)} %param.25) | copy-start | bytes 196
  43.1 786.3 %all-gather.2.cloned.1.call-start = ((), (), s32[]{:S(2)}) async-start(), calls=%async_computation.4 | async-start | bytes 4718592 | tf_op jit(solution)/shard_map/all_gather | solution.py:205
  554.0 1.0 copy-start.7
  566.9 1.0 copy-start.7
  579.8 1.0 copy-start.7
  592.6 1.0 copy-start.7
  605.5 1.0 copy-start.7
  618.4 1.0 copy-start.7
  631.2 1.0 copy-start.7
  644.1 1.0 copy-start.7
  659.0 1.0 copy-start.5
  672.1 1.0 copy-start.5
  685.2 1.0 copy-start.5
  711.5 1.0 copy-start.5
  724.6 1.0 copy-start.5
  737.7 1.0 copy-start.5
  750.8 1.0 copy-start.5
  757.2 111.6 %reduce-scatter.5.cloned.1.call-start = ((), (), s32[]{:S(2)}) async-start(), calls=%async_computation.5 | async-start | bytes 2621440 | tf_op jit(solution)/shard_map/reduce_scatter | solution.py:209
  829.4 39.3 %copy-start.1 = (bf16[1024,1024]{1,0:T(8,128)(2,1)S(1)}, bf16[1024,1024]{1,0:T(8,128)(2,1)}, u32[]{:S(2)}) copy-start(bf16[1024,1024]{1,0:T(8,128)(2,1)} %param.18) | copy-start | bytes 6291460
  (17 other events, 13.8 us)
Sparse Core Ops, SparseCore 0:
  43.3 480.1 reduce-scatter.2
  757.3 72.0 all-gather.1
  839.0 29.7 reduce-scatter.4
where the time goes:
time: 878 us; the launch traced here: 875 us
  waiting for transfers between devices  439 us (50%)
  local copies, waits for them, and re-layouts  219 us (25%)
  other arithmetic  137 us (16%)
  matrix products  45.9 us (5%)
  between operations  13.4 us (2%)
  loops' own time  12.8 us (1%)
    reduce_scatter x1, waiting for transfers between devices, body(): lax.psum_scatter(jnp.dot(draft_states, w_qkv, preferred_element_type=jnp....  337 us
    gather x16, local copies, waits for them, and re-layouts, visit_block(): source[page_ids].reshape(per_block * page_size, heads_kv, 2, head_dim)  111 us
    another operation x130, other arithmetic  93.7 us
    all_gather x1, waiting for transfers between devices, body(): lax.all_gather(attention, 'pool', axis=0, tiled=True)  72 us
    gather x64, local copies, waits for them, and re-layouts, visit_token(): parent_rows = ancestry[jnp.arange(users_count), jnp.maximum(parent_ids, 0)]  36.5 us
    reduce_scatter x1, waiting for transfers between devices, body(): lax.psum_scatter(partial_out.astype(jnp.bfloat16), 'tp', scatter_dimensio...  29.9 us
    while x80, local copies, waits for them, and re-layouts  21.2 us
  transfers between devices with their start and end apart: 4, of which 3 were waited for; matrix products, arithmetic and copies ran while one was open for 18% of the time, Pallas kernels for 0%

commit v1 on v0

v1 whole, which is shorter than its diff:
```python
import math

import jax
import jax.numpy as jnp
from jax import lax
from jax.sharding import PartitionSpec as P

H = 64
KVH = 8
HD = 128
DRAFT = 64
PAGE = 128
MAXP = 32
MAXRES = 8
USER_DEV = 2


ROPE_BASE = 500000.0


def ancestry_of(parents):
    users_count, draft_len = parents.shape
    tokens = jnp.arange(draft_len)
    reach = (parents[:, :, None] == tokens[None, None, :]).astype(jnp.float32)
    reach = reach + (tokens[:, None] == tokens[None, :]).astype(jnp.float32)[None]
    for unused in range(max(1, math.ceil(math.log2(draft_len)))):
        reach = jnp.minimum(
            jnp.einsum(
                "uij,ujk->uik",
                reach.astype(jnp.bfloat16),
                reach.astype(jnp.bfloat16),
                preferred_element_type=jnp.float32,
            ),
            1.0,
        )
    return reach


def rotate(vectors, positions):
    half_size = vectors.shape[-1] // 2
    frequencies = jnp.exp(
        jnp.arange(half_size).astype(jnp.float32) * (-2.0 * math.log(ROPE_BASE) / vectors.shape[-1])
    )
    angles = positions[..., None] * frequencies
    cosines = jnp.cos(angles)
    sines = jnp.sin(angles)
    lower_half = vectors[..., :half_size]
    upper_half = vectors[..., half_size:]
    return jnp.concatenate(
        [lower_half * cosines - upper_half * sines, upper_half * cosines + lower_half * sines], -1
    )


def attend_dense(queries, history, draft_key, draft_value, visible, length):
    heads_kv, row_count, head_dim = queries.shape
    score_scale = head_dim ** (-0.5)
    hist_scores = (
        jnp.einsum("krd,skd->krs", queries, history[:, :, 0], preferred_element_type=jnp.float32)
        * score_scale
    )
    draft_scores = (
        jnp.einsum("krd,jkd->krj", queries, draft_key, preferred_element_type=jnp.float32)
        * score_scale
    )
    hist_ok = (jnp.arange(history.shape[0]) < length)[None, None, :]
    draft_ok = visible[None]
    row_max = jnp.maximum(
        jnp.max(jnp.where(hist_ok, hist_scores, -jnp.inf), -1),
        jnp.max(jnp.where(draft_ok, draft_scores, -jnp.inf), -1),
    )
    hist_weight = jnp.where(hist_ok, jnp.exp(hist_scores - row_max[..., None]), 0.0)
    draft_weight = jnp.where(draft_ok, jnp.exp(draft_scores - row_max[..., None]), 0.0)
    denominator = jnp.sum(hist_weight, -1) + jnp.sum(draft_weight, -1)
    weighted = jnp.einsum(
        "krs,skd->krd",
        hist_weight.astype(jnp.bfloat16),
        history[:, :, 1],
        preferred_element_type=jnp.float32,
    ) + jnp.einsum(
        "krj,jkd->krd",
        draft_weight.astype(jnp.bfloat16),
        draft_value,
        preferred_element_type=jnp.float32,
    )
    return weighted / denominator[..., None]


def finish(result, draft_len):
    heads_kv, row_count, head_dim = result.shape
    result = result.reshape(heads_kv, draft_len, row_count // draft_len, head_dim).transpose(
        1, 0, 2, 3
    )
    return result.reshape(draft_len, heads_kv * row_count // draft_len * head_dim).astype(
        jnp.bfloat16
    )


def body(
    draft_states,
    w_qkv,
    w_out,
    kv_pool,
    resident_kv,
    page_owner,
    page_slot,
    hist_len,
    res_count,
    parents,
):
    pool_size = lax.axis_size("pool")
    my_index = lax.axis_index("pool")
    group_size = H // KVH
    local_cols = w_qkv.shape[1]
    heads_kv = local_cols // ((group_size + 2) * HD)
    projected = lax.psum_scatter(
        jnp.dot(draft_states, w_qkv, preferred_element_type=jnp.float32),
        "pool",
        scatter_dimension=0,
        tiled=True,
    )
    projected = projected.reshape(USER_DEV, DRAFT, heads_kv, group_size + 2, HD)
    first_user = my_index * USER_DEV
    my_lengths = lax.dynamic_slice_in_dim(hist_len, first_user, USER_DEV)
    my_resident = lax.dynamic_slice_in_dim(res_count, first_user, USER_DEV)
    my_parents = lax.dynamic_slice_in_dim(parents, first_user, USER_DEV, 0)
    ancestry = ancestry_of(my_parents)
    positions = my_lengths.astype(jnp.float32)[:, None] + jnp.sum(ancestry, -1) - 1.0
    queries = rotate(projected[:, :, :, :group_size], positions[:, :, None, None]).astype(
        jnp.bfloat16
    )
    draft_key = rotate(projected[:, :, :, group_size], positions[:, :, None]).astype(jnp.bfloat16)
    draft_value = projected[:, :, :, group_size + 1].astype(jnp.bfloat16)
    row_count = DRAFT * group_size
    query_rows = queries.transpose(0, 2, 1, 3, 4).reshape(USER_DEV, heads_kv, row_count, HD)
    visible = jnp.repeat(ancestry > 0.5, group_size, axis=1)
    block_rows = USER_DEV * MAXP
    capacity = 2 * block_rows // pool_size
    kv_cols = kv_pool.shape[2]
    owner_blocks = page_owner.reshape(pool_size, block_rows)
    slot_blocks = page_slot.reshape(pool_size, block_rows)
    one_hot = (owner_blocks[:, :, None] == jnp.arange(pool_size)[None, None, :]).astype(jnp.int32)
    slot_ranks = jnp.sum((jnp.cumsum(one_hot, axis=1) - one_hot) * one_hot, axis=2)
    targets = jnp.arange(pool_size)[:, None] * capacity + slot_ranks
    send_to = jnp.where(owner_blocks == my_index, targets, pool_size * capacity).reshape(-1)
    pack_index = (
        jnp.zeros((pool_size * capacity,), jnp.int32)
        .at[send_to]
        .set(slot_blocks.reshape(-1), mode="drop")
    )
    local_source = resident_kv.reshape(USER_DEV * MAXRES, PAGE, kv_cols)
    outputs = []
    packed = kv_pool[pack_index]
    arrived = lax.all_to_all(packed, "pool", split_axis=0, concat_axis=0, tiled=True)
    my_owner = lax.dynamic_index_in_dim(owner_blocks, my_index, 0, keepdims=False).reshape(
        USER_DEV, MAXP
    )
    my_rank = lax.dynamic_index_in_dim(slot_ranks, my_index, 0, keepdims=False).reshape(
        USER_DEV, MAXP
    )
    numbers = jnp.arange(MAXP)
    for local_user in range(USER_DEV):
        resident_pages = local_source[local_user * MAXRES + jnp.minimum(numbers, MAXRES - 1)]
        pool_pages = arrived[my_owner[local_user] * capacity + my_rank[local_user]]
        history = jnp.where(
            (numbers < my_resident[local_user])[:, None, None], resident_pages, pool_pages
        ).reshape(MAXP * PAGE, heads_kv, 2, HD)
        result = attend_dense(
            query_rows[local_user],
            history,
            draft_key[local_user],
            draft_value[local_user],
            visible[local_user],
            my_lengths[local_user],
        )
        outputs.append(finish(result, DRAFT))
    attention = jnp.concatenate(outputs, 0)
    partial_out = jnp.dot(
        lax.all_gather(attention, "pool", axis=0, tiled=True),
        w_out,
        preferred_element_type=jnp.float32,
    )
    return lax.psum_scatter(partial_out.astype(jnp.bfloat16), "tp", scatter_dimension=0, tiled=True)


def solution(mesh):
    in_specs = (
        P(None, "pool"),
        P("pool", "tp"),
        P("tp", "pool"),
        P("pool", None, "tp"),
        P("pool", None, None, "tp"),
        P(),
        P(),
        P(),
        P(),
        P(),
    )
    out_specs = P("tp", "pool")
    return jax.shard_map(body, mesh=mesh, in_specs=in_specs, out_specs=out_specs, check_vma=False)
```

time: 878 us -> 734 us (0.84)
  local copies, waits for them, and re-layouts: 219 us -> 72.4 us
  waiting for transfers between devices: 439 us -> 555 us
  other arithmetic: 137 us -> 32.7 us
  loops' own time: 12.8 us -> 0 us
    reduce_scatter x1, waiting for transfers between devices: 337 us -> 453 us  [body(): lax.psum_scatter(jnp.dot(draft_states, w_qkv, preferred_element_type=jnp....]
    gather x80 -> x8, local copies, waits for them, and re-layouts: 148 us -> 50.7 us  [the longest x4 30.9 us: body(): pool_pages = arrived[my_owner[local_user] * capacity + my_rank[local_user]]]
    another operation x130 -> x2, other arithmetic: 93.7 us -> 0.61 us
    while x80 -> x0, local copies, waits for them, and re-layouts: 21.2 us -> none
    concatenate x65 -> x0, other arithmetic: 15.8 us -> none  [the longest x1 14.9 us: body(): source = jnp.concatenate([local_source, arrived], 0)]
    another operation x3 -> x0, loops' own time: 12.8 us -> none  [the longest x2 10.9 us: attend(): lax.scan(visit_block, running, jnp.arange(page_count // per_block))]
    slice x16 -> x0, local copies, waits for them, and re-layouts: 11.7 us -> none  [visit_block(): page_data[:, :, 1]]
    dynamic_slice x16 -> x0, local copies, waits for them, and re-layouts: 9.08 us -> none  [attend(): lax.scan(visit_block, running, jnp.arange(page_count // per_block))]
  transfers between devices with their start and end apart: 4 -> 4, of which waited for: 3 -> 3; matrix products, arithmetic and copies ran while one was open for 18% -> 6% of each run, Pallas kernels for 0% -> 0%
where the time goes in v1:
time: 734 us; the launch traced here: 733 us
  waiting for transfers between devices  555 us (76%)
  local copies, waits for them, and re-layouts  72.4 us (10%)
  matrix products  51.4 us (7%)
  other arithmetic  32.7 us (4%)
  between operations  13.5 us (2%)
  starting transfers between devices  7.58 us (1%)
    reduce_scatter x1, waiting for transfers between devices, body(): lax.psum_scatter(jnp.dot(draft_states, w_qkv, preferred_element_type=jnp....  453 us
    all_gather x1, waiting for transfers between devices, body(): lax.all_gather(attention, 'pool', axis=0, tiled=True)  71.9 us
    gather x4, local copies, waits for them, and re-layouts, body(): pool_pages = arrived[my_owner[local_user] * capacity + my_rank[local_user]]  30.9 us
    reduce_scatter x1, waiting for transfers between devices, body(): lax.psum_scatter(partial_out.astype(jnp.bfloat16), 'tp', scatter_dimensio...  29.9 us
    gather x4, local copies, waits for them, and re-layouts, body(): local_source[local_user * MAXRES + jnp.minimum(numbers, MAXRES - 1)]  19.7 us
    reduce_sum x4, other arithmetic, attend_dense(): denominator = jnp.sum(hist_weight, -1) + jnp.sum(draft_weight, -1)  16.2 us
  transfers between devices with their start and end apart: 4, of which 3 were waited for; matrix products, arithmetic and copies ran while one was open for 6% of the time, Pallas kernels for 0%

profile of v1, /device:TPU:0, one launch (start us, length us, event | category | flops | bytes accessed | tf_op | source)
XLA Modules:
  0.0 732.6 jit_solution(341258270010901477)
XLA Ops:
  10.7 2.4 scatter_custom_fusion
  13.2 12.0 %gather_fusion.1 = bf16[128,128,512]{2,1,0:T(8,128)(2,1)} fusion(bf16[80,128,512]{2,1,0:T(8,128)(2,1)} %param.13, s32[1024]{0:T(1024)S(1)} %pad_clamp_fusion.3), kind=kCustom, calls=%fused_computation.1 | custom fusion | bytes 33554944 | tf_op jit(solution)/shard_map/gather | solution.py:152
  25.2 7.3 all-to-all-start
  32.6 10.9 %fusion.85 = f32[1024,2560]{1,0:T(8,128)} fusion(bf16[1024,1024]{1,0:T(8,128)(2,1)} %param.10, bf16[1024,2560]{1,0:T(8,128)(2,1)} %param.11), kind=kOutput, calls=%fused_computation.162 | convolution fusion | flops 5368709120 | bytes 17825792 | tf_op jit(solution)/shard_map/dot_general | solution.py:116
  43.8 2.9 gather_fusion.3
  46.7 7.1 reshape.361
  55.9 2.8 gather_fusion
  58.7 6.9 reshape.359
  70.6 453.2 %reduce-scatter.3.cloned.1.call-done = f32[128,2560]{1,0:T(8,128)} async-done(((f32[1024,2560]{1,0:T(8,128)}), f32[128,2560]{1,0:T(8,128)}) %reduce-scatter.3.cloned.1.call-update) | async-done | bytes 1310736 | tf_op jit(solution)/shard_map/reduce_scatter | solution.py:115
  527.7 8.6 %gather_fusion.4 = bf16[32,128,512]{2,1,0:T(8,128)(2,1)} fusion(bf16[128,128,512]{2,1,0:T(8,128)(2,1)} %all-to-all-done, s32[1024]{0:T(1024)S(1)} %pad_clamp_fusion), kind=kCustom, calls=%fused_computation.4 | custom fusion | bytes 8388736 | tf_op jit(solution)/shard_map/gather | solution.py:163
  536.3 6.9 reshape.362
  543.2 4.6 copy_select_fusion
  547.8 7.0 select_reduce_fusion
  554.9 7.3 fusion.4
  562.2 8.0 %fusion.2 = f32[2,512]{1,0:T(2,128)S(1)} fusion(f32[2,512,4096]{2,1,0:T(8,128)} %get-tuple-element.26, f32[2,512]{1,0:T(2,128)S(1)} %max.15, pred[4096]{0:T(1024)(128)(4,1)S(1)} %iota_compare_fusion.4), kind=kLoop, calls=%fused_computation.12 | loop fusion | flops 16776192 | bytes 16789504 | tf_op jit(solution)/shard_map/reduce_sum | solution.py:73
  570.2 8.5 %gather_fusion.2 = bf16[32,128,512]{2,1,0:T(8,128)(2,1)} fusion(bf16[128,128,512]{2,1,0:T(8,128)(2,1)} %all-to-all-done, s32[1024]{0:T(1024)S(1)} %pad_clamp_fusion.2), kind=kCustom, calls=%fused_computation.2 | custom fusion | bytes 8388736 | tf_op jit(solution)/shard_map/gather | solution.py:163
  578.7 6.9 reshape.360
  585.6 4.6 copy_select_fusion.1
  590.2 7.3 select_reduce_fusion.1
  597.5 7.3 fusion.6
  604.8 8.0 %fusion = f32[2,512]{1,0:T(2,128)S(1)} fusion(f32[2,512,4096]{2,1,0:T(8,128)} %get-tuple-element.30, f32[2,512]{1,0:T(2,128)S(1)} %max.14, pred[4096]{0:T(1024)(128)(4,1)S(1)} %iota_compare_fusion.5), kind=kLoop, calls=%fused_computation.10 | loop fusion | flops 16776192 | bytes 16789504 | tf_op jit(solution)/shard_map/reduce_sum | solution.py:73
  614.9 71.9 %all-gather.2.cloned.1.call-done = bf16[1024,2048]{1,0:T(8,128)(2,1)} async-done(((bf16[128,2048]{1,0:T(8,128)(2,1)}), bf16[1024,2048]{1,0:T(8,128)(2,1)}) %all-gather.2.cloned.1.call-update) | async-done | bytes 4194320 | tf_op jit(solution)/shard_map/all_gather | solution.py:178
  686.8 9.4 %convolution_convert_fusion = bf16[1024,1024]{1,0:T(8,128)(2,1)} fusion(bf16[1024,2048]{1,0:T(8,128)(2,1)} %all-gather.2.cloned.1.call-done, bf16[2048,1024]{1,0:T(8,128)(2,1)} %param.12), kind=kOutput, calls=%fused_computation.26 | convolution fusion | flops 4296015872 | bytes 10485760 | tf_op jit(solution)/shard_map/dot_general | solution.py:177
  696.2 29.9 %reduce-scatter.5.cloned.1.call-done = bf16[256,1024]{1,0:T(8,128)(2,1)} async-done(((bf16[1024,1024]{1,0:T(8,128)(2,1)}), bf16[256,1024]{1,0:T(8,128)(2,1)}) %reduce-scatter.5.cloned.1.call-update) | async-done | bytes 524304 | tf_op jit(solution)/shard_map/reduce_scatter | solution.py:182
  (82 shorter events, 17.3 us)
Async XLA Ops:
  6.5 37.2 %copy-start = (bf16[2,8,128,512]{3,2,1,0:T(8,128)(2,1)S(1)}, bf16[2,8,128,512]{3,2,1,0:T(8,128)(2,1)}, u32[]{:S(2)}) copy-start(bf16[2,8,128,512]{3,2,1,0:T(8,128)(2,1)} %param.14) | copy-start | bytes 6291460
  25.2 502.5 %all-to-all-start = ((bf16[128,128,512]{2,1,0:T(8,128)(2,1)}), bf16[128,128,512]{2,1,0:T(8,128)(2,1)}, u32[]{:S(2)}, u32[]{:S(2)}) async-start(bf16[128,128,512]{2,1,0:T(8,128)(2,1)} %gather_fusion.1), calls=%async_computation.1 | async-start | bytes 33554432 | tf_op jit(solution)/shard_map/all_to_all | solution.py:153
  32.5 491.3 %reduce-scatter.3.cloned.1.call-start = ((), (), s32[]{:S(2)}) async-start(), calls=%async_computation.3 | async-start | bytes 11796480 | tf_op jit(solution)/shard_map/reduce_scatter | solution.py:115
  43.5 643.3 %all-gather.2.cloned.1.call-start = ((), (), s32[]{:S(2)}) async-start(), calls=%async_computation.4 | async-start | bytes 4718592 | tf_op jit(solution)/shard_map/all_gather | solution.py:178
  46.7 7.1 copy-start.3
  58.7 9.3 %copy-start.2 = (s32[16]{0:T(128)S(1)}, s32[16]{0:T(128)}, u32[]{:S(2)}) copy-start(s32[16]{0:T(128)} %param.17) | copy-start | bytes 196
  614.8 111.3 %reduce-scatter.5.cloned.1.call-start = ((), (), s32[]{:S(2)}) async-start(), calls=%async_computation.5 | async-start | bytes 2621440 | tf_op jit(solution)/shard_map/reduce_scatter | solution.py:182
  686.8 39.3 %copy-start.1 = (bf16[2,8,128,512]{3,2,1,0:T(8,128)(2,1)S(1)}, bf16[2,8,128,512]{3,2,1,0:T(8,128)(2,1)}, u32[]{:S(2)}) copy-start(bf16[2,8,128,512]{3,2,1,0:T(8,128)(2,1)} %param.14) | copy-start | bytes 6291460
Sparse Core Ops, SparseCore 0:
  43.6 480.1 reduce-scatter.2
  614.9 71.7 all-gather.1
  696.3 29.7 reduce-scatter.4

commit v2 on v1

--- a/solution.py
+++ b/solution.py
@@ -54,35 +54,41 @@
 def attend_dense(queries, history, draft_key, draft_value, visible, length):
     heads_kv, row_count, head_dim = queries.shape
     score_scale = head_dim ** (-0.5)
-    hist_scores = (
-        jnp.einsum("krd,skd->krs", queries, history[:, :, 0], preferred_element_type=jnp.float32)
-        * score_scale
-    )
-    draft_scores = (
-        jnp.einsum("krd,jkd->krj", queries, draft_key, preferred_element_type=jnp.float32)
-        * score_scale
-    )
-    hist_ok = (jnp.arange(history.shape[0]) < length)[None, None, :]
-    draft_ok = visible[None]
-    row_max = jnp.maximum(
-        jnp.max(jnp.where(hist_ok, hist_scores, -jnp.inf), -1),
-        jnp.max(jnp.where(draft_ok, draft_scores, -jnp.inf), -1),
-    )
-    hist_weight = jnp.where(hist_ok, jnp.exp(hist_scores - row_max[..., None]), 0.0)
-    draft_weight = jnp.where(draft_ok, jnp.exp(draft_scores - row_max[..., None]), 0.0)
-    denominator = jnp.sum(hist_weight, -1) + jnp.sum(draft_weight, -1)
-    weighted = jnp.einsum(
-        "krs,skd->krd",
-        hist_weight.astype(jnp.bfloat16),
-        history[:, :, 1],
-        preferred_element_type=jnp.float32,
-    ) + jnp.einsum(
-        "krj,jkd->krd",
-        draft_weight.astype(jnp.bfloat16),
-        draft_value,
-        preferred_element_type=jnp.float32,
-    )
-    return weighted / denominator[..., None]
+    hist_ok = (jnp.arange(history.shape[0]) < length)[None, :]
+    results = []
+    for head in range(heads_kv):
+        keys = history[:, 2 * head * head_dim : (2 * head + 1) * head_dim]
+        values = history[:, (2 * head + 1) * head_dim : (2 * head + 2) * head_dim]
+        hist_scores = (
+            jnp.einsum("rd,sd->rs", queries[head], keys, preferred_element_type=jnp.float32)
+            * score_scale
+        )
+        draft_scores = (
+            jnp.einsum(
+                "rd,jd->rj", queries[head], draft_key[:, head], preferred_element_type=jnp.float32
+            )
+            * score_scale
+        )
+        row_max = jnp.maximum(
+            jnp.max(jnp.where(hist_ok, hist_scores, -jnp.inf), -1),
+            jnp.max(jnp.where(visible, draft_scores, -jnp.inf), -1),
+        )
+        hist_weight = jnp.where(hist_ok, jnp.exp(hist_scores - row_max[:, None]), 0.0)
+        draft_weight = jnp.where(visible, jnp.exp(draft_scores - row_max[:, None]), 0.0)
+        denominator = jnp.sum(hist_weight, -1) + jnp.sum(draft_weight, -1)
+        weighted = jnp.einsum(
+            "rs,sd->rd",
+            hist_weight.astype(jnp.bfloat16),
+            values,
+            preferred_element_type=jnp.float32,
+        ) + jnp.einsum(
+            "rj,jd->rd",
+            draft_weight.astype(jnp.bfloat16),
+            draft_value[:, head],
+            preferred_element_type=jnp.float32,
+        )
+        results.append(weighted / denominator[:, None])
+    return jnp.stack(results, 0)
 
 
 def finish(result, draft_len):
@@ -134,23 +140,43 @@
     query_rows = queries.transpose(0, 2, 1, 3, 4).reshape(USER_DEV, heads_kv, row_count, HD)
     visible = jnp.repeat(ancestry > 0.5, group_size, axis=1)
     block_rows = USER_DEV * MAXP
-    capacity = 2 * block_rows // pool_size
+    capacity = block_rows // pool_size
     kv_cols = kv_pool.shape[2]
     owner_blocks = page_owner.reshape(pool_size, block_rows)
     slot_blocks = page_slot.reshape(pool_size, block_rows)
     one_hot = (owner_blocks[:, :, None] == jnp.arange(pool_size)[None, None, :]).astype(jnp.int32)
     slot_ranks = jnp.sum((jnp.cumsum(one_hot, axis=1) - one_hot) * one_hot, axis=2)
+    hot_owner = jnp.argmax(jnp.sum(one_hot, axis=1), axis=1)
+    mine = owner_blocks == my_index
     targets = jnp.arange(pool_size)[:, None] * capacity + slot_ranks
-    send_to = jnp.where(owner_blocks == my_index, targets, pool_size * capacity).reshape(-1)
+    send_to = jnp.where(mine & (slot_ranks < capacity), targets, pool_size * capacity)
     pack_index = (
         jnp.zeros((pool_size * capacity,), jnp.int32)
-        .at[send_to]
+        .at[send_to.reshape(-1)]
         .set(slot_blocks.reshape(-1), mode="drop")
     )
+    extra_to = jnp.where(mine & (slot_ranks >= capacity), slot_ranks - capacity, capacity)
+    extra_index = (
+        jnp.zeros((capacity,), jnp.int32)
+        .at[extra_to.reshape(-1)]
+        .set(slot_blocks.reshape(-1), mode="drop")
+    )
+    piece_rows = capacity * PAGE // pool_size
+    arrived = lax.all_to_all(
+        kv_pool[pack_index], "pool", split_axis=0, concat_axis=0, tiled=True
+    )
+    spread = lax.all_to_all(
+        kv_pool[extra_index].reshape(pool_size, piece_rows, kv_cols),
+        "pool",
+        split_axis=0,
+        concat_axis=0,
+        tiled=True,
+    )
+    extra = lax.all_to_all(
+        spread[hot_owner], "pool", split_axis=0, concat_axis=0, tiled=True
+    ).reshape(capacity, PAGE, kv_cols)
     local_source = resident_kv.reshape(USER_DEV * MAXRES, PAGE, kv_cols)
     outputs = []
-    packed = kv_pool[pack_index]
-    arrived = lax.all_to_all(packed, "pool", split_axis=0, concat_axis=0, tiled=True)
     my_owner = lax.dynamic_index_in_dim(owner_blocks, my_index, 0, keepdims=False).reshape(
         USER_DEV, MAXP
     )
@@ -159,11 +185,16 @@
     )
     numbers = jnp.arange(MAXP)
     for local_user in range(USER_DEV):
+        owner = my_owner[local_user]
+        rank = my_rank[local_user]
         resident_pages = local_source[local_user * MAXRES + jnp.minimum(numbers, MAXRES - 1)]
-        pool_pages = arrived[my_owner[local_user] * capacity + my_rank[local_user]]
+        regular_pages = arrived[owner * capacity + jnp.minimum(rank, capacity - 1)]
+        extra_pages = extra[jnp.clip(rank - capacity, 0, capacity - 1)]
         history = jnp.where(
-            (numbers < my_resident[local_user])[:, None, None], resident_pages, pool_pages
-        ).reshape(MAXP * PAGE, heads_kv, 2, HD)
+            (numbers < my_resident[local_user])[:, None, None],
+            resident_pages,
+            jnp.where((rank < capacity)[:, None, None], regular_pages, extra_pages),
+        ).reshape(MAXP * PAGE, kv_cols)
         result = attend_dense(
             query_rows[local_user],
             history,

time: 734 us -> 546 us (0.74)
  waiting for transfers between devices: 555 us -> 386 us
  local copies, waits for them, and re-layouts: 72.4 us -> 52.9 us
  matrix products: 51.4 us -> 40 us
  starting transfers between devices: 7.58 us -> 16.3 us
    reduce_scatter x1, waiting for transfers between devices: 453 us -> 0.01 us  [body(): lax.psum_scatter(jnp.dot(draft_states, w_qkv, preferred_element_type=jnp....]
    all_to_all x1 -> x3, waiting for transfers between devices: 0.01 us -> 287 us  [the longest x1 222 us: body(): lax.all_to_all(kv_pool[pack_index], 'pool', split_axis=0, concat_axis=0,...]
    gather x4 -> x2, local copies, waits for them, and re-layouts: 19.7 us -> 5.68 us  [body(): local_source[local_user * MAXRES + jnp.minimum(numbers, MAXRES - 1)]]
    reduce_sum x4, other arithmetic: 16.2 us -> 4.67 us  [attend_dense(): denominator = jnp.sum(hist_weight, -1) + jnp.sum(draft_weight, -1)]
    dot_general x8 -> x16, matrix products: 30.1 us -> 18.6 us  [the longest x4 11 us: attend_dense(): jnp.einsum('rd,sd->rs', queries[head], keys, preferred_element_type=jnp.f...]
    all_to_all x1 -> x3, starting transfers between devices: 7.28 us -> 15.9 us  [the longest x1 7.28 us: body(): lax.all_to_all(kv_pool[extra_index].reshape(pool_size, piece_rows, kv_col...]
    gather x5 -> x7, local copies, waits for them, and re-layouts: 43 us -> 35.1 us  [the longest x2 12.6 us: body(): regular_pages = arrived[owner * capacity + jnp.minimum(rank, capacity - 1)]]
  transfers between devices with their start and end apart: 4 -> 6, of which waited for: 3 -> 5; matrix products, arithmetic and copies ran while one was open for 6% -> 13% of each run, Pallas kernels for 0% -> 0%
where the time goes in v2:
time: 546 us; the launch traced here: 537 us
  waiting for transfers between devices  386 us (71%)
  local copies, waits for them, and re-layouts  52.9 us (10%)
  matrix products  40 us (7%)
  other arithmetic  27.6 us (5%)
  starting transfers between devices  16.3 us (3%)
  between operations  14.1 us (3%)
    all_to_all x1, waiting for transfers between devices, body(): lax.all_to_all(kv_pool[pack_index], 'pool', split_axis=0, concat_axis=0,...  222 us
    all_gather x1, waiting for transfers between devices, body(): lax.all_gather(attention, 'pool', axis=0, tiled=True)  70 us
    all_to_all x1, waiting for transfers between devices, body(): lax.all_to_all(spread[hot_owner], 'pool', split_axis=0, concat_axis=0, ti...  38.4 us
    reduce_scatter x1, waiting for transfers between devices, body(): lax.psum_scatter(partial_out.astype(jnp.bfloat16), 'tp', scatter_dimensio...  29.8 us
    all_to_all x1, waiting for transfers between devices, body(): lax.all_to_all(kv_pool[extra_index].reshape(pool_size, piece_rows, kv_col...  25.7 us
    select_n x2, other arithmetic, body(): jnp.where((numbers < my_resident[local_user])[:, None, None], resident_pa...  14.1 us
    gather x2, local copies, waits for them, and re-layouts, body(): regular_pages = arrived[owner * capacity + jnp.minimum(rank, capacity - 1)]  12.6 us
    dot_general x4, matrix products, attend_dense(): jnp.einsum('rd,sd->rs', queries[head], keys, preferred_element_type=jnp.f...  11 us
  transfers between devices with their start and end apart: 6, of which 5 were waited for; matrix products, arithmetic and copies ran while one was open for 13% of the time, Pallas kernels for 0%

profile of v2, /device:TPU:0, one launch (start us, length us, event | category | flops | bytes accessed | tf_op | source)
XLA Modules:
  0.0 537.3 jit_solution(13276837173701073685)
XLA Ops:
  11.0 2.4 scatter_custom_fusion.1
  13.4 5.6 %gather_fusion.3 = bf16[8,128,512]{2,1,0:T(8,128)(2,1)} fusion(bf16[80,128,512]{2,1,0:T(8,128)(2,1)} %param.13, s32[1024]{0:T(1024)S(1)} %pad_clamp_fusion.5), kind=kCustom, calls=%fused_computation.3 | custom fusion | bytes 2097184 | tf_op jit(solution)/shard_map/gather | solution.py:169
  19.0 7.3 %all-to-all-start.1 = ((bf16[8,128,512]{2,1,0:T(8,128)(2,1)}), bf16[8,128,512]{2,1,0:T(8,128)(2,1)S(1)}, u32[]{:S(2)}, u32[]{:S(2)}) async-start(bf16[8,128,512]{2,1,0:T(8,128)(2,1)} %gather_fusion.3), calls=%async_computation.2 | async-start | bytes 2097152 | tf_op jit(solution)/shard_map/all_to_all | solution.py:168
  26.3 10.9 %fusion.130 = f32[1024,2560]{1,0:T(8,128)} fusion(bf16[1024,1024]{1,0:T(8,128)(2,1)} %param.10, bf16[1024,2560]{1,0:T(8,128)(2,1)} %param.11), kind=kOutput, calls=%fused_computation.246 | convolution fusion | flops 5368709120 | bytes 17825792 | tf_op jit(solution)/shard_map/dot_general | solution.py:122
  38.1 25.7 %all-to-all-done.1 = bf16[8,128,512]{2,1,0:T(8,128)(2,1)S(1)} async-done(((bf16[8,128,512]{2,1,0:T(8,128)(2,1)}), bf16[8,128,512]{2,1,0:T(8,128)(2,1)S(1)}, u32[]{:S(2)}, u32[]{:S(2)}) %all-to-all-start.1) | async-done | bytes 1048608 | tf_op jit(solution)/shard_map/all_to_all | solution.py:168
  65.4 3.6 all-to-all-start.2
  71.4 9.8 %gather_fusion.1 = bf16[64,128,512]{2,1,0:T(8,128)(2,1)} fusion(bf16[80,128,512]{2,1,0:T(8,128)(2,1)} %param.13, s32[1024]{0:T(1024)S(1)} %pad_clamp_fusion.7), kind=kCustom, calls=%fused_computation.1 | custom fusion | bytes 16777472 | tf_op jit(solution)/shard_map/gather | solution.py:166
  81.2 38.4 %all-to-all-done.2 = bf16[8,128,512]{2,1,0:T(8,128)(2,1)S(1)} async-done(((bf16[8,128,512]{2,1,0:T(8,128)(2,1)}), bf16[8,128,512]{2,1,0:T(8,128)(2,1)S(1)}, u32[]{:S(2)}, u32[]{:S(2)}) %all-to-all-start.2) | async-done | bytes 1048608 | tf_op jit(solution)/shard_map/all_to_all | solution.py:175
  119.6 5.1 all-to-all-start
  126.9 2.8 gather_fusion
  129.7 2.9 gather_fusion.6
  137.5 2.8 gather_fusion.5
  140.3 2.8 gather_fusion.8
  143.1 222.4 %all-to-all-done = bf16[64,128,512]{2,1,0:T(8,128)(2,1)} async-done(((bf16[64,128,512]{2,1,0:T(8,128)(2,1)}), bf16[64,128,512]{2,1,0:T(8,128)(2,1)}, u32[]{:S(2)}, u32[]{:S(2)}) %all-to-all-start) | async-done | bytes 8388640 | tf_op jit(solution)/shard_map/all_to_all | solution.py:165
  365.5 6.3 %gather_fusion.2 = bf16[32,128,512]{2,1,0:T(8,128)(2,1)} fusion(bf16[64,128,512]{2,1,0:T(8,128)(2,1)} %all-to-all-done, s32[1024]{0:T(1024)S(1)} %pad_clamp_fusion.6), kind=kCustom, calls=%fused_computation.2 | custom fusion | bytes 8388736 | tf_op jit(solution)/shard_map/gather | solution.py:191
  371.8 6.3 %gather_fusion.7 = bf16[32,128,512]{2,1,0:T(8,128)(2,1)} fusion(bf16[64,128,512]{2,1,0:T(8,128)(2,1)} %all-to-all-done, s32[1024]{0:T(1024)S(1)} %pad_clamp_fusion.1), kind=kCustom, calls=%fused_computation.7 | custom fusion | bytes 8388736 | tf_op jit(solution)/shard_map/gather | solution.py:191
  378.1 9.6 %fusion.9 = bf16[4096,512]{1,0:T(8,128)(2,1)} fusion(bf16[32,128,512]{2,1,0:T(8,128)(2,1)} %gather_fusion.5, bf16[32,128,512]{2,1,0:T(8,128)(2,1)} %gather_fusion.2, bf16[32,128,512]{2,1,0:T(8,128)(2,1)} %gather_fusion, pred[4096]{0:T(1024)(128)(4,1)S(1)} %get-tuple-element.68, pred[4096]{0:T(1024)(128)(4,1)S(1)} %broadcast_bitcast_fusion.5), kind=kLoop, calls=%fused_computation.30 | loop fusion | flops 4194304 | bytes 16785408 | tf_op jit(solution)/shard_map/jit(_where)/select_n | solution.py:193
  387.8 4.4 fusion.8
  395.4 3.1 select_reduce_fusion.3
  398.7 3.3 fusion
  409.9 3.3 fusion.4
  421.1 70.0 %all-gather.2.cloned.1.call-done = bf16[1024,2048]{1,0:T(8,128)(2,1)} async-done(((bf16[128,2048]{1,0:T(8,128)(2,1)}), bf16[1024,2048]{1,0:T(8,128)(2,1)}) %all-gather.2.cloned.1.call-update) | async-done | bytes 4194320 | tf_op jit(solution)/shard_map/all_gather | solution.py:209
  491.1 9.4 %convolution_convert_fusion = bf16[1024,1024]{1,0:T(8,128)(2,1)} fusion(bf16[1024,2048]{1,0:T(8,128)(2,1)} %all-gather.2.cloned.1.call-done, bf16[2048,1024]{1,0:T(8,128)(2,1)} %param.12), kind=kOutput, calls=%fused_computation.39 | convolution fusion | flops 4296015872 | bytes 10485760 | tf_op jit(solution)/shard_map/dot_general | solution.py:208
  500.5 29.8 %reduce-scatter.5.cloned.1.call-done = bf16[256,1024]{1,0:T(8,128)(2,1)} async-done(((bf16[1024,1024]{1,0:T(8,128)(2,1)}), bf16[256,1024]{1,0:T(8,128)(2,1)}) %reduce-scatter.5.cloned.1.call-update) | async-done | bytes 524304 | tf_op jit(solution)/shard_map/reduce_scatter | solution.py:213
  (126 shorter events, 35.3 us)
Async XLA Ops:
  6.5 120.4 %copy-start = (bf16[2,8,128,512]{3,2,1,0:T(8,128)(2,1)S(1)}, bf16[2,8,128,512]{3,2,1,0:T(8,128)(2,1)}, u32[]{:S(2)}) copy-start(bf16[2,8,128,512]{3,2,1,0:T(8,128)(2,1)} %param.14) | copy-start | bytes 6291460
  19.0 44.8 %all-to-all-start.1 = ((bf16[8,128,512]{2,1,0:T(8,128)(2,1)}), bf16[8,128,512]{2,1,0:T(8,128)(2,1)S(1)}, u32[]{:S(2)}, u32[]{:S(2)}) async-start(bf16[8,128,512]{2,1,0:T(8,128)(2,1)} %gather_fusion.3), calls=%async_computation.2 | async-start | bytes 2097152 | tf_op jit(solution)/shard_map/all_to_all | solution.py:168
  26.3 365.9 %reduce-scatter.3.cloned.1.call-start = ((), (), s32[]{:S(2)}) async-start(), calls=%async_computation.5 | async-start | bytes 11796480 | tf_op jit(solution)/shard_map/reduce_scatter | solution.py:121
  65.4 54.1 %all-to-all-start.2 = ((bf16[8,128,512]{2,1,0:T(8,128)(2,1)}), bf16[8,128,512]{2,1,0:T(8,128)(2,1)S(1)}, u32[]{:S(2)}, u32[]{:S(2)}) async-start(bf16[8,128,512]{2,1,0:T(8,128)(2,1)} %gather_fusion.4), calls=%async_computation.3 | async-start | bytes 2097152 | tf_op jit(solution)/shard_map/all_to_all | solution.py:175
  81.2 45.5 %copy-start.8 = (s32[16]{0:T(128)S(1)}, s32[16]{0:T(128)}, u32[]{:S(2)}) copy-start(s32[16]{0:T(128)} %param.18) | copy-start | bytes 196
  119.6 246.0 %all-to-all-start = ((bf16[64,128,512]{2,1,0:T(8,128)(2,1)}), bf16[64,128,512]{2,1,0:T(8,128)(2,1)}, u32[]{:S(2)}, u32[]{:S(2)}) async-start(bf16[64,128,512]{2,1,0:T(8,128)(2,1)} %gather_fusion.1), calls=%async_computation.1 | async-start | bytes 16777216 | tf_op jit(solution)/shard_map/all_to_all | solution.py:165
  124.6 366.4 %all-gather.2.cloned.1.call-start = ((), (), s32[]{:S(2)}) async-start(), calls=%async_computation.6 | async-start | bytes 4718592 | tf_op jit(solution)/shard_map/all_gather | solution.py:209
  126.9 8.0 %copy-start.7 = (s32[16]{0:T(128)S(1)}, s32[16]{0:T(128)}, u32[]{:S(2)}) copy-start(s32[16]{0:T(128)} %param.17) | copy-start | bytes 196
  378.1 9.7 %copy-start.2 = (bf16[32,128,512]{2,1,0:T(8,128)(2,1)S(1)}, bf16[32,128,512]{2,1,0:T(8,128)(2,1)}, u32[]{:S(2)}) copy-start(bf16[32,128,512]{2,1,0:T(8,128)(2,1)} %gather_fusion.6) | copy-start | bytes 12582916
  378.1 9.7 %copy-start.3 = (bf16[32,128,512]{2,1,0:T(8,128)(2,1)S(1)}, bf16[32,128,512]{2,1,0:T(8,128)(2,1)}, u32[]{:S(2)}) copy-start(bf16[32,128,512]{2,1,0:T(8,128)(2,1)} %gather_fusion.8) | copy-start | bytes 12582916
  378.1 9.7 %copy-start.4 = (bf16[32,128,512]{2,1,0:T(8,128)(2,1)S(1)}, bf16[32,128,512]{2,1,0:T(8,128)(2,1)}, u32[]{:S(2)}) copy-start(bf16[32,128,512]{2,1,0:T(8,128)(2,1)} %gather_fusion.7) | copy-start | bytes 12582916
  394.6 4.0 copy-start.6
  406.1 2.2 copy-start.5
  420.8 109.6 %reduce-scatter.5.cloned.1.call-start = ((), (), s32[]{:S(2)}) async-start(), calls=%async_computation.7 | async-start | bytes 2621440 | tf_op jit(solution)/shard_map/reduce_scatter | solution.py:213
  491.1 39.3 %copy-start.1 = (bf16[2,8,128,512]{3,2,1,0:T(8,128)(2,1)S(1)}, bf16[2,8,128,512]{3,2,1,0:T(8,128)(2,1)}, u32[]{:S(2)}) copy-start(bf16[2,8,128,512]{3,2,1,0:T(8,128)(2,1)} %param.14) | copy-start | bytes 6291460
Sparse Core Ops, SparseCore 0:
  37.4 346.5 reduce-scatter.2
  420.9 70.1 all-gather.1
  500.6 29.6 reduce-scatter.4

commit v3 on v2

--- a/solution.py
+++ b/solution.py
@@ -162,16 +162,16 @@
         .set(slot_blocks.reshape(-1), mode="drop")
     )
     piece_rows = capacity * PAGE // pool_size
-    arrived = lax.all_to_all(
-        kv_pool[pack_index], "pool", split_axis=0, concat_axis=0, tiled=True
-    )
-    spread = lax.all_to_all(
-        kv_pool[extra_index].reshape(pool_size, piece_rows, kv_cols),
-        "pool",
-        split_axis=0,
-        concat_axis=0,
-        tiled=True,
-    )
+    outgoing = jnp.concatenate(
+        [
+            kv_pool[pack_index].reshape(pool_size, capacity * PAGE, kv_cols),
+            kv_pool[extra_index].reshape(pool_size, piece_rows, kv_cols),
+        ],
+        1,
+    )
+    incoming = lax.all_to_all(outgoing, "pool", split_axis=0, concat_axis=0, tiled=True)
+    arrived = incoming[:, : capacity * PAGE].reshape(pool_size * capacity, PAGE, kv_cols)
+    spread = incoming[:, capacity * PAGE :]
     extra = lax.all_to_all(
         spread[hot_owner], "pool", split_axis=0, concat_axis=0, tiled=True
     ).reshape(capacity, PAGE, kv_cols)

time: 546 us -> 569 us (1.042)
  waiting for transfers between devices: 386 us -> 396 us
  other arithmetic: 27.6 us -> 37.5 us
  local copies, waits for them, and re-layouts: 52.9 us -> 61.4 us
    all_to_all x2 -> x1, waiting for transfers between devices: 248 us -> 274 us  [body(): lax.all_to_all(outgoing, 'pool', split_axis=0, concat_axis=0, tiled=True)]
    all_to_all x1, waiting for transfers between devices: 38.4 us -> 15.5 us  [body(): lax.all_to_all(spread[hot_owner], 'pool', split_axis=0, concat_axis=0, ti...]
    concatenate x0 -> x1, other arithmetic: none -> 9.6 us  [body(): jnp.concatenate([kv_pool[pack_index].reshape(pool_size, capacity * PAGE,...]
    slice x0 -> x2, local copies, waits for them, and re-layouts: none -> 8.91 us  [the longest x1 7.58 us: body(): incoming[:, :capacity * PAGE].reshape(pool_size * capacity, PAGE, kv_cols)]
    all_to_all x2 -> x1, starting transfers between devices: 12.4 us -> 7.28 us  [body(): lax.all_to_all(outgoing, 'pool', split_axis=0, concat_axis=0, tiled=True)]
  transfers between devices with their start and end apart: 6 -> 5, of which waited for: 5 -> 5; matrix products, arithmetic and copies ran while one was open for 13% -> 12% of each run, Pallas kernels for 0% -> 0%
where the time goes in v3:
time: 569 us; the launch traced here: 560 us
  waiting for transfers between devices  396 us (70%)
  local copies, waits for them, and re-layouts  61.4 us (11%)
  matrix products  40 us (7%)
  other arithmetic  37.5 us (7%)
  between operations  14.1 us (2%)
  starting transfers between devices  11.3 us (2%)
    all_to_all x1, waiting for transfers between devices, body(): lax.all_to_all(outgoing, 'pool', split_axis=0, concat_axis=0, tiled=True)  274 us
    all_gather x1, waiting for transfers between devices, body(): lax.all_gather(attention, 'pool', axis=0, tiled=True)  71.8 us
    reduce_scatter x1, waiting for transfers between devices, body(): lax.psum_scatter(partial_out.astype(jnp.bfloat16), 'tp', scatter_dimensio...  29.8 us
    all_to_all x1, waiting for transfers between devices, body(): lax.all_to_all(spread[hot_owner], 'pool', split_axis=0, concat_axis=0, ti...  15.5 us
    select_n x2, other arithmetic, body(): jnp.where((numbers < my_resident[local_user])[:, None, None], resident_pa...  14.1 us
    gather x2, local copies, waits for them, and re-layouts, body(): regular_pages = arrived[owner * capacity + jnp.minimum(rank, capacity - 1)]  12.6 us
  transfers between devices with their start and end apart: 5, of which 5 were waited for; matrix products, arithmetic and copies ran while one was open for 12% of the time, Pallas kernels for 0%

profile of v3, /device:TPU:0, one launch (start us, length us, event | category | flops | bytes accessed | tf_op | source)
XLA Modules:
  0.0 560.0 jit_solution(4556441357739619437)
XLA Ops:
  15.9 9.5 %gather_fusion.1 = bf16[64,128,512]{2,1,0:T(8,128)(2,1)} fusion(bf16[80,128,512]{2,1,0:T(8,128)(2,1)} %param.13, s32[1024]{0:T(1024)S(1)} %pad_clamp_fusion.7), kind=kCustom, calls=%fused_computation.1 | custom fusion | bytes 16777472 | tf_op jit(solution)/shard_map/gather | solution.py:167
  25.4 4.6 gather_fusion.2
  30.0 9.6 %pad_maximum_fusion = bf16[8,1152,512]{2,1,0:T(8,128)(2,1)} fusion(bf16[8,128,512]{2,1,0:T(8,128)(2,1)S(1)} %gather_fusion.2, bf16[8,1024,512]{2,1,0:T(8,128)(2,1)} %bitcast.166), kind=kLoop, calls=%fused_computation.11 | loop fusion | flops 18874368 | bytes 18874368 | tf_op jit(solution)/shard_map/concatenate | solution.py:165
  39.6 7.3 %all-to-all-start = ((bf16[8,1152,512]{2,1,0:T(8,128)(2,1)}), bf16[8,1152,512]{2,1,0:T(8,128)(2,1)}, u32[]{:S(2)}, u32[]{:S(2)}) async-start(bf16[8,1152,512]{2,1,0:T(8,128)(2,1)} %pad_maximum_fusion), calls=%async_computation.1 | async-start | bytes 18874368 | tf_op jit(solution)/shard_map/all_to_all | solution.py:172
  47.0 10.9 %fusion.130 = f32[1024,2560]{1,0:T(8,128)} fusion(bf16[1024,1024]{1,0:T(8,128)(2,1)} %param.10, bf16[1024,2560]{1,0:T(8,128)(2,1)} %param.11), kind=kOutput, calls=%fused_computation.247 | convolution fusion | flops 5368709120 | bytes 17825792 | tf_op jit(solution)/shard_map/dot_general | solution.py:122
  63.0 273.8 %all-to-all-done = bf16[8,1152,512]{2,1,0:T(8,128)(2,1)} async-done(((bf16[8,1152,512]{2,1,0:T(8,128)(2,1)}), bf16[8,1152,512]{2,1,0:T(8,128)(2,1)}, u32[]{:S(2)}, u32[]{:S(2)}) %all-to-all-start) | async-done | bytes 9437216 | tf_op jit(solution)/shard_map/all_to_all | solution.py:172
  339.8 3.6 all-to-all-start.1
  344.4 2.8 gather_fusion
  347.2 2.9 gather_fusion.6
  352.8 7.6 %slice.224 = bf16[8,1024,512]{2,1,0:T(8,128)(2,1)} slice(bf16[8,1152,512]{2,1,0:T(8,128)(2,1)} %all-to-all-done), slice={[0:8], [0:1024], [0:512]} | slice | bytes 16777216 | tf_op jit(solution)/shard_map/slice | solution.py:173
  360.4 6.2 %gather_fusion.3 = bf16[32,128,512]{2,1,0:T(8,128)(2,1)} fusion(bf16[64,128,512]{2,1,0:T(8,128)(2,1)} %bitcast.167, s32[1024]{0:T(1024)S(1)} %pad_clamp_fusion.5), kind=kCustom, calls=%fused_computation.3 | custom fusion | bytes 8388736 | tf_op jit(solution)/shard_map/gather | solution.py:191
  366.6 6.3 %gather_fusion.7 = bf16[32,128,512]{2,1,0:T(8,128)(2,1)} fusion(bf16[64,128,512]{2,1,0:T(8,128)(2,1)} %bitcast.168, s32[1024]{0:T(1024)S(1)} %pad_clamp_fusion.1), kind=kCustom, calls=%fused_computation.7 | custom fusion | bytes 8388736 | tf_op jit(solution)/shard_map/gather | solution.py:191
  373.0 15.5 %all-to-all-done.1 = bf16[8,128,512]{2,1,0:T(8,128)(2,1)S(1)} async-done(((bf16[8,128,512]{2,1,0:T(8,128)(2,1)}), bf16[8,128,512]{2,1,0:T(8,128)(2,1)S(1)}, u32[]{:S(2)}, u32[]{:S(2)}) %all-to-all-start.1) | async-done | bytes 1048608 | tf_op jit(solution)/shard_map/all_to_all | solution.py:175
  388.4 2.8 gather_fusion.5
  391.3 2.8 gather_fusion.8
  394.1 9.8 %fusion.9 = bf16[4096,512]{1,0:T(8,128)(2,1)} fusion(bf16[32,128,512]{2,1,0:T(8,128)(2,1)} %gather_fusion.5, bf16[32,128,512]{2,1,0:T(8,128)(2,1)} %gather_fusion.3, bf16[32,128,512]{2,1,0:T(8,128)(2,1)} %gather_fusion, pred[4096]{0:T(1024)(128)(4,1)S(1)} %get-tuple-element.68, pred[4096]{0:T(1024)(128)(4,1)S(1)} %broadcast_bitcast_fusion.5), kind=kLoop, calls=%fused_computation.31 | loop fusion | flops 4194304 | bytes 16785408 | tf_op jit(solution)/shard_map/jit(_where)/select_n | solution.py:193
  403.9 4.4 fusion.8
  408.3 4.7 reduce-scatter.3.cloned.1.call-done
  416.2 3.1 select_reduce_fusion.3
  419.5 3.3 fusion
  430.7 3.3 fusion.4
  441.9 71.8 %all-gather.2.cloned.1.call-done = bf16[1024,2048]{1,0:T(8,128)(2,1)} async-done(((bf16[128,2048]{1,0:T(8,128)(2,1)}), bf16[1024,2048]{1,0:T(8,128)(2,1)}) %all-gather.2.cloned.1.call-update) | async-done | bytes 4194320 | tf_op jit(solution)/shard_map/all_gather | solution.py:209
  513.7 9.4 %convolution_convert_fusion = bf16[1024,1024]{1,0:T(8,128)(2,1)} fusion(bf16[1024,2048]{1,0:T(8,128)(2,1)} %all-gather.2.cloned.1.call-done, bf16[2048,1024]{1,0:T(8,128)(2,1)} %param.12), kind=kOutput, calls=%fused_computation.40 | convolution fusion | flops 4296015872 | bytes 10485760 | tf_op jit(solution)/shard_map/dot_general | solution.py:208
  523.1 29.8 %reduce-scatter.5.cloned.1.call-done = bf16[256,1024]{1,0:T(8,128)(2,1)} async-done(((bf16[1024,1024]{1,0:T(8,128)(2,1)}), bf16[256,1024]{1,0:T(8,128)(2,1)}) %reduce-scatter.5.cloned.1.call-update) | async-done | bytes 524304 | tf_op jit(solution)/shard_map/reduce_scatter | solution.py:213
  (127 shorter events, 39.9 us)
Async XLA Ops:
  6.5 337.8 %copy-start = (bf16[2,8,128,512]{3,2,1,0:T(8,128)(2,1)S(1)}, bf16[2,8,128,512]{3,2,1,0:T(8,128)(2,1)}, u32[]{:S(2)}) copy-start(bf16[2,8,128,512]{3,2,1,0:T(8,128)(2,1)} %param.14) | copy-start | bytes 6291460
  39.6 297.2 %all-to-all-start = ((bf16[8,1152,512]{2,1,0:T(8,128)(2,1)}), bf16[8,1152,512]{2,1,0:T(8,128)(2,1)}, u32[]{:S(2)}, u32[]{:S(2)}) async-start(bf16[8,1152,512]{2,1,0:T(8,128)(2,1)} %pad_maximum_fusion), calls=%async_computation.1 | async-start | bytes 18874368 | tf_op jit(solution)/shard_map/all_to_all | solution.py:172
  46.9 366.1 %reduce-scatter.3.cloned.1.call-start = ((), (), s32[]{:S(2)}) async-start(), calls=%async_computation.4 | async-start | bytes 11796480 | tf_op jit(solution)/shard_map/reduce_scatter | solution.py:121
  57.9 0.7 copy-start.8
  57.9 3.0 copy-start.7
  339.8 48.7 %all-to-all-start.1 = ((bf16[8,128,512]{2,1,0:T(8,128)(2,1)}), bf16[8,128,512]{2,1,0:T(8,128)(2,1)S(1)}, u32[]{:S(2)}, u32[]{:S(2)}) async-start(bf16[8,128,512]{2,1,0:T(8,128)(2,1)} %gather_fusion.4), calls=%async_computation.2 | async-start | bytes 2097152 | tf_op jit(solution)/shard_map/all_to_all | solution.py:175
  343.4 170.3 %all-gather.2.cloned.1.call-start = ((), (), s32[]{:S(2)}) async-start(), calls=%async_computation.5 | async-start | bytes 4718592 | tf_op jit(solution)/shard_map/all_gather | solution.py:209
  394.1 9.8 %copy-start.2 = (bf16[32,128,512]{2,1,0:T(8,128)(2,1)S(1)}, bf16[32,128,512]{2,1,0:T(8,128)(2,1)}, u32[]{:S(2)}) copy-start(bf16[32,128,512]{2,1,0:T(8,128)(2,1)} %gather_fusion.6) | copy-start | bytes 12582916
  394.1 9.8 %copy-start.3 = (bf16[32,128,512]{2,1,0:T(8,128)(2,1)S(1)}, bf16[32,128,512]{2,1,0:T(8,128)(2,1)}, u32[]{:S(2)}) copy-start(bf16[32,128,512]{2,1,0:T(8,128)(2,1)} %gather_fusion.7) | copy-start | bytes 12582916
  394.1 9.8 %copy-start.4 = (bf16[32,128,512]{2,1,0:T(8,128)(2,1)S(1)}, bf16[32,128,512]{2,1,0:T(8,128)(2,1)}, u32[]{:S(2)}) copy-start(bf16[32,128,512]{2,1,0:T(8,128)(2,1)} %gather_fusion.8) | copy-start | bytes 12582916
  415.4 4.0 copy-start.6
  426.8 2.2 copy-start.5
  441.6 111.4 %reduce-scatter.5.cloned.1.call-start = ((), (), s32[]{:S(2)}) async-start(), calls=%async_computation.6 | async-start | bytes 2621440 | tf_op jit(solution)/shard_map/reduce_scatter | solution.py:213
  513.7 39.3 %copy-start.1 = (bf16[2,8,128,512]{3,2,1,0:T(8,128)(2,1)S(1)}, bf16[2,8,128,512]{3,2,1,0:T(8,128)(2,1)}, u32[]{:S(2)}) copy-start(bf16[2,8,128,512]{3,2,1,0:T(8,128)(2,1)} %param.14) | copy-start | bytes 6291460
Sparse Core Ops, SparseCore 0:
  58.1 354.9 reduce-scatter.2
  441.7 71.9 all-gather.1
  523.3 29.6 reduce-scatter.4

commit v4 on v2

--- a/solution.py
+++ b/solution.py
@@ -51,21 +51,26 @@
     )
 
 
-def attend_dense(queries, history, draft_key, draft_value, visible, length):
-    heads_kv, row_count, head_dim = queries.shape
+def attend_dense(queries, history, draft_key, draft_value, visible, lengths):
+    users, heads_kv, row_count, head_dim = queries.shape
     score_scale = head_dim ** (-0.5)
-    hist_ok = (jnp.arange(history.shape[0]) < length)[None, :]
+    hist_ok = (jnp.arange(history.shape[1])[None, :] < lengths[:, None])[:, None, :]
     results = []
     for head in range(heads_kv):
-        keys = history[:, 2 * head * head_dim : (2 * head + 1) * head_dim]
-        values = history[:, (2 * head + 1) * head_dim : (2 * head + 2) * head_dim]
+        keys = history[:, :, 2 * head * head_dim : (2 * head + 1) * head_dim]
+        values = history[:, :, (2 * head + 1) * head_dim : (2 * head + 2) * head_dim]
         hist_scores = (
-            jnp.einsum("rd,sd->rs", queries[head], keys, preferred_element_type=jnp.float32)
+            jnp.einsum(
+                "urd,usd->urs", queries[:, head], keys, preferred_element_type=jnp.float32
+            )
             * score_scale
         )
         draft_scores = (
             jnp.einsum(
-                "rd,jd->rj", queries[head], draft_key[:, head], preferred_element_type=jnp.float32
+                "urd,ujd->urj",
+                queries[:, head],
+                draft_key[:, :, head],
+                preferred_element_type=jnp.float32,
             )
             * score_scale
         )
@@ -73,31 +78,31 @@
             jnp.max(jnp.where(hist_ok, hist_scores, -jnp.inf), -1),
             jnp.max(jnp.where(visible, draft_scores, -jnp.inf), -1),
         )
-        hist_weight = jnp.where(hist_ok, jnp.exp(hist_scores - row_max[:, None]), 0.0)
-        draft_weight = jnp.where(visible, jnp.exp(draft_scores - row_max[:, None]), 0.0)
+        hist_weight = jnp.where(hist_ok, jnp.exp(hist_scores - row_max[..., None]), 0.0)
+        draft_weight = jnp.where(visible, jnp.exp(draft_scores - row_max[..., None]), 0.0)
         denominator = jnp.sum(hist_weight, -1) + jnp.sum(draft_weight, -1)
         weighted = jnp.einsum(
-            "rs,sd->rd",
+            "urs,usd->urd",
             hist_weight.astype(jnp.bfloat16),
             values,
             preferred_element_type=jnp.float32,
         ) + jnp.einsum(
-            "rj,jd->rd",
+            "urj,ujd->urd",
             draft_weight.astype(jnp.bfloat16),
-            draft_value[:, head],
+            draft_value[:, :, head],
             preferred_element_type=jnp.float32,
         )
-        results.append(weighted / denominator[:, None])
-    return jnp.stack(results, 0)
+        results.append(weighted / denominator[..., None])
+    return jnp.stack(results, 1)
 
 
 def finish(result, draft_len):
-    heads_kv, row_count, head_dim = result.shape
-    result = result.reshape(heads_kv, draft_len, row_count // draft_len, head_dim).transpose(
-        1, 0, 2, 3
-    )
-    return result.reshape(draft_len, heads_kv * row_count // draft_len * head_dim).astype(
-        jnp.bfloat16
+    users, heads_kv, row_count, head_dim = result.shape
+    result = result.reshape(users, heads_kv, draft_len, row_count // draft_len, head_dim)
+    return (
+        result.transpose(0, 2, 1, 3, 4)
+        .reshape(users * draft_len, heads_kv * row_count // draft_len * head_dim)
+        .astype(jnp.bfloat16)
     )
 
 
@@ -118,8 +123,12 @@
     group_size = H // KVH
     local_cols = w_qkv.shape[1]
     heads_kv = local_cols // ((group_size + 2) * HD)
+    partial_projection = jnp.dot(draft_states, w_qkv, preferred_element_type=jnp.float32)
+    partial_projection, page_owner, page_slot = lax.optimization_barrier(
+        (partial_projection, page_owner, page_slot)
+    )
     projected = lax.psum_scatter(
-        jnp.dot(draft_states, w_qkv, preferred_element_type=jnp.float32),
+        partial_projection,
         "pool",
         scatter_dimension=0,
         tiled=True,
@@ -176,7 +185,6 @@
         spread[hot_owner], "pool", split_axis=0, concat_axis=0, tiled=True
     ).reshape(capacity, PAGE, kv_cols)
     local_source = resident_kv.reshape(USER_DEV * MAXRES, PAGE, kv_cols)
-    outputs = []
     my_owner = lax.dynamic_index_in_dim(owner_blocks, my_index, 0, keepdims=False).reshape(
         USER_DEV, MAXP
     )
@@ -184,27 +192,18 @@
         USER_DEV, MAXP
     )
     numbers = jnp.arange(MAXP)
-    for local_user in range(USER_DEV):
-        owner = my_owner[local_user]
-        rank = my_rank[local_user]
-        resident_pages = local_source[local_user * MAXRES + jnp.minimum(numbers, MAXRES - 1)]
-        regular_pages = arrived[owner * capacity + jnp.minimum(rank, capacity - 1)]
-        extra_pages = extra[jnp.clip(rank - capacity, 0, capacity - 1)]
-        history = jnp.where(
-            (numbers < my_resident[local_user])[:, None, None],
-            resident_pages,
-            jnp.where((rank < capacity)[:, None, None], regular_pages, extra_pages),
-        ).reshape(MAXP * PAGE, kv_cols)
-        result = attend_dense(
-            query_rows[local_user],
-            history,
-            draft_key[local_user],
-            draft_value[local_user],
-            visible[local_user],
-            my_lengths[local_user],
-        )
-        outputs.append(finish(result, DRAFT))
-    attention = jnp.concatenate(outputs, 0)
+    user_ids = jnp.arange(USER_DEV)[:, None]
+    resident_pages = local_source[user_ids * MAXRES + jnp.minimum(numbers, MAXRES - 1)[None, :]]
+    regular_pages = arrived[my_owner * capacity + jnp.minimum(my_rank, capacity - 1)]
+    extra_pages = extra[jnp.clip(my_rank - capacity, 0, capacity - 1)]
+    history = jnp.where(
+        (numbers[None, :] < my_resident[:, None])[:, :, None, None],
+        resident_pages,
+        jnp.where((my_rank < capacity)[:, :, None, None], regular_pages, extra_pages),
+    ).reshape(USER_DEV, MAXP * PAGE, kv_cols)
+    attention = finish(
+        attend_dense(query_rows, history, draft_key, draft_value, visible, my_lengths), DRAFT
+    )
     partial_out = jnp.dot(
         lax.all_gather(attention, "pool", axis=0, tiled=True),
         w_out,

time: 546 us -> 554 us (1.015); the launches traced: 537 us -> 554 us
  matrix products: 40 us -> 61.7 us
    all_to_all x1, waiting for transfers between devices: 222 us -> 193 us  [body(): lax.all_to_all(kv_pool[pack_index], 'pool', split_axis=0, concat_axis=0,...]
    all_to_all x1, waiting for transfers between devices: 25.7 us -> 53.3 us  [body(): lax.all_to_all(kv_pool[extra_index].reshape(pool_size, piece_rows, kv_col...]
    dot_general x16 -> x8, matrix products: 18.6 us -> 40.2 us  [the longest x2 22.6 us: attend_dense(): jnp.einsum('urd,usd->urs', queries[:, head], keys, preferred_element_type...]
    gather x6 -> x3, local copies, waits for them, and re-layouts: 23.9 us -> 20.2 us  [the longest x1 9.02 us: body(): arrived[my_owner * capacity + jnp.minimum(my_rank, capacity - 1)]]
    select_n x5 -> x3, other arithmetic: 14.1 us -> 13.6 us  [the longest x1 13.5 us: body(): jnp.where((numbers[None, :] < my_resident[:, None])[:, :, None, None], re...]
  transfers between devices with their start and end apart: 6 -> 6, of which waited for: 5 -> 6; matrix products, arithmetic and copies ran while one was open for 13% -> 11% of each run, Pallas kernels for 0% -> 0%
where the time goes in v4:
time: 554 us
  waiting for transfers between devices  388 us (70%)
  matrix products  61.7 us (11%)
  local copies, waits for them, and re-layouts  48.1 us (9%)
  other arithmetic  26.1 us (5%)
  starting transfers between devices  16.8 us (3%)
  between operations  13.4 us (2%)
    all_to_all x1, waiting for transfers between devices, body(): lax.all_to_all(kv_pool[pack_index], 'pool', split_axis=0, concat_axis=0,...  193 us
    all_gather x1, waiting for transfers between devices, body(): lax.all_gather(attention, 'pool', axis=0, tiled=True)  71.6 us
    all_to_all x1, waiting for transfers between devices, body(): lax.all_to_all(kv_pool[extra_index].reshape(pool_size, piece_rows, kv_col...  53.3 us
    all_to_all x1, waiting for transfers between devices, body(): lax.all_to_all(spread[hot_owner], 'pool', split_axis=0, concat_axis=0, ti...  39.4 us
    reduce_scatter x1, waiting for transfers between devices, body(): lax.psum_scatter(partial_out.astype(jnp.bfloat16), 'tp', scatter_dimensio...  29.9 us
    dot_general x2, matrix products, attend_dense(): jnp.einsum('urd,usd->urs', queries[:, head], keys, preferred_element_type...  22.6 us
    dot_general x2, matrix products, attend_dense(): jnp.einsum('urs,usd->urd', hist_weight.astype(jnp.bfloat16), values, pref...  16.4 us
    select_n x1, other arithmetic, body(): jnp.where((numbers[None, :] < my_resident[:, None])[:, :, None, None], re...  13.5 us
  transfers between devices with their start and end apart: 6, of which 6 were waited for; matrix products, arithmetic and copies ran while one was open for 11% of the time, Pallas kernels for 0%

profile of v4, /device:TPU:0, one launch (start us, length us, event | category | flops | bytes accessed | tf_op | source)
XLA Modules:
  0.0 553.9 jit_solution(223292223915347299)
XLA Ops:
  6.5 11.1 %fusion.74 = f32[1024,2560]{1,0:T(8,128)} fusion(bf16[1024,1024]{1,0:T(8,128)(2,1)} %param.10, bf16[1024,2560]{1,0:T(8,128)(2,1)} %param.11), kind=kOutput, calls=%fused_computation.157 | convolution fusion | flops 5368709120 | bytes 17825792 | tf_op jit(solution)/shard_map/dot_general | solution.py:126
  20.5 2.4 scatter_custom_fusion.1
  23.0 5.6 %gather_fusion.3 = bf16[8,128,512]{2,1,0:T(8,128)(2,1)} fusion(bf16[80,128,512]{2,1,0:T(8,128)(2,1)} %param.13, s32[1024]{0:T(1024)S(1)} %pad_clamp_fusion.2), kind=kCustom, calls=%fused_computation.3 | custom fusion | bytes 2097184 | tf_op jit(solution)/shard_map/gather | solution.py:178
  28.6 8.0 %all-to-all-start.1 = ((bf16[8,128,512]{2,1,0:T(8,128)(2,1)}), bf16[8,128,512]{2,1,0:T(8,128)(2,1)S(1)}, u32[]{:S(2)}, u32[]{:S(2)}) async-start(bf16[8,128,512]{2,1,0:T(8,128)(2,1)} %gather_fusion.3), calls=%async_computation.2 | async-start | bytes 2097152 | tf_op jit(solution)/shard_map/all_to_all | solution.py:177
  37.3 53.3 %all-to-all-done.1 = bf16[8,128,512]{2,1,0:T(8,128)(2,1)S(1)} async-done(((bf16[8,128,512]{2,1,0:T(8,128)(2,1)}), bf16[8,128,512]{2,1,0:T(8,128)(2,1)S(1)}, u32[]{:S(2)}, u32[]{:S(2)}) %all-to-all-start.1) | async-done | bytes 1048608 | tf_op jit(solution)/shard_map/all_to_all | solution.py:177
  90.6 1.6 gather_fusion.4
  92.2 3.6 all-to-all-start.2
  95.8 2.4 scatter_custom_fusion
  98.2 10.0 %gather_fusion.1 = bf16[64,128,512]{2,1,0:T(8,128)(2,1)} fusion(bf16[80,128,512]{2,1,0:T(8,128)(2,1)} %param.13, s32[1024]{0:T(1024)S(1)} %pad_clamp_fusion.4), kind=kCustom, calls=%fused_computation.1 | custom fusion | bytes 16777472 | tf_op jit(solution)/shard_map/gather | solution.py:175
  108.2 39.4 %all-to-all-done.2 = bf16[8,128,512]{2,1,0:T(8,128)(2,1)S(1)} async-done(((bf16[8,128,512]{2,1,0:T(8,128)(2,1)}), bf16[8,128,512]{2,1,0:T(8,128)(2,1)S(1)}, u32[]{:S(2)}, u32[]{:S(2)}) %all-to-all-start.2) | async-done | bytes 1048608 | tf_op jit(solution)/shard_map/all_to_all | solution.py:184
  147.7 5.0 all-to-all-start
  156.0 5.7 %gather_fusion = bf16[64,128,512]{2,1,0:T(8,128)(2,1)} fusion(bf16[16,128,512]{2,1,0:T(8,128)(2,1)S(1)} %bitcast.91, s32[1024]{0:T(1024)S(1)} %pad_clamp_fusion.5), kind=kCustom, calls=%fused_computation | custom fusion | bytes 16777472 | tf_op jit(solution)/shard_map/gather | solution.py:196
  162.6 5.4 gather_fusion.5
  168.0 192.8 %all-to-all-done = bf16[64,128,512]{2,1,0:T(8,128)(2,1)} async-done(((bf16[64,128,512]{2,1,0:T(8,128)(2,1)}), bf16[64,128,512]{2,1,0:T(8,128)(2,1)}, u32[]{:S(2)}, u32[]{:S(2)}) %all-to-all-start) | async-done | bytes 8388640 | tf_op jit(solution)/shard_map/all_to_all | solution.py:174
  360.8 9.0 %gather_fusion.2 = bf16[64,128,512]{2,1,0:T(8,128)(2,1)} fusion(bf16[64,128,512]{2,1,0:T(8,128)(2,1)} %all-to-all-done, s32[1024]{0:T(1024)S(1)} %pad_clamp_fusion.3), kind=kCustom, calls=%fused_computation.2 | custom fusion | bytes 16777472 | tf_op jit(solution)/shard_map/gather | solution.py:197
  369.8 13.5 %fusion.4 = bf16[2,4096,512]{2,1,0:T(8,128)(2,1)} fusion(pred[2,4096]{1,0:T(4,128)(4,1)S(1)} %get-tuple-element.43, pred[2,4096]{1,0:T(4,128)(4,1)S(1)} %get-tuple-element.44, bf16[2,4096,512]{2,1,0:T(8,128)(2,1)} %bitcast.93, bf16[2,4096,512]{2,1,0:T(8,128)(2,1)} %bitcast.94, bf16[2,4096,512]{2,1,0:T(8,128)(2,1)} %bitcast.92), kind=kLoop, calls=%fused_computation.17 | loop fusion | flops 8388608 | bytes 33570816 | tf_op jit(solution)/shard_map/jit(_where)/select_n | solution.py:199
  387.4 8.7 %select_reduce_fusion.1 = (f32[2,512]{1,0:T(2,128)S(1)}, f32[2,512,4096]{2,1,0:T(8,128)}) fusion(pred[2,4096]{1,0:T(4,128)(4,1)S(1)} %iota_compare_fusion.4, bf16[2,4096,512]{2,1,0:T(8,128)(2,1)} %fusion.4, bf16[2,2,512,128]{3,2,0,1:T(8,128)(2,1)S(1)} %copy_bitcast_fusion), kind=kOutput, calls=%fused_computation.11 | convolution fusion | flops 1086323712 | bytes 19156992 | tf_op jit(solution)/shard_map/urd,usd->urs/dot_general | solution.py:63
  396.1 8.2 %fusion.7 = f32[2,512,128]{2,1,0:T(8,128)S(1)} fusion(f32[2,512,4096]{2,1,0:T(8,128)} %get-tuple-element.38, f32[2,512]{1,0:T(2,128)S(1)} %max.18, pred[2,4096]{1,0:T(4,128)(4,1)S(1)} %iota_compare_fusion.4, bf16[2,4096,512]{2,1,0:T(8,128)(2,1)} %fusion.4), kind=kOutput, calls=%fused_computation.19 | convolution fusion | flops 1090519040 | bytes 19410944 | tf_op jit(solution)/shard_map/urs,usd->urd/dot_general | solution.py:84
  404.3 13.9 %fusion = (f32[2,512]{1,0:T(2,128)S(1)}, f32[2,512]{1,0:T(2,128)S(1)}, f32[2,512,4096]{2,1,0:T(8,128)}) fusion(f32[2,512,4096]{2,1,0:T(8,128)} %get-tuple-element.38, f32[2,512]{1,0:T(2,128)S(1)} %max.18, pred[2,4096]{1,0:T(4,128)(4,1)S(1)} %iota_compare_fusion.4, bf16[2,4096,512]{2,1,0:T(8,128)(2,1)} %fusion.4, ...), kind=kOutput, calls=%fused_computation.12 | convolution fusion | flops 1103099904 | bytes 35942400 | tf_op jit(solution)/shard_map/urd,usd->urs/dot_general | solution.py:63
  418.2 8.2 %fusion.5 = f32[2,512,128]{2,1,0:T(8,128)S(1)} fusion(f32[2,512,4096]{2,1,0:T(8,128)} %get-tuple-element.40, f32[2,512]{1,0:T(2,128)S(1)} %max.19, pred[2,4096]{1,0:T(4,128)(4,1)S(1)} %iota_compare_fusion.4, bf16[2,4096,512]{2,1,0:T(8,128)(2,1)} %fusion.4), kind=kOutput, calls=%fused_computation.18 | convolution fusion | flops 1090519040 | bytes 19410944 | tf_op jit(solution)/shard_map/urs,usd->urd/dot_general | solution.py:84
  426.4 8.0 %fusion.2 = f32[2,512]{1,0:T(2,128)S(1)} fusion(f32[2,512,4096]{2,1,0:T(8,128)} %get-tuple-element.40, f32[2,512]{1,0:T(2,128)S(1)} %max.19, pred[2,4096]{1,0:T(4,128)(4,1)S(1)} %iota_compare_fusion.4), kind=kLoop, calls=%fused_computation.14 | loop fusion | flops 16776192 | bytes 16793600 | tf_op jit(solution)/shard_map/reduce_sum | solution.py:83
  436.4 71.6 %all-gather.2.cloned.1.call-done = bf16[1024,2048]{1,0:T(8,128)(2,1)} async-done(((bf16[128,2048]{1,0:T(8,128)(2,1)}), bf16[1024,2048]{1,0:T(8,128)(2,1)}) %all-gather.2.cloned.1.call-update) | async-done | bytes 4194320 | tf_op jit(solution)/shard_map/all_gather | solution.py:208
  508.1 9.4 %convolution_convert_fusion = bf16[1024,1024]{1,0:T(8,128)(2,1)} fusion(bf16[1024,2048]{1,0:T(8,128)(2,1)} %all-gather.2.cloned.1.call-done, bf16[2048,1024]{1,0:T(8,128)(2,1)} %param.12), kind=kOutput, calls=%fused_computation.28 | convolution fusion | flops 4296015872 | bytes 10485760 | tf_op jit(solution)/shard_map/dot_general | solution.py:207
  517.5 29.9 %reduce-scatter.5.cloned.1.call-done = bf16[256,1024]{1,0:T(8,128)(2,1)} async-done(((bf16[1024,1024]{1,0:T(8,128)(2,1)}), bf16[256,1024]{1,0:T(8,128)(2,1)}) %reduce-scatter.5.cloned.1.call-update) | async-done | bytes 524304 | tf_op jit(solution)/shard_map/reduce_scatter | solution.py:212
  (94 shorter events, 13.8 us)
Async XLA Ops:
  6.5 149.4 %copy-start = (bf16[2,8,128,512]{3,2,1,0:T(8,128)(2,1)S(1)}, bf16[2,8,128,512]{3,2,1,0:T(8,128)(2,1)}, u32[]{:S(2)}) copy-start(bf16[2,8,128,512]{3,2,1,0:T(8,128)(2,1)} %param.14) | copy-start | bytes 6291460
  6.5 377.6 %reduce-scatter.3.cloned.1.call-start = ((), (), s32[]{:S(2)}) async-start(), calls=%async_computation.5 | async-start | bytes 11796480 | tf_op jit(solution)/shard_map/reduce_scatter | solution.py:130
  17.6 0.7 copy-start.2
  17.6 0.9 copy-start.3
  28.6 62.0 %all-to-all-start.1 = ((bf16[8,128,512]{2,1,0:T(8,128)(2,1)}), bf16[8,128,512]{2,1,0:T(8,128)(2,1)S(1)}, u32[]{:S(2)}, u32[]{:S(2)}) async-start(bf16[8,128,512]{2,1,0:T(8,128)(2,1)} %gather_fusion.3), calls=%async_computation.2 | async-start | bytes 2097152 | tf_op jit(solution)/shard_map/all_to_all | solution.py:177
  92.2 55.5 %all-to-all-start.2 = ((bf16[8,128,512]{2,1,0:T(8,128)(2,1)}), bf16[8,128,512]{2,1,0:T(8,128)(2,1)S(1)}, u32[]{:S(2)}, u32[]{:S(2)}) async-start(bf16[8,128,512]{2,1,0:T(8,128)(2,1)} %gather_fusion.4), calls=%async_computation.3 | async-start | bytes 2097152 | tf_op jit(solution)/shard_map/all_to_all | solution.py:184
  108.2 44.8 %copy-start.5 = (s32[16]{0:T(128)S(1)}, s32[16]{0:T(128)}, u32[]{:S(2)}) copy-start(s32[16]{0:T(128)} %param.18) | copy-start | bytes 196
  147.7 213.1 %all-to-all-start = ((bf16[64,128,512]{2,1,0:T(8,128)(2,1)}), bf16[64,128,512]{2,1,0:T(8,128)(2,1)}, u32[]{:S(2)}, u32[]{:S(2)}) async-start(bf16[64,128,512]{2,1,0:T(8,128)(2,1)} %gather_fusion.1), calls=%async_computation.1 | async-start | bytes 16777216 | tf_op jit(solution)/shard_map/all_to_all | solution.py:174
  152.6 355.4 %all-gather.2.cloned.1.call-start = ((), (), s32[]{:S(2)}) async-start(), calls=%async_computation.6 | async-start | bytes 4718592 | tf_op jit(solution)/shard_map/all_gather | solution.py:208
  156.0 5.8 %copy-start.4 = (s32[16]{0:T(128)S(1)}, s32[16]{0:T(128)}, u32[]{:S(2)}) copy-start(s32[16]{0:T(128)} %param.17) | copy-start | bytes 196
  436.4 111.0 %reduce-scatter.5.cloned.1.call-start = ((), (), s32[]{:S(2)}) async-start(), calls=%async_computation.7 | async-start | bytes 2621440 | tf_op jit(solution)/shard_map/reduce_scatter | solution.py:212
  508.1 39.3 %copy-start.1 = (bf16[2,8,128,512]{3,2,1,0:T(8,128)(2,1)S(1)}, bf16[2,8,128,512]{3,2,1,0:T(8,128)(2,1)}, u32[]{:S(2)}) copy-start(bf16[2,8,128,512]{3,2,1,0:T(8,128)(2,1)} %param.14) | copy-start | bytes 6291460
Sparse Core Ops, SparseCore 0:
  17.8 366.3 reduce-scatter.2
  436.5 71.5 all-gather.1
  517.6 29.7 reduce-scatter.4

commit v5 on v2

--- a/solution.py
+++ b/solution.py
@@ -176,7 +176,6 @@
         spread[hot_owner], "pool", split_axis=0, concat_axis=0, tiled=True
     ).reshape(capacity, PAGE, kv_cols)
     local_source = resident_kv.reshape(USER_DEV * MAXRES, PAGE, kv_cols)
-    outputs = []
     my_owner = lax.dynamic_index_in_dim(owner_blocks, my_index, 0, keepdims=False).reshape(
         USER_DEV, MAXP
     )
@@ -184,33 +183,59 @@
         USER_DEV, MAXP
     )
     numbers = jnp.arange(MAXP)
-    for local_user in range(USER_DEV):
-        owner = my_owner[local_user]
-        rank = my_rank[local_user]
+
+    def attend_user(operands):
+        local_user, owner, rank, resident, user_queries, user_key, user_value, seen, length = operands
         resident_pages = local_source[local_user * MAXRES + jnp.minimum(numbers, MAXRES - 1)]
         regular_pages = arrived[owner * capacity + jnp.minimum(rank, capacity - 1)]
         extra_pages = extra[jnp.clip(rank - capacity, 0, capacity - 1)]
         history = jnp.where(
-            (numbers < my_resident[local_user])[:, None, None],
+            (numbers < resident)[:, None, None],
             resident_pages,
             jnp.where((rank < capacity)[:, None, None], regular_pages, extra_pages),
         ).reshape(MAXP * PAGE, kv_cols)
-        result = attend_dense(
-            query_rows[local_user],
-            history,
-            draft_key[local_user],
-            draft_value[local_user],
-            visible[local_user],
-            my_lengths[local_user],
-        )
-        outputs.append(finish(result, DRAFT))
-    attention = jnp.concatenate(outputs, 0)
+        result = attend_dense(user_queries, history, user_key, user_value, seen, length)
+        return finish(result, DRAFT)
+
+    attention = lax.map(
+        attend_user,
+        (
+            jnp.arange(USER_DEV),
+            my_owner,
+            my_rank,
+            my_resident,
+            query_rows,
+            draft_key,
+            draft_value,
+            visible,
+            my_lengths,
+        ),
+    ).reshape(USER_DEV * DRAFT, -1)
     partial_out = jnp.dot(
         lax.all_gather(attention, "pool", axis=0, tiled=True),
         w_out,
         preferred_element_type=jnp.float32,
     )
-    return lax.psum_scatter(partial_out.astype(jnp.bfloat16), "tp", scatter_dimension=0, tiled=True)
+    return halving_sum(partial_out, "tp").astype(jnp.bfloat16)
+
+
+def halving_sum(partial, axis_name):
+    size = lax.axis_size(axis_name)
+    me = lax.axis_index(axis_name)
+    rows = partial.shape[0] // size
+    cols = partial.shape[1]
+    held = partial
+    bit = 1
+    while bit < size:
+        blocks = held.shape[0] // rows
+        grouped = held.reshape(blocks // 2, 2, rows, cols)
+        mine = (me // bit) % 2
+        keep = lax.dynamic_index_in_dim(grouped, mine, 1, keepdims=False)
+        send = lax.dynamic_index_in_dim(grouped, 1 - mine, 1, keepdims=False)
+        received = lax.ppermute(send, axis_name, [(j, j ^ bit) for j in range(size)])
+        held = (keep + received).reshape(blocks // 2 * rows, cols)
+        bit *= 2
+    return held
 
 
 def solution(mesh):

time: 546 us -> 604 us (1.11); the launches traced: 537 us -> 603 us
  waiting for transfers between devices: 386 us -> 421 us
  local copies, waits for them, and re-layouts: 52.9 us -> 70.3 us
  matrix products: 40 us -> 48.6 us
    reduce_scatter x1, waiting for transfers between devices: 0.01 us -> 229 us  [body(): lax.psum_scatter(jnp.dot(draft_states, w_qkv, preferred_element_type=jnp....]
    all_to_all x1, waiting for transfers between devices: 222 us -> 0.01 us  [body(): lax.all_to_all(kv_pool[pack_index], 'pool', split_axis=0, concat_axis=0,...]
    reduce_scatter x1 -> x0, waiting for transfers between devices: 29.8 us -> none  [body(): lax.psum_scatter(partial_out.astype(jnp.bfloat16), 'tp', scatter_dimensio...]
    ppermute x0 -> x2, waiting for transfers between devices: none -> 28.3 us  [halving_sum(): lax.ppermute(send, axis_name, [(j, j ^ bit) for j in range(size)])]
    all_to_all x1, waiting for transfers between devices: 25.7 us -> 53.3 us  [body(): lax.all_to_all(kv_pool[extra_index].reshape(pool_size, piece_rows, kv_col...]
    dot_general x4, matrix products: 11 us -> 21.9 us  [attend_dense(): jnp.einsum('rd,sd->rs', queries[head], keys, preferred_element_type=jnp.f...]
    select_n x6 -> x5, other arithmetic: 14.1 us -> 11.2 us  [the longest x2 11.2 us: attend_user(): jnp.where((numbers < resident)[:, None, None], resident_pages, jnp.where(...]
  transfers between devices with their start and end apart: 6 -> 7, of which waited for: 5 -> 6; matrix products, arithmetic and copies ran while one was open for 13% -> 6% of each run, Pallas kernels for 0% -> 0%
where the time goes in v5:
time: 604 us; the launch traced here: 603 us
  waiting for transfers between devices  421 us (70%)
  local copies, waits for them, and re-layouts  70.3 us (12%)
  matrix products  48.6 us (8%)
  other arithmetic  29.2 us (5%)
  starting transfers between devices  18.1 us (3%)
  between operations  13.7 us (2%)
    reduce_scatter x1, waiting for transfers between devices, body(): lax.psum_scatter(jnp.dot(draft_states, w_qkv, preferred_element_type=jnp....  229 us
    all_gather x1, waiting for transfers between devices, body(): lax.all_gather(attention, 'pool', axis=0, tiled=True)  71.7 us
    all_to_all x1, waiting for transfers between devices, body(): lax.all_to_all(kv_pool[extra_index].reshape(pool_size, piece_rows, kv_col...  53.3 us
    all_to_all x1, waiting for transfers between devices, body(): lax.all_to_all(spread[hot_owner], 'pool', split_axis=0, concat_axis=0, ti...  39.4 us
    ppermute x2, waiting for transfers between devices, halving_sum(): lax.ppermute(send, axis_name, [(j, j ^ bit) for j in range(size)])  28.3 us
    dot_general x4, matrix products, attend_dense(): jnp.einsum('rd,sd->rs', queries[head], keys, preferred_element_type=jnp.f...  21.9 us
    gather x2, local copies, waits for them, and re-layouts, attend_user(): regular_pages = arrived[owner * capacity + jnp.minimum(rank, capacity - 1)]  12.3 us
  transfers between devices with their start and end apart: 7, of which 6 were waited for; matrix products, arithmetic and copies ran while one was open for 6% of the time, Pallas kernels for 0%

profile of v5, /device:TPU:0, one launch (start us, length us, event | category | flops | bytes accessed | tf_op | source)
XLA Modules:
  0.0 603.0 jit_solution(13495931558460901073)
XLA Ops:
  8.1 10.6 %fusion.80 = f32[1024,2560]{1,0:T(8,128)} fusion(bf16[1024,1024]{1,0:T(8,128)(2,1)S(1)} %copy-done, bf16[1024,2560]{1,0:T(8,128)(2,1)} %param.13), kind=kOutput, calls=%fused_computation.171 | convolution fusion | flops 5368709120 | bytes 17825792 | tf_op jit(solution)/shard_map/dot_general | solution.py:122
  24.1 5.6 gather_fusion.4
  29.7 8.0 %all-to-all-start.1 = ((bf16[8,128,512]{2,1,0:T(8,128)(2,1)}), bf16[8,128,512]{2,1,0:T(8,128)(2,1)S(1)}, u32[]{:S(2)}, u32[]{:S(2)}) async-start(bf16[8,128,512]{2,1,0:T(8,128)(2,1)} %gather_fusion.4), calls=%async_computation.2 | async-start | bytes 2097152 | tf_op jit(solution)/shard_map/all_to_all | solution.py:168
  38.4 53.3 %all-to-all-done.1 = bf16[8,128,512]{2,1,0:T(8,128)(2,1)S(1)} async-done(((bf16[8,128,512]{2,1,0:T(8,128)(2,1)}), bf16[8,128,512]{2,1,0:T(8,128)(2,1)S(1)}, u32[]{:S(2)}, u32[]{:S(2)}) %all-to-all-start.1) | async-done | bytes 1048608 | tf_op jit(solution)/shard_map/all_to_all | solution.py:168
  93.3 3.6 all-to-all-start.2
  99.3 10.0 %gather_fusion.3 = bf16[64,128,512]{2,1,0:T(8,128)(2,1)} fusion(bf16[80,128,512]{2,1,0:T(8,128)(2,1)} %param.15, s32[1024]{0:T(1024)S(1)} %pad_clamp_fusion.5), kind=kCustom, calls=%fused_computation.3 | custom fusion | bytes 16777472 | tf_op jit(solution)/shard_map/gather | solution.py:166
  109.4 39.4 %all-to-all-done.2 = bf16[8,128,512]{2,1,0:T(8,128)(2,1)S(1)} async-done(((bf16[8,128,512]{2,1,0:T(8,128)(2,1)}), bf16[8,128,512]{2,1,0:T(8,128)(2,1)S(1)}, u32[]{:S(2)}, u32[]{:S(2)}) %all-to-all-start.2) | async-done | bytes 1048608 | tf_op jit(solution)/shard_map/all_to_all | solution.py:175
  148.8 5.0 all-to-all-start
  156.8 228.5 %reduce-scatter.2.cloned.1.call-done = f32[128,2560]{1,0:T(8,128)} async-done(((f32[1024,2560]{1,0:T(8,128)}), f32[128,2560]{1,0:T(8,128)}) %reduce-scatter.2.cloned.1.call-update) | async-done | bytes 1310736 | tf_op jit(solution)/shard_map/reduce_scatter | solution.py:121
  393.7 82.5 %while.14 = (s32[]{:T(128)}, bf16[2,64,2048]{2,1,0:T(8,128)(2,1)S(1)}, s32[2]{0:T(128)S(1)}, bf16[2,2,512,128]{3,2,1,0:T(8,128)(2,1)S(1)}, s32[2]{0:T(128)S(1)},...) while((s32[]{:T(128)}, ...), condition=%wide.region_17.18_spmd.clone.clone, body=%wide.region_8.17_spmd.clone.clone.sunk | while | flops 2232489472 | bytes 168841696 | solution.py:200
  397.9 6.2 %gather_fusion.1 = bf16[32,128,512]{2,1,0:T(8,128)(2,1)} fusion(bf16[64,128,512]{2,1,0:T(8,128)(2,1)} %get-tuple-element.563, s32[1024]{0:T(1024)S(1)} %pad_clamp_fusion.10), kind=kCustom, calls=%fused_computation.1.clone.clone.1 | custom fusion | bytes 8388736 | tf_op jit(solution)/shard_map/while/body/eval_jaxpr/gather | solution.py:190
  404.0 4.4 gather_fusion.2
  409.7 5.6 fusion.113
  416.8 4.6 select_reduce_fusion.6
  421.6 6.4 %fusion.114 = (f32[512]{0:T(512)S(1)}, f32[512]{0:T(512)S(1)}, f32[512,4096]{1,0:T(8,128)S(1)}) fusion(f32[512,4096]{1,0:T(8,128)} %get-tuple-element.508, f32[512]{0:T(512)S(1)} %max.30, pred[4096]{0:T(1024)(128)(4,1)S(1)} %iota_compare_fusion.8, bf16[4096,512]{1,0:T(8,128)(2,1)} %copy-done.3, bf16[2,2,512,128]{3,2,1,0:T(8,128)(2,1)S(1)} %get-tuple-element.557, ...), kind=kOutput, calls=%fused_computation.13.clone.1 | convolution fusion | flops 551549952 | bytes 17967620 | tf_op jit(solution)/shard_map/while/body/eval_jaxpr/rd,sd->rs/dot_general | solution.py:63
  439.1 6.2 %gather_fusion.1 = bf16[32,128,512]{2,1,0:T(8,128)(2,1)} fusion(bf16[64,128,512]{2,1,0:T(8,128)(2,1)} %get-tuple-element.563, s32[1024]{0:T(1024)S(1)} %pad_clamp_fusion.10), kind=kCustom, calls=%fused_computation.1.clone.clone.1 | custom fusion | bytes 8388736 | tf_op jit(solution)/shard_map/while/body/eval_jaxpr/gather | solution.py:190
  445.3 4.4 gather_fusion.2
  450.9 5.6 fusion.113
  458.0 4.6 select_reduce_fusion.6
  462.9 6.4 %fusion.114 = (f32[512]{0:T(512)S(1)}, f32[512]{0:T(512)S(1)}, f32[512,4096]{1,0:T(8,128)S(1)}) fusion(f32[512,4096]{1,0:T(8,128)} %get-tuple-element.508, f32[512]{0:T(512)S(1)} %max.30, pred[4096]{0:T(1024)(128)(4,1)S(1)} %iota_compare_fusion.8, bf16[4096,512]{1,0:T(8,128)(2,1)} %copy-done.3, bf16[2,2,512,128]{3,2,1,0:T(8,128)(2,1)S(1)} %get-tuple-element.557, ...), kind=kOutput, calls=%fused_computation.13.clone.1 | convolution fusion | flops 551549952 | bytes 17967620 | tf_op jit(solution)/shard_map/while/body/eval_jaxpr/rd,sd->rs/dot_general | solution.py:63
  477.0 71.7 %all-gather.2.cloned.1.call-done = bf16[1024,2048]{1,0:T(8,128)(2,1)} async-done(((bf16[128,2048]{1,0:T(8,128)(2,1)}), bf16[1024,2048]{1,0:T(8,128)(2,1)}) %all-gather.2.cloned.1.call-update) | async-done | bytes 4194320 | tf_op jit(solution)/shard_map/all_gather | solution.py:215
  548.8 7.5 %fusion.81 = f32[1024,1024]{1,0:T(8,128)S(1)} fusion(bf16[1024,2048]{1,0:T(8,128)(2,1)} %all-gather.2.cloned.1.call-done, bf16[2048,1024]{1,0:T(8,128)(2,1)} %param.14), kind=kOutput, calls=%fused_computation.172 | convolution fusion | flops 4294967296 | bytes 12582912 | tf_op jit(solution)/shard_map/dot_general | solution.py:214
  559.8 4.5 collective-permute-done
  569.9 23.8 %collective-permute-done.1 = f32[1,256,1024]{2,1,0:T(8,128)} collective-permute-done((f32[1,256,1024]{2,1,0:T(8,128)S(1)}, f32[1,256,1024]{2,1,0:T(8,128)}, u32[]{:S(2)}, u32[]{:S(2)}) %collective-permute-start.1) | collective-permute-done | bytes 1048608 | tf_op jit(solution)/shard_map/ppermute | solution.py:235
  (156 shorter events, 61.8 us)
Async XLA Ops:
  6.5 1.6 copy-start
  6.5 378.8 %reduce-scatter.2.cloned.1.call-start = ((), (), s32[]{:S(2)}) async-start(), calls=%async_computation.4 | async-start | bytes 11796480 | tf_op jit(solution)/shard_map/reduce_scatter | solution.py:121
  18.7 0.7 copy-start.8
  18.7 2.8 copy-start.9
  29.7 62.0 %all-to-all-start.1 = ((bf16[8,128,512]{2,1,0:T(8,128)(2,1)}), bf16[8,128,512]{2,1,0:T(8,128)(2,1)S(1)}, u32[]{:S(2)}, u32[]{:S(2)}) async-start(bf16[8,128,512]{2,1,0:T(8,128)(2,1)} %gather_fusion.4), calls=%async_computation.2 | async-start | bytes 2097152 | tf_op jit(solution)/shard_map/all_to_all | solution.py:168
  93.3 55.5 %all-to-all-start.2 = ((bf16[8,128,512]{2,1,0:T(8,128)(2,1)}), bf16[8,128,512]{2,1,0:T(8,128)(2,1)S(1)}, u32[]{:S(2)}, u32[]{:S(2)}) async-start(bf16[8,128,512]{2,1,0:T(8,128)(2,1)} %gather_fusion.5), calls=%async_computation.3 | async-start | bytes 2097152 | tf_op jit(solution)/shard_map/all_to_all | solution.py:175
  109.4 46.5 %copy-start.11 = (s32[16]{0:T(128)S(1)}, s32[16]{0:T(128)}, u32[]{:S(2)}) copy-start(s32[16]{0:T(128)} %param.20) | copy-start | bytes 196
  109.4 46.9 %copy-start.10 = (s32[16]{0:T(128)S(1)}, s32[16]{0:T(128)}, u32[]{:S(2)}) copy-start(s32[16]{0:T(128)} %param.19) | copy-start | bytes 196
  148.8 244.9 %all-to-all-start = ((bf16[64,128,512]{2,1,0:T(8,128)(2,1)}), bf16[64,128,512]{2,1,0:T(8,128)(2,1)}, u32[]{:S(2)}, u32[]{:S(2)}) async-start(bf16[64,128,512]{2,1,0:T(8,128)(2,1)} %gather_fusion.3), calls=%async_computation.1 | async-start | bytes 16777216 | tf_op jit(solution)/shard_map/all_to_all | solution.py:165
  153.7 395.0 %all-gather.2.cloned.1.call-start = ((), (), s32[]{:S(2)}) async-start(), calls=%async_computation.5 | async-start | bytes 4718592 | tf_op jit(solution)/shard_map/all_gather | solution.py:215
  415.3 6.1 %copy-start.3 = (bf16[4096,512]{1,0:T(8,128)(2,1)}, bf16[4096,512]{1,0:T(8,128)(2,1)S(1)}, u32[]{:S(2)}) copy-start(bf16[4096,512]{1,0:T(8,128)(2,1)S(1)} %fusion.113) | copy-start | bytes 12582916 | tf_op jit(solution)/shard_map/while
  421.6 6.6 %copy-start.2 = (f32[512,4096]{1,0:T(8,128)S(1)}, f32[512,4096]{1,0:T(8,128)}, u32[]{:S(2)}) copy-start(f32[512,4096]{1,0:T(8,128)} %get-tuple-element.508) | copy-start | bytes 25165828 | tf_op jit(solution)/shard_map/while
  421.6 7.3 %copy-start.4 = (bf16[4096,512]{1,0:T(8,128)(2,1)S(1)}, bf16[4096,512]{1,0:T(8,128)(2,1)}, u32[]{:S(2)}) copy-start(bf16[4096,512]{1,0:T(8,128)(2,1)} %copy-done.3) | copy-start | bytes 12582916 | tf_op jit(solution)/shard_map/while
  456.5 6.1 %copy-start.3 = (bf16[4096,512]{1,0:T(8,128)(2,1)}, bf16[4096,512]{1,0:T(8,128)(2,1)S(1)}, u32[]{:S(2)}) copy-start(bf16[4096,512]{1,0:T(8,128)(2,1)S(1)} %fusion.113) | copy-start | bytes 12582916 | tf_op jit(solution)/shard_map/while
  462.9 6.6 %copy-start.2 = (f32[512,4096]{1,0:T(8,128)S(1)}, f32[512,4096]{1,0:T(8,128)}, u32[]{:S(2)}) copy-start(f32[512,4096]{1,0:T(8,128)} %get-tuple-element.508) | copy-start | bytes 25165828 | tf_op jit(solution)/shard_map/while
  462.9 7.3 %copy-start.4 = (bf16[4096,512]{1,0:T(8,128)(2,1)S(1)}, bf16[4096,512]{1,0:T(8,128)(2,1)}, u32[]{:S(2)}) copy-start(bf16[4096,512]{1,0:T(8,128)(2,1)} %copy-done.3) | copy-start | bytes 12582916 | tf_op jit(solution)/shard_map/while
  476.2 0.8 copy-start.7
  556.3 1.9 copy-start.6
  559.8 4.5 collective-permute-start
  559.8 36.4 %copy-start.1 = (bf16[1024,1024]{1,0:T(8,128)(2,1)S(1)}, bf16[1024,1024]{1,0:T(8,128)(2,1)}, u32[]{:S(2)}) copy-start(bf16[1024,1024]{1,0:T(8,128)(2,1)} %param.12) | copy-start | bytes 6291460
  566.9 1.4 copy-start.5
  568.4 25.4 %collective-permute-start.1 = (f32[1,256,1024]{2,1,0:T(8,128)S(1)}, f32[1,256,1024]{2,1,0:T(8,128)}, u32[]{:S(2)}, u32[]{:S(2)}) collective-permute-start(f32[1,256,1024]{2,1,0:T(8,128)S(1)} %constant_dynamic-slice_fusion.6), channel_id=1, source_target_pairs={{0,2},{1,3},{2,0},{3,1},{4,6},{5,7},{6,4},{7,5},{8,10},{9,11},{10,... | collective-permute-start | bytes 3145736 | tf_op jit(solution)/shard_map/ppermute | solution.py:235
Sparse Core Ops, SparseCore 0:
  18.9 366.4 reduce-scatter.1
  477.1 71.5 all-gather.1

commit v6 on v2

--- a/solution.py
+++ b/solution.py
@@ -204,13 +204,37 @@
             my_lengths[local_user],
         )
         outputs.append(finish(result, DRAFT))
-    attention = jnp.concatenate(outputs, 0)
-    partial_out = jnp.dot(
-        lax.all_gather(attention, "pool", axis=0, tiled=True),
-        w_out,
-        preferred_element_type=jnp.float32,
-    )
-    return lax.psum_scatter(partial_out.astype(jnp.bfloat16), "tp", scatter_dimension=0, tiled=True)
+    tp_size = lax.axis_size("tp")
+    pieces = []
+    for user_attention in outputs:
+        partial_out = jnp.dot(
+            lax.all_gather(user_attention, "pool", axis=0, tiled=True),
+            w_out,
+            preferred_element_type=jnp.float32,
+        )
+        pieces.append(halving_sum(partial_out, "tp").reshape(pool_size // tp_size, DRAFT, -1))
+    return jnp.stack(pieces, 1).reshape(pool_size // tp_size * USER_DEV * DRAFT, -1).astype(
+        jnp.bfloat16
+    )
+
+
+def halving_sum(partial, axis_name):
+    size = lax.axis_size(axis_name)
+    me = lax.axis_index(axis_name)
+    rows = partial.shape[0] // size
+    cols = partial.shape[1]
+    held = partial
+    bit = 1
+    while bit < size:
+        blocks = held.shape[0] // rows
+        grouped = held.reshape(blocks // 2, 2, rows, cols)
+        mine = (me // bit) % 2
+        keep = lax.dynamic_index_in_dim(grouped, mine, 1, keepdims=False)
+        send = lax.dynamic_index_in_dim(grouped, 1 - mine, 1, keepdims=False)
+        received = lax.ppermute(send, axis_name, [(j, j ^ bit) for j in range(size)])
+        held = (keep + received).reshape(blocks // 2 * rows, cols)
+        bit *= 2
+    return held
 
 
 def solution(mesh):

time: 546 us -> 557 us (1.020)
  local copies, waits for them, and re-layouts: 52.9 us -> 59.8 us
  other arithmetic: 27.6 us -> 33.4 us
    reduce_scatter x1 -> x0, waiting for transfers between devices: 29.8 us -> none  [body(): lax.psum_scatter(partial_out.astype(jnp.bfloat16), 'tp', scatter_dimensio...]
    ppermute x0 -> x4, waiting for transfers between devices: none -> 19.2 us  [halving_sum(): lax.ppermute(send, axis_name, [(j, j ^ bit) for j in range(size)])]
    all_gather x1 -> x2, waiting for transfers between devices: 70 us -> 76.6 us  [body(): lax.all_gather(user_attention, 'pool', axis=0, tiled=True)]
  transfers between devices with their start and end apart: 6 -> 10, of which waited for: 5 -> 7; matrix products, arithmetic and copies ran while one was open for 13% -> 18% of each run, Pallas kernels for 0% -> 0%
where the time goes in v6:
time: 557 us; the launch traced here: 548 us
  waiting for transfers between devices  382 us (69%)
  local copies, waits for them, and re-layouts  59.8 us (11%)
  matrix products  40.6 us (7%)
  other arithmetic  33.4 us (6%)
  starting transfers between devices  18.1 us (3%)
  between operations  14.2 us (3%)
    all_to_all x1, waiting for transfers between devices, body(): lax.all_to_all(kv_pool[pack_index], 'pool', split_axis=0, concat_axis=0,...  222 us
    all_gather x2, waiting for transfers between devices, body(): lax.all_gather(user_attention, 'pool', axis=0, tiled=True)  76.6 us
    all_to_all x1, waiting for transfers between devices, body(): lax.all_to_all(spread[hot_owner], 'pool', split_axis=0, concat_axis=0, ti...  38.4 us
    all_to_all x1, waiting for transfers between devices, body(): lax.all_to_all(kv_pool[extra_index].reshape(pool_size, piece_rows, kv_col...  25.7 us
    ppermute x4, waiting for transfers between devices, halving_sum(): lax.ppermute(send, axis_name, [(j, j ^ bit) for j in range(size)])  19.2 us
    select_n x2, other arithmetic, body(): jnp.where((numbers < my_resident[local_user])[:, None, None], resident_pa...  14.1 us
    gather x2, local copies, waits for them, and re-layouts, body(): regular_pages = arrived[owner * capacity + jnp.minimum(rank, capacity - 1)]  12.6 us
  transfers between devices with their start and end apart: 10, of which 7 were waited for; matrix products, arithmetic and copies ran while one was open for 18% of the time, Pallas kernels for 0%

profile of v6, /device:TPU:0, one launch (start us, length us, event | category | flops | bytes accessed | tf_op | source)
XLA Modules:
  0.0 548.4 jit_solution(2004358901668572680)
XLA Ops:
  13.4 5.6 %gather_fusion.3 = bf16[8,128,512]{2,1,0:T(8,128)(2,1)} fusion(bf16[80,128,512]{2,1,0:T(8,128)(2,1)} %param.13, s32[1024]{0:T(1024)S(1)} %pad_clamp_fusion.5), kind=kCustom, calls=%fused_computation.3 | custom fusion | bytes 2097184 | tf_op jit(solution)/shard_map/gather | solution.py:169
  19.0 7.3 %all-to-all-start.1 = ((bf16[8,128,512]{2,1,0:T(8,128)(2,1)}), bf16[8,128,512]{2,1,0:T(8,128)(2,1)S(1)}, u32[]{:S(2)}, u32[]{:S(2)}) async-start(bf16[8,128,512]{2,1,0:T(8,128)(2,1)} %gather_fusion.3), calls=%async_computation.2 | async-start | bytes 2097152 | tf_op jit(solution)/shard_map/all_to_all | solution.py:168
  26.3 10.9 %fusion.130 = f32[1024,2560]{1,0:T(8,128)} fusion(bf16[1024,1024]{1,0:T(8,128)(2,1)} %param.10, bf16[1024,2560]{1,0:T(8,128)(2,1)} %param.11), kind=kOutput, calls=%fused_computation.253 | convolution fusion | flops 5368709120 | bytes 17825792 | tf_op jit(solution)/shard_map/dot_general | solution.py:122
  38.1 25.7 %all-to-all-done.1 = bf16[8,128,512]{2,1,0:T(8,128)(2,1)S(1)} async-done(((bf16[8,128,512]{2,1,0:T(8,128)(2,1)}), bf16[8,128,512]{2,1,0:T(8,128)(2,1)S(1)}, u32[]{:S(2)}, u32[]{:S(2)}) %all-to-all-start.1) | async-done | bytes 1048608 | tf_op jit(solution)/shard_map/all_to_all | solution.py:168
  65.4 3.6 all-to-all-start.2
  71.4 9.7 %gather_fusion.1 = bf16[64,128,512]{2,1,0:T(8,128)(2,1)} fusion(bf16[80,128,512]{2,1,0:T(8,128)(2,1)} %param.13, s32[1024]{0:T(1024)S(1)} %pad_clamp_fusion.7), kind=kCustom, calls=%fused_computation.1 | custom fusion | bytes 16777472 | tf_op jit(solution)/shard_map/gather | solution.py:166
  81.2 38.4 %all-to-all-done.2 = bf16[8,128,512]{2,1,0:T(8,128)(2,1)S(1)} async-done(((bf16[8,128,512]{2,1,0:T(8,128)(2,1)}), bf16[8,128,512]{2,1,0:T(8,128)(2,1)S(1)}, u32[]{:S(2)}, u32[]{:S(2)}) %all-to-all-start.2) | async-done | bytes 1048608 | tf_op jit(solution)/shard_map/all_to_all | solution.py:175
  119.6 5.1 all-to-all-start
  129.7 2.9 gather_fusion.6
  137.5 2.8 gather_fusion.5
  143.1 222.4 %all-to-all-done = bf16[64,128,512]{2,1,0:T(8,128)(2,1)} async-done(((bf16[64,128,512]{2,1,0:T(8,128)(2,1)}), bf16[64,128,512]{2,1,0:T(8,128)(2,1)}, u32[]{:S(2)}, u32[]{:S(2)}) %all-to-all-start) | async-done | bytes 8388640 | tf_op jit(solution)/shard_map/all_to_all | solution.py:165
  365.5 6.3 %gather_fusion.2 = bf16[32,128,512]{2,1,0:T(8,128)(2,1)} fusion(bf16[64,128,512]{2,1,0:T(8,128)(2,1)} %all-to-all-done, s32[1024]{0:T(1024)S(1)} %pad_clamp_fusion.6), kind=kCustom, calls=%fused_computation.2 | custom fusion | bytes 8388736 | tf_op jit(solution)/shard_map/gather | solution.py:191
  371.8 6.3 %gather_fusion.7 = bf16[32,128,512]{2,1,0:T(8,128)(2,1)} fusion(bf16[64,128,512]{2,1,0:T(8,128)(2,1)} %all-to-all-done, s32[1024]{0:T(1024)S(1)} %pad_clamp_fusion.1), kind=kCustom, calls=%fused_computation.7 | custom fusion | bytes 8388736 | tf_op jit(solution)/shard_map/gather | solution.py:191
  378.1 9.6 %fusion.9 = bf16[4096,512]{1,0:T(8,128)(2,1)} fusion(bf16[32,128,512]{2,1,0:T(8,128)(2,1)} %gather_fusion.5, bf16[32,128,512]{2,1,0:T(8,128)(2,1)} %gather_fusion.2, bf16[32,128,512]{2,1,0:T(8,128)(2,1)} %gather_fusion, pred[4096]{0:T(1024)(128)(4,1)S(1)} %get-tuple-element.68, pred[4096]{0:T(1024)(128)(4,1)S(1)} %broadcast_bitcast_fusion.5), kind=kLoop, calls=%fused_computation.30 | loop fusion | flops 4194304 | bytes 16785408 | tf_op jit(solution)/shard_map/jit(_where)/select_n | solution.py:193
  387.8 4.4 fusion.8
  397.6 3.2 fusion
  408.2 2.8 select_reduce_fusion.1
  411.2 3.2 fusion.4
  421.3 33.2 %all-gather.3.cloned.1.call-done = bf16[512,2048]{1,0:T(8,128)(2,1)} async-done(((bf16[64,2048]{1,0:T(8,128)(2,1)}), bf16[512,2048]{1,0:T(8,128)(2,1)}) %all-gather.3.cloned.1.call-update) | async-done | bytes 2097168 | tf_op jit(solution)/shard_map/all_gather | solution.py:211
  454.6 5.1 fusion.131
  461.0 43.3 %all-gather.5.cloned.1.call-done = bf16[512,2048]{1,0:T(8,128)(2,1)} async-done(((bf16[64,2048]{1,0:T(8,128)(2,1)}), bf16[512,2048]{1,0:T(8,128)(2,1)}) %all-gather.5.cloned.1.call-update) | async-done | bytes 2097168 | tf_op jit(solution)/shard_map/all_gather | solution.py:211
  504.3 5.1 fusion.132
  519.1 9.9 %collective-permute-done.1 = f32[1,128,1024]{2,1,0:T(8,128)} collective-permute-done((f32[1,128,1024]{2,1,0:T(8,128)}, f32[1,128,1024]{2,1,0:T(8,128)}, u32[]{:S(2)}, u32[]{:S(2)}) %collective-permute-start.1) | collective-permute-done | bytes 524320 | tf_op jit(solution)/shard_map/ppermute | solution.py:234
  530.1 9.3 %collective-permute-done.3 = f32[1,128,1024]{2,1,0:T(8,128)} collective-permute-done((f32[1,128,1024]{2,1,0:T(8,128)}, f32[1,128,1024]{2,1,0:T(8,128)}, u32[]{:S(2)}, u32[]{:S(2)}) %collective-permute-start.3) | collective-permute-done | bytes 524320 | tf_op jit(solution)/shard_map/ppermute | solution.py:234
  (151 shorter events, 57.9 us)
Async XLA Ops:
  6.5 120.4 %copy-start = (bf16[2,8,128,512]{3,2,1,0:T(8,128)(2,1)S(1)}, bf16[2,8,128,512]{3,2,1,0:T(8,128)(2,1)}, u32[]{:S(2)}) copy-start(bf16[2,8,128,512]{3,2,1,0:T(8,128)(2,1)} %param.14) | copy-start | bytes 6291460
  19.0 44.8 %all-to-all-start.1 = ((bf16[8,128,512]{2,1,0:T(8,128)(2,1)}), bf16[8,128,512]{2,1,0:T(8,128)(2,1)S(1)}, u32[]{:S(2)}, u32[]{:S(2)}) async-start(bf16[8,128,512]{2,1,0:T(8,128)(2,1)} %gather_fusion.3), calls=%async_computation.2 | async-start | bytes 2097152 | tf_op jit(solution)/shard_map/all_to_all | solution.py:168
  26.3 365.9 %reduce-scatter.2.cloned.1.call-start = ((), (), s32[]{:S(2)}) async-start(), calls=%async_computation.4 | async-start | bytes 11796480 | tf_op jit(solution)/shard_map/reduce_scatter | solution.py:121
  65.4 54.1 %all-to-all-start.2 = ((bf16[8,128,512]{2,1,0:T(8,128)(2,1)}), bf16[8,128,512]{2,1,0:T(8,128)(2,1)S(1)}, u32[]{:S(2)}, u32[]{:S(2)}) async-start(bf16[8,128,512]{2,1,0:T(8,128)(2,1)} %gather_fusion.4), calls=%async_computation.3 | async-start | bytes 2097152 | tf_op jit(solution)/shard_map/all_to_all | solution.py:175
  81.2 45.5 %copy-start.12 = (s32[16]{0:T(128)S(1)}, s32[16]{0:T(128)}, u32[]{:S(2)}) copy-start(s32[16]{0:T(128)} %param.18) | copy-start | bytes 196
  119.6 246.0 %all-to-all-start = ((bf16[64,128,512]{2,1,0:T(8,128)(2,1)}), bf16[64,128,512]{2,1,0:T(8,128)(2,1)}, u32[]{:S(2)}, u32[]{:S(2)}) async-start(bf16[64,128,512]{2,1,0:T(8,128)(2,1)} %gather_fusion.1), calls=%async_computation.1 | async-start | bytes 16777216 | tf_op jit(solution)/shard_map/all_to_all | solution.py:165
  124.6 329.9 %all-gather.3.cloned.1.call-start = ((), (), s32[]{:S(2)}) async-start(), calls=%async_computation.5 | async-start | bytes 2359296 | tf_op jit(solution)/shard_map/all_gather | solution.py:211
  129.7 5.2 copy-start.11
  378.1 9.7 %copy-start.2 = (bf16[32,128,512]{2,1,0:T(8,128)(2,1)S(1)}, bf16[32,128,512]{2,1,0:T(8,128)(2,1)}, u32[]{:S(2)}) copy-start(bf16[32,128,512]{2,1,0:T(8,128)(2,1)} %gather_fusion.6) | copy-start | bytes 12582916
  378.1 9.7 %copy-start.3 = (bf16[32,128,512]{2,1,0:T(8,128)(2,1)S(1)}, bf16[32,128,512]{2,1,0:T(8,128)(2,1)}, u32[]{:S(2)}) copy-start(bf16[32,128,512]{2,1,0:T(8,128)(2,1)} %gather_fusion.8) | copy-start | bytes 12582916
  378.1 9.7 %copy-start.4 = (bf16[32,128,512]{2,1,0:T(8,128)(2,1)S(1)}, bf16[32,128,512]{2,1,0:T(8,128)(2,1)}, u32[]{:S(2)}) copy-start(bf16[32,128,512]{2,1,0:T(8,128)(2,1)} %gather_fusion.7) | copy-start | bytes 12582916
  393.7 2.2 copy-start.6
  408.0 96.4 %all-gather.5.cloned.1.call-start = ((), (), s32[]{:S(2)}) async-start(), calls=%async_computation.6 | async-start | bytes 2359296 | tf_op jit(solution)/shard_map/all_gather | solution.py:211
  408.2 3.0 copy-start.5
  459.7 1.3 copy-start.10
  459.8 51.4 %collective-permute-start = (f32[2,128,1024]{2,1,0:T(8,128)S(1)}, f32[2,128,1024]{2,1,0:T(8,128)}, u32[]{:S(2)}, u32[]{:S(2)}) collective-permute-start(f32[2,128,1024]{2,1,0:T(8,128)S(1)} %dynamic-slice_bitcast_fusion.1), channel_id=1, source_target_pairs={{0,1},{1,0},{2,3},{3,2},{4,5},{5,4},{6,7},{7,6},{8,9},{9,8},{10,11... | collective-permute-start | bytes 3145736 | tf_op jit(solution)/shard_map/ppermute | solution.py:234
  509.5 1.7 copy-start.8
  510.8 4.6 collective-permute-start.2
  511.2 4.2 copy-start.9
  513.0 28.4 %copy-start.1 = (bf16[2,8,128,512]{3,2,1,0:T(8,128)(2,1)S(1)}, bf16[2,8,128,512]{3,2,1,0:T(8,128)(2,1)}, u32[]{:S(2)}) copy-start(bf16[2,8,128,512]{3,2,1,0:T(8,128)(2,1)} %param.14) | copy-start | bytes 6291460
  513.9 15.1 %collective-permute-start.1 = (f32[1,128,1024]{2,1,0:T(8,128)}, f32[1,128,1024]{2,1,0:T(8,128)}, u32[]{:S(2)}, u32[]{:S(2)}) collective-permute-start(f32[1,128,1024]{2,1,0:T(8,128)} %constant_dynamic-slice_fusion.1), channel_id=1, source_target_pairs={{0,2},{1,3},{2,0},{3,1},{4,6},{5,7},{6,4},{7,5},{8,10},{9,11},{10,... | collective-permute-start | bytes 1572872 | tf_op jit(solution)/shard_map/ppermute | solution.py:234
  516.7 1.0 copy-start.7
  518.5 20.8 %collective-permute-start.3 = (f32[1,128,1024]{2,1,0:T(8,128)}, f32[1,128,1024]{2,1,0:T(8,128)}, u32[]{:S(2)}, u32[]{:S(2)}) collective-permute-start(f32[1,128,1024]{2,1,0:T(8,128)} %constant_dynamic-slice_fusion), channel_id=1, source_target_pairs={{0,2},{1,3},{2,0},{3,1},{4,6},{5,7},{6,4},{7,5},{8,10},{9,11},{10,... | collective-permute-start | bytes 1572872 | tf_op jit(solution)/shard_map/ppermute | solution.py:234
Sparse Core Ops, SparseCore 0:
  37.4 346.5 reduce-scatter.1
  408.1 46.3 all-gather.2
  456.7 47.6 all-gather.4

commit v7 on v6

--- a/solution.py
+++ b/solution.py
@@ -204,18 +204,13 @@
             my_lengths[local_user],
         )
         outputs.append(finish(result, DRAFT))
-    tp_size = lax.axis_size("tp")
-    pieces = []
-    for user_attention in outputs:
-        partial_out = jnp.dot(
-            lax.all_gather(user_attention, "pool", axis=0, tiled=True),
-            w_out,
-            preferred_element_type=jnp.float32,
-        )
-        pieces.append(halving_sum(partial_out, "tp").reshape(pool_size // tp_size, DRAFT, -1))
-    return jnp.stack(pieces, 1).reshape(pool_size // tp_size * USER_DEV * DRAFT, -1).astype(
-        jnp.bfloat16
-    )
+    attention = jnp.concatenate(outputs, 0)
+    partial_out = jnp.dot(
+        lax.all_gather(attention, "pool", axis=0, tiled=True),
+        w_out,
+        preferred_element_type=jnp.float32,
+    )
+    return halving_sum(partial_out, "tp").astype(jnp.bfloat16)
 
 
 def halving_sum(partial, axis_name):
@@ -231,8 +226,10 @@
         mine = (me // bit) % 2
         keep = lax.dynamic_index_in_dim(grouped, mine, 1, keepdims=False)
         send = lax.dynamic_index_in_dim(grouped, 1 - mine, 1, keepdims=False)
+        if bit > 1:
+            send = send.astype(jnp.bfloat16)
         received = lax.ppermute(send, axis_name, [(j, j ^ bit) for j in range(size)])
-        held = (keep + received).reshape(blocks // 2 * rows, cols)
+        held = (keep + received.astype(jnp.float32)).reshape(blocks // 2 * rows, cols)
         bit *= 2
     return held
 

time: 557 us -> 533 us (0.957); the launches traced: 548 us -> 533 us
  waiting for transfers between devices: 382 us -> 374 us
    all_gather x2 -> x1, waiting for transfers between devices: 76.6 us -> 70.3 us  [body(): lax.all_gather(attention, 'pool', axis=0, tiled=True)]
    ppermute x4 -> x2, waiting for transfers between devices: 19.2 us -> 17 us  [halving_sum(): lax.ppermute(send, axis_name, [(j, j ^ bit) for j in range(size)])]
  transfers between devices with their start and end apart: 10 -> 7, of which waited for: 7 -> 6; matrix products, arithmetic and copies ran while one was open for 18% -> 13% of each run, Pallas kernels for 0% -> 0%
where the time goes in v7:
time: 533 us
  waiting for transfers between devices  374 us (70%)
  local copies, waits for them, and re-layouts  58.3 us (11%)
  matrix products  36.5 us (7%)
  other arithmetic  32.4 us (6%)
  starting transfers between devices  17.5 us (3%)
  between operations  14 us (3%)
    all_to_all x1, waiting for transfers between devices, body(): lax.all_to_all(kv_pool[pack_index], 'pool', split_axis=0, concat_axis=0,...  222 us
    all_gather x1, waiting for transfers between devices, body(): lax.all_gather(attention, 'pool', axis=0, tiled=True)  70.3 us
    all_to_all x1, waiting for transfers between devices, body(): lax.all_to_all(spread[hot_owner], 'pool', split_axis=0, concat_axis=0, ti...  38.4 us
    all_to_all x1, waiting for transfers between devices, body(): lax.all_to_all(kv_pool[extra_index].reshape(pool_size, piece_rows, kv_col...  25.7 us
    ppermute x2, waiting for transfers between devices, halving_sum(): lax.ppermute(send, axis_name, [(j, j ^ bit) for j in range(size)])  17 us
    select_n x2, other arithmetic, body(): jnp.where((numbers < my_resident[local_user])[:, None, None], resident_pa...  14.1 us
    gather x2, local copies, waits for them, and re-layouts, body(): regular_pages = arrived[owner * capacity + jnp.minimum(rank, capacity - 1)]  12.6 us
    dot_general x1, matrix products, body(): jnp.dot(draft_states, w_qkv, preferred_element_type=jnp.float32)  10.9 us
  transfers between devices with their start and end apart: 7, of which 6 were waited for; matrix products, arithmetic and copies ran while one was open for 13% of the time, Pallas kernels for 0%

profile of v7, /device:TPU:0, one launch (start us, length us, event | category | flops | bytes accessed | tf_op | source)
XLA Modules:
  0.0 532.6 jit_solution(16786594691708455211)
XLA Ops:
  13.4 5.6 %gather_fusion.3 = bf16[8,128,512]{2,1,0:T(8,128)(2,1)} fusion(bf16[80,128,512]{2,1,0:T(8,128)(2,1)} %param.13, s32[1024]{0:T(1024)S(1)} %pad_clamp_fusion.5), kind=kCustom, calls=%fused_computation.3 | custom fusion | bytes 2097184 | tf_op jit(solution)/shard_map/gather | solution.py:169
  19.0 7.3 %all-to-all-start.1 = ((bf16[8,128,512]{2,1,0:T(8,128)(2,1)}), bf16[8,128,512]{2,1,0:T(8,128)(2,1)S(1)}, u32[]{:S(2)}, u32[]{:S(2)}) async-start(bf16[8,128,512]{2,1,0:T(8,128)(2,1)} %gather_fusion.3), calls=%async_computation.2 | async-start | bytes 2097152 | tf_op jit(solution)/shard_map/all_to_all | solution.py:168
  26.3 10.9 %fusion.131 = f32[1024,2560]{1,0:T(8,128)} fusion(bf16[1024,1024]{1,0:T(8,128)(2,1)} %param.10, bf16[1024,2560]{1,0:T(8,128)(2,1)} %param.11), kind=kOutput, calls=%fused_computation.250 | convolution fusion | flops 5368709120 | bytes 17825792 | tf_op jit(solution)/shard_map/dot_general | solution.py:122
  38.1 25.7 %all-to-all-done.1 = bf16[8,128,512]{2,1,0:T(8,128)(2,1)S(1)} async-done(((bf16[8,128,512]{2,1,0:T(8,128)(2,1)}), bf16[8,128,512]{2,1,0:T(8,128)(2,1)S(1)}, u32[]{:S(2)}, u32[]{:S(2)}) %all-to-all-start.1) | async-done | bytes 1048608 | tf_op jit(solution)/shard_map/all_to_all | solution.py:168
  65.4 3.6 all-to-all-start.2
  71.4 9.8 %gather_fusion.1 = bf16[64,128,512]{2,1,0:T(8,128)(2,1)} fusion(bf16[80,128,512]{2,1,0:T(8,128)(2,1)} %param.13, s32[1024]{0:T(1024)S(1)} %pad_clamp_fusion.7), kind=kCustom, calls=%fused_computation.1 | custom fusion | bytes 16777472 | tf_op jit(solution)/shard_map/gather | solution.py:166
  81.2 38.4 %all-to-all-done.2 = bf16[8,128,512]{2,1,0:T(8,128)(2,1)S(1)} async-done(((bf16[8,128,512]{2,1,0:T(8,128)(2,1)}), bf16[8,128,512]{2,1,0:T(8,128)(2,1)S(1)}, u32[]{:S(2)}, u32[]{:S(2)}) %all-to-all-start.2) | async-done | bytes 1048608 | tf_op jit(solution)/shard_map/all_to_all | solution.py:175
  119.6 5.1 all-to-all-start
  126.9 2.8 gather_fusion
  129.7 2.9 gather_fusion.6
  137.5 2.8 gather_fusion.5
  140.3 2.8 gather_fusion.8
  143.1 222.5 %all-to-all-done = bf16[64,128,512]{2,1,0:T(8,128)(2,1)} async-done(((bf16[64,128,512]{2,1,0:T(8,128)(2,1)}), bf16[64,128,512]{2,1,0:T(8,128)(2,1)}, u32[]{:S(2)}, u32[]{:S(2)}) %all-to-all-start) | async-done | bytes 8388640 | tf_op jit(solution)/shard_map/all_to_all | solution.py:165
  365.5 6.3 %gather_fusion.2 = bf16[32,128,512]{2,1,0:T(8,128)(2,1)} fusion(bf16[64,128,512]{2,1,0:T(8,128)(2,1)} %all-to-all-done, s32[1024]{0:T(1024)S(1)} %pad_clamp_fusion.6), kind=kCustom, calls=%fused_computation.2 | custom fusion | bytes 8388736 | tf_op jit(solution)/shard_map/gather | solution.py:191
  371.8 6.3 %gather_fusion.7 = bf16[32,128,512]{2,1,0:T(8,128)(2,1)} fusion(bf16[64,128,512]{2,1,0:T(8,128)(2,1)} %all-to-all-done, s32[1024]{0:T(1024)S(1)} %pad_clamp_fusion.1), kind=kCustom, calls=%fused_computation.7 | custom fusion | bytes 8388736 | tf_op jit(solution)/shard_map/gather | solution.py:191
  378.1 9.7 %fusion.9 = bf16[4096,512]{1,0:T(8,128)(2,1)} fusion(bf16[32,128,512]{2,1,0:T(8,128)(2,1)} %gather_fusion.5, bf16[32,128,512]{2,1,0:T(8,128)(2,1)} %gather_fusion.2, bf16[32,128,512]{2,1,0:T(8,128)(2,1)} %gather_fusion, pred[4096]{0:T(1024)(128)(4,1)S(1)} %get-tuple-element.70, pred[4096]{0:T(1024)(128)(4,1)S(1)} %broadcast_bitcast_fusion.5), kind=kLoop, calls=%fused_computation.30 | loop fusion | flops 4194304 | bytes 16785408 | tf_op jit(solution)/shard_map/jit(_where)/select_n | solution.py:193
  387.8 4.4 fusion.8
  397.6 3.3 fusion
  408.8 3.3 fusion.4
  419.7 70.3 %all-gather.2.cloned.1.call-done = bf16[1024,2048]{1,0:T(8,128)(2,1)} async-done(((bf16[128,2048]{1,0:T(8,128)(2,1)}), bf16[1024,2048]{1,0:T(8,128)(2,1)}) %all-gather.2.cloned.1.call-update) | async-done | bytes 4194320 | tf_op jit(solution)/shard_map/all_gather | solution.py:209
  489.9 7.5 %fusion.132 = f32[1024,1024]{1,0:T(8,128)S(1)} fusion(bf16[1024,2048]{1,0:T(8,128)(2,1)} %all-gather.2.cloned.1.call-done, bf16[2048,1024]{1,0:T(8,128)(2,1)} %param.12), kind=kOutput, calls=%fused_computation.251 | convolution fusion | flops 4294967296 | bytes 12582912 | tf_op jit(solution)/shard_map/dot_general | solution.py:208
  501.0 4.5 collective-permute-done
  505.5 2.6 bitcast_add_fusion
  511.1 12.5 %collective-permute-done.1 = bf16[1,256,1024]{2,1,0:T(8,128)(2,1)S(1)} collective-permute-done((bf16[1,256,1024]{2,1,0:T(8,128)(2,1)S(1)}, bf16[1,256,1024]{2,1,0:T(8,128)(2,1)S(1)}, u32[]{:S(2)}, u32[]{:S(2)}) %collective-permute-start.1) | collective-permute-done | bytes 524320 | tf_op jit(solution)/shard_map/ppermute | solution.py:231
  (135 shorter events, 48.1 us)
Async XLA Ops:
  6.5 120.4 %copy-start = (bf16[2,8,128,512]{3,2,1,0:T(8,128)(2,1)S(1)}, bf16[2,8,128,512]{3,2,1,0:T(8,128)(2,1)}, u32[]{:S(2)}) copy-start(bf16[2,8,128,512]{3,2,1,0:T(8,128)(2,1)} %param.14) | copy-start | bytes 6291460
  19.0 44.8 %all-to-all-start.1 = ((bf16[8,128,512]{2,1,0:T(8,128)(2,1)}), bf16[8,128,512]{2,1,0:T(8,128)(2,1)S(1)}, u32[]{:S(2)}, u32[]{:S(2)}) async-start(bf16[8,128,512]{2,1,0:T(8,128)(2,1)} %gather_fusion.3), calls=%async_computation.2 | async-start | bytes 2097152 | tf_op jit(solution)/shard_map/all_to_all | solution.py:168
  26.3 365.9 %reduce-scatter.2.cloned.1.call-start = ((), (), s32[]{:S(2)}) async-start(), calls=%async_computation.4 | async-start | bytes 11796480 | tf_op jit(solution)/shard_map/reduce_scatter | solution.py:121
  65.4 54.1 %all-to-all-start.2 = ((bf16[8,128,512]{2,1,0:T(8,128)(2,1)}), bf16[8,128,512]{2,1,0:T(8,128)(2,1)S(1)}, u32[]{:S(2)}, u32[]{:S(2)}) async-start(bf16[8,128,512]{2,1,0:T(8,128)(2,1)} %gather_fusion.4), calls=%async_computation.3 | async-start | bytes 2097152 | tf_op jit(solution)/shard_map/all_to_all | solution.py:175
  81.2 45.5 %copy-start.10 = (s32[16]{0:T(128)S(1)}, s32[16]{0:T(128)}, u32[]{:S(2)}) copy-start(s32[16]{0:T(128)} %param.18) | copy-start | bytes 196
  119.6 246.0 %all-to-all-start = ((bf16[64,128,512]{2,1,0:T(8,128)(2,1)}), bf16[64,128,512]{2,1,0:T(8,128)(2,1)}, u32[]{:S(2)}, u32[]{:S(2)}) async-start(bf16[64,128,512]{2,1,0:T(8,128)(2,1)} %gather_fusion.1), calls=%async_computation.1 | async-start | bytes 16777216 | tf_op jit(solution)/shard_map/all_to_all | solution.py:165
  124.6 365.3 %all-gather.2.cloned.1.call-start = ((), (), s32[]{:S(2)}) async-start(), calls=%async_computation.5 | async-start | bytes 4718592 | tf_op jit(solution)/shard_map/all_gather | solution.py:209
  129.7 5.2 copy-start.9
  378.1 9.7 %copy-start.2 = (bf16[32,128,512]{2,1,0:T(8,128)(2,1)S(1)}, bf16[32,128,512]{2,1,0:T(8,128)(2,1)}, u32[]{:S(2)}) copy-start(bf16[32,128,512]{2,1,0:T(8,128)(2,1)} %gather_fusion.6) | copy-start | bytes 12582916
  378.1 9.7 %copy-start.3 = (bf16[32,128,512]{2,1,0:T(8,128)(2,1)S(1)}, bf16[32,128,512]{2,1,0:T(8,128)(2,1)}, u32[]{:S(2)}) copy-start(bf16[32,128,512]{2,1,0:T(8,128)(2,1)} %gather_fusion.8) | copy-start | bytes 12582916
  378.1 9.7 %copy-start.4 = (bf16[32,128,512]{2,1,0:T(8,128)(2,1)S(1)}, bf16[32,128,512]{2,1,0:T(8,128)(2,1)}, u32[]{:S(2)}) copy-start(bf16[32,128,512]{2,1,0:T(8,128)(2,1)} %gather_fusion.7) | copy-start | bytes 12582916
  393.7 2.2 copy-start.6
  404.9 2.2 copy-start.5
  497.5 1.9 copy-start.8
  499.4 26.3 %copy-start.1 = (bf16[2,8,128,512]{3,2,1,0:T(8,128)(2,1)S(1)}, bf16[2,8,128,512]{3,2,1,0:T(8,128)(2,1)}, u32[]{:S(2)}) copy-start(bf16[2,8,128,512]{3,2,1,0:T(8,128)(2,1)} %param.14) | copy-start | bytes 6291460
  501.0 4.5 collective-permute-start
  508.1 1.4 copy-start.7
  509.5 14.0 %collective-permute-start.1 = (bf16[1,256,1024]{2,1,0:T(8,128)(2,1)S(1)}, bf16[1,256,1024]{2,1,0:T(8,128)(2,1)S(1)}, u32[]{:S(2)}, u32[]{:S(2)}) collective-permute-start(bf16[1,256,1024]{2,1,0:T(8,128)(2,1)S(1)} %dynamic-slice_convert_fusion), channel_id=1, source_target_pairs={{0,2},{1,3},{2,0},{3,1},{4,6},{5,7},{6,4},{7,5},{8,10},{9,11},{10,... | collective-permute-start | bytes 1572872 | tf_op jit(solution)/shard_map/ppermute | solution.py:231
Sparse Core Ops, SparseCore 0:
  37.4 346.5 reduce-scatter.1
  419.8 70.1 all-gather.1

commit v8 on v7

--- a/solution.py
+++ b/solution.py
@@ -55,18 +55,17 @@
     heads_kv, row_count, head_dim = queries.shape
     score_scale = head_dim ** (-0.5)
     hist_ok = (jnp.arange(history.shape[0]) < length)[None, :]
-    results = []
-    for head in range(heads_kv):
-        keys = history[:, 2 * head * head_dim : (2 * head + 1) * head_dim]
-        values = history[:, (2 * head + 1) * head_dim : (2 * head + 2) * head_dim]
+
+    def attend_head(operands):
+        head, head_queries, head_key, head_value = operands
+        keys = lax.dynamic_slice_in_dim(history, 2 * head * head_dim, head_dim, axis=1)
+        values = lax.dynamic_slice_in_dim(history, (2 * head + 1) * head_dim, head_dim, axis=1)
         hist_scores = (
-            jnp.einsum("rd,sd->rs", queries[head], keys, preferred_element_type=jnp.float32)
+            jnp.einsum("rd,sd->rs", head_queries, keys, preferred_element_type=jnp.float32)
             * score_scale
         )
         draft_scores = (
-            jnp.einsum(
-                "rd,jd->rj", queries[head], draft_key[:, head], preferred_element_type=jnp.float32
-            )
+            jnp.einsum("rd,jd->rj", head_queries, head_key, preferred_element_type=jnp.float32)
             * score_scale
         )
         row_max = jnp.maximum(
@@ -84,11 +83,20 @@
         ) + jnp.einsum(
             "rj,jd->rd",
             draft_weight.astype(jnp.bfloat16),
-            draft_value[:, head],
+            head_value,
             preferred_element_type=jnp.float32,
         )
-        results.append(weighted / denominator[:, None])
-    return jnp.stack(results, 0)
+        return weighted / denominator[:, None]
+
+    return lax.map(
+        attend_head,
+        (
+            jnp.arange(heads_kv),
+            queries,
+            draft_key.transpose(1, 0, 2),
+            draft_value.transpose(1, 0, 2),
+        ),
+    )
 
 
 def finish(result, draft_len):

time: 533 us -> 566 us (1.062)
  matrix products: 36.5 us -> 52.2 us
    dot_general x16, matrix products: 17 us -> 32.7 us  [the longest x4 20.2 us: attend_head(): jnp.einsum('rs,sd->rd', hist_weight.astype(jnp.bfloat16), values, preferr...]
  transfers between devices with their start and end apart: 7 -> 7, of which waited for: 6 -> 6; matrix products, arithmetic and copies ran while one was open for 13% -> 12% of each run, Pallas kernels for 0% -> 0%
where the time goes in v8:
time: 566 us; the launch traced here: 565 us
  waiting for transfers between devices  375 us (66%)
  local copies, waits for them, and re-layouts  62.8 us (11%)
  matrix products  52.2 us (9%)
  other arithmetic  37.8 us (7%)
  starting transfers between devices  17.7 us (3%)
  between operations  13.9 us (2%)
    all_to_all x1, waiting for transfers between devices, body(): lax.all_to_all(kv_pool[pack_index], 'pool', split_axis=0, concat_axis=0,...  224 us
    all_gather x1, waiting for transfers between devices, body(): lax.all_gather(attention, 'pool', axis=0, tiled=True)  70.3 us
    all_to_all x1, waiting for transfers between devices, body(): lax.all_to_all(spread[hot_owner], 'pool', split_axis=0, concat_axis=0, ti...  38.4 us
    all_to_all x1, waiting for transfers between devices, body(): lax.all_to_all(kv_pool[extra_index].reshape(pool_size, piece_rows, kv_col...  25.7 us
    dot_general x4, matrix products, attend_head(): jnp.einsum('rs,sd->rd', hist_weight.astype(jnp.bfloat16), values, preferr...  20.2 us
    ppermute x2, waiting for transfers between devices, halving_sum(): lax.ppermute(send, axis_name, [(j, j ^ bit) for j in range(size)])  17 us
    select_n x2, other arithmetic, body(): jnp.where((numbers < my_resident[local_user])[:, None, None], resident_pa...  13.9 us
    gather x2, local copies, waits for them, and re-layouts, body(): regular_pages = arrived[owner * capacity + jnp.minimum(rank, capacity - 1)]  12.6 us
  transfers between devices with their start and end apart: 7, of which 6 were waited for; matrix products, arithmetic and copies ran while one was open for 12% of the time, Pallas kernels for 0%

profile of v8, /device:TPU:0, one launch (start us, length us, event | category | flops | bytes accessed | tf_op | source)
XLA Modules:
  0.0 564.6 jit_solution(7674546704152248791)
XLA Ops:
  13.4 5.6 gather_fusion.3
  19.0 7.3 %all-to-all-start.1 = ((bf16[8,128,512]{2,1,0:T(8,128)(2,1)}), bf16[8,128,512]{2,1,0:T(8,128)(2,1)S(1)}, u32[]{:S(2)}, u32[]{:S(2)}) async-start(bf16[8,128,512]{2,1,0:T(8,128)(2,1)} %gather_fusion.3), calls=%async_computation.2 | async-start | bytes 2097152 | tf_op jit(solution)/shard_map/all_to_all | solution.py:176
  26.3 10.9 %fusion.116 = f32[1024,2560]{1,0:T(8,128)} fusion(bf16[1024,1024]{1,0:T(8,128)(2,1)} %param.14, bf16[1024,2560]{1,0:T(8,128)(2,1)} %param.15), kind=kOutput, calls=%fused_computation.217 | convolution fusion | flops 5368709120 | bytes 17825792 | tf_op jit(solution)/shard_map/dot_general | solution.py:130
  38.1 25.7 %all-to-all-done.1 = bf16[8,128,512]{2,1,0:T(8,128)(2,1)S(1)} async-done(((bf16[8,128,512]{2,1,0:T(8,128)(2,1)}), bf16[8,128,512]{2,1,0:T(8,128)(2,1)S(1)}, u32[]{:S(2)}, u32[]{:S(2)}) %all-to-all-start.1) | async-done | bytes 1048608 | tf_op jit(solution)/shard_map/all_to_all | solution.py:176
  65.4 3.6 all-to-all-start.2
  71.4 9.8 %gather_fusion.1 = bf16[64,128,512]{2,1,0:T(8,128)(2,1)} fusion(bf16[80,128,512]{2,1,0:T(8,128)(2,1)} %param.17, s32[1024]{0:T(1024)S(1)} %pad_clamp_fusion.7), kind=kCustom, calls=%fused_computation.1 | custom fusion | bytes 16777472 | tf_op jit(solution)/shard_map/gather | solution.py:174
  81.2 38.4 %all-to-all-done.2 = bf16[8,128,512]{2,1,0:T(8,128)(2,1)S(1)} async-done(((bf16[8,128,512]{2,1,0:T(8,128)(2,1)}), bf16[8,128,512]{2,1,0:T(8,128)(2,1)S(1)}, u32[]{:S(2)}, u32[]{:S(2)}) %all-to-all-start.2) | async-done | bytes 1048608 | tf_op jit(solution)/shard_map/all_to_all | solution.py:183
  119.6 5.1 all-to-all-start
  127.7 2.9 gather_fusion.6
  141.8 223.8 %all-to-all-done = bf16[64,128,512]{2,1,0:T(8,128)(2,1)} async-done(((bf16[64,128,512]{2,1,0:T(8,128)(2,1)}), bf16[64,128,512]{2,1,0:T(8,128)(2,1)}, u32[]{:S(2)}, u32[]{:S(2)}) %all-to-all-start) | async-done | bytes 8388640 | tf_op jit(solution)/shard_map/all_to_all | solution.py:173
  365.5 6.3 %gather_fusion.2 = bf16[32,128,512]{2,1,0:T(8,128)(2,1)} fusion(bf16[64,128,512]{2,1,0:T(8,128)(2,1)} %all-to-all-done, s32[1024]{0:T(1024)S(1)} %pad_clamp_fusion.6), kind=kCustom, calls=%fused_computation.2 | custom fusion | bytes 8388736 | tf_op jit(solution)/shard_map/gather | solution.py:199
  371.8 6.3 %gather_fusion.7 = bf16[32,128,512]{2,1,0:T(8,128)(2,1)} fusion(bf16[64,128,512]{2,1,0:T(8,128)(2,1)} %all-to-all-done, s32[1024]{0:T(1024)S(1)} %pad_clamp_fusion.1), kind=kCustom, calls=%fused_computation.7 | custom fusion | bytes 8388736 | tf_op jit(solution)/shard_map/gather | solution.py:199
  378.1 9.6 %fusion.71 = bf16[4096,512]{1,0:T(8,128)(2,1)} fusion(bf16[32,128,512]{2,1,0:T(8,128)(2,1)} %gather_fusion.5, bf16[32,128,512]{2,1,0:T(8,128)(2,1)} %gather_fusion.2, bf16[32,128,512]{2,1,0:T(8,128)(2,1)} %gather_fusion, pred[4096]{0:T(1024)(128)(4,1)S(1)} %get-tuple-element.474, pred[4096]{0:T(1024)(128)(4,1)S(1)} %broadcast_bitcast_fusion.5), kind=kLoop, calls=%fused_computation.92 | loop fusion | flops 4194304 | bytes 16785408 | tf_op jit(solution)/shard_map/jit(_where)/select_n | solution.py:201
  387.9 4.3 fusion.70
  395.7 27.1 %while.26 = (s32[]{:T(128)}, bf16[2,512,128]{2,1,0:T(8,128)(2,1)S(1)}, bf16[2,512,128]{2,1,0:T(8,128)(2,1)S(1)}, s32[2]{0:T(128)S(1)}, bf16[4096,512]{1,0:T(8,12...) while((s32[]{:T(128)}, ...), condition=%wide.region_13.14_spmd.clone, body=%wide.region_8.13_spmd.clone.sunk | while | flops 1114016768 | bytes 62542648 | solution.py:91
  404.0 5.1 fusion.146
  417.6 5.1 fusion.146
  423.1 27.6 %while.27 = (s32[]{:T(128)}, bf16[2,512,128]{2,1,0:T(8,128)(2,1)S(1)}, bf16[2,512,128]{2,1,0:T(8,128)(2,1)S(1)}, s32[2]{0:T(128)S(1)}, bf16[4096,512]{1,0:T(8,12...) while((s32[]{:T(128)}, ...), condition=%wide.region_19.20_spmd.clone, body=%wide.region_14.19_spmd.clone.sunk | while | flops 1114016768 | bytes 62542648 | solution.py:91
  431.7 5.1 fusion.154
  445.4 5.1 fusion.154
  451.7 70.3 %all-gather.2.cloned.1.call-done = bf16[1024,2048]{1,0:T(8,128)(2,1)} async-done(((bf16[128,2048]{1,0:T(8,128)(2,1)}), bf16[1024,2048]{1,0:T(8,128)(2,1)}) %all-gather.2.cloned.1.call-update) | async-done | bytes 4194320 | tf_op jit(solution)/shard_map/all_gather | solution.py:217
  522.0 7.5 %fusion.117 = f32[1024,1024]{1,0:T(8,128)S(1)} fusion(bf16[1024,2048]{1,0:T(8,128)(2,1)} %all-gather.2.cloned.1.call-done, bf16[2048,1024]{1,0:T(8,128)(2,1)} %param.16), kind=kOutput, calls=%fused_computation.218 | convolution fusion | flops 4294967296 | bytes 12582912 | tf_op jit(solution)/shard_map/dot_general | solution.py:216
  533.0 4.5 collective-permute-done
  543.1 12.5 %collective-permute-done.1 = bf16[1,256,1024]{2,1,0:T(8,128)(2,1)S(1)} collective-permute-done((bf16[1,256,1024]{2,1,0:T(8,128)(2,1)S(1)}, bf16[1,256,1024]{2,1,0:T(8,128)(2,1)S(1)}, u32[]{:S(2)}, u32[]{:S(2)}) %collective-permute-start.1) | collective-permute-done | bytes 524320 | tf_op jit(solution)/shard_map/ppermute | solution.py:239
  (163 shorter events, 71.3 us)
Async XLA Ops:
  6.5 118.4 %copy-start = (bf16[2,8,128,512]{3,2,1,0:T(8,128)(2,1)S(1)}, bf16[2,8,128,512]{3,2,1,0:T(8,128)(2,1)}, u32[]{:S(2)}) copy-start(bf16[2,8,128,512]{3,2,1,0:T(8,128)(2,1)} %param.18) | copy-start | bytes 6291460
  19.0 44.8 %all-to-all-start.1 = ((bf16[8,128,512]{2,1,0:T(8,128)(2,1)}), bf16[8,128,512]{2,1,0:T(8,128)(2,1)S(1)}, u32[]{:S(2)}, u32[]{:S(2)}) async-start(bf16[8,128,512]{2,1,0:T(8,128)(2,1)} %gather_fusion.3), calls=%async_computation.2 | async-start | bytes 2097152 | tf_op jit(solution)/shard_map/all_to_all | solution.py:176
  26.3 365.9 %reduce-scatter.2.cloned.1.call-start = ((), (), s32[]{:S(2)}) async-start(), calls=%async_computation.4 | async-start | bytes 11796480 | tf_op jit(solution)/shard_map/reduce_scatter | solution.py:129
  65.4 54.1 %all-to-all-start.2 = ((bf16[8,128,512]{2,1,0:T(8,128)(2,1)}), bf16[8,128,512]{2,1,0:T(8,128)(2,1)S(1)}, u32[]{:S(2)}, u32[]{:S(2)}) async-start(bf16[8,128,512]{2,1,0:T(8,128)(2,1)} %gather_fusion.4), calls=%async_computation.3 | async-start | bytes 2097152 | tf_op jit(solution)/shard_map/all_to_all | solution.py:183
  119.6 246.0 %all-to-all-start = ((bf16[64,128,512]{2,1,0:T(8,128)(2,1)}), bf16[64,128,512]{2,1,0:T(8,128)(2,1)}, u32[]{:S(2)}, u32[]{:S(2)}) async-start(bf16[64,128,512]{2,1,0:T(8,128)(2,1)} %gather_fusion.1), calls=%async_computation.1 | async-start | bytes 16777216 | tf_op jit(solution)/shard_map/all_to_all | solution.py:173
  124.6 397.4 %all-gather.2.cloned.1.call-start = ((), (), s32[]{:S(2)}) async-start(), calls=%async_computation.5 | async-start | bytes 4718592 | tf_op jit(solution)/shard_map/all_gather | solution.py:217
  127.7 2.9 copy-start.10
  127.7 6.0 %copy-start.9 = (s32[16]{0:T(128)S(1)}, s32[16]{0:T(128)}, u32[]{:S(2)}) copy-start(s32[16]{0:T(128)} %param.21) | copy-start | bytes 196
  378.1 9.6 %copy-start.4 = (bf16[32,128,512]{2,1,0:T(8,128)(2,1)S(1)}, bf16[32,128,512]{2,1,0:T(8,128)(2,1)}, u32[]{:S(2)}) copy-start(bf16[32,128,512]{2,1,0:T(8,128)(2,1)} %gather_fusion.6) | copy-start | bytes 12582916
  378.1 9.6 %copy-start.5 = (bf16[32,128,512]{2,1,0:T(8,128)(2,1)S(1)}, bf16[32,128,512]{2,1,0:T(8,128)(2,1)}, u32[]{:S(2)}) copy-start(bf16[32,128,512]{2,1,0:T(8,128)(2,1)} %gather_fusion.8) | copy-start | bytes 12582916
  378.1 9.7 %copy-start.6 = (bf16[32,128,512]{2,1,0:T(8,128)(2,1)S(1)}, bf16[32,128,512]{2,1,0:T(8,128)(2,1)}, u32[]{:S(2)}) copy-start(bf16[32,128,512]{2,1,0:T(8,128)(2,1)} %gather_fusion.7) | copy-start | bytes 12582916
  400.2 3.2 copy-start.2
  413.8 3.2 copy-start.2
  427.9 3.2 copy-start.3
  441.6 3.2 copy-start.3
  529.5 1.9 copy-start.8
  533.0 4.5 collective-permute-start
  533.0 24.7 %copy-start.1 = (bf16[2,8,128,512]{3,2,1,0:T(8,128)(2,1)S(1)}, bf16[2,8,128,512]{3,2,1,0:T(8,128)(2,1)}, u32[]{:S(2)}) copy-start(bf16[2,8,128,512]{3,2,1,0:T(8,128)(2,1)} %param.18) | copy-start | bytes 6291460
  540.1 1.4 copy-start.7
  541.6 14.0 %collective-permute-start.1 = (bf16[1,256,1024]{2,1,0:T(8,128)(2,1)S(1)}, bf16[1,256,1024]{2,1,0:T(8,128)(2,1)S(1)}, u32[]{:S(2)}, u32[]{:S(2)}) collective-permute-start(bf16[1,256,1024]{2,1,0:T(8,128)(2,1)S(1)} %dynamic-slice_convert_fusion), channel_id=1, source_target_pairs={{0,2},{1,3},{2,0},{3,1},{4,6},{5,7},{6,4},{7,5},{8,10},{9,11},{10,... | collective-permute-start | bytes 1572872 | tf_op jit(solution)/shard_map/ppermute | solution.py:239
Sparse Core Ops, SparseCore 0:
  37.4 346.5 reduce-scatter.1
  451.9 70.1 all-gather.1

commit v9 on v7

--- a/solution.py
+++ b/solution.py
@@ -205,12 +205,20 @@
         )
         outputs.append(finish(result, DRAFT))
     attention = jnp.concatenate(outputs, 0)
-    partial_out = jnp.dot(
-        lax.all_gather(attention, "pool", axis=0, tiled=True),
-        w_out,
-        preferred_element_type=jnp.float32,
-    )
-    return halving_sum(partial_out, "tp").astype(jnp.bfloat16)
+    gathered = lax.all_gather(attention, "pool", axis=0, tiled=True)
+    half_cols = w_out.shape[1] // 2
+    halves = [
+        halving_sum(
+            jnp.dot(
+                gathered,
+                w_out[:, part * half_cols : (part + 1) * half_cols],
+                preferred_element_type=jnp.float32,
+            ),
+            "tp",
+        )
+        for part in range(2)
+    ]
+    return jnp.concatenate(halves, 1).astype(jnp.bfloat16)
 
 
 def halving_sum(partial, axis_name):

time: 533 us -> 535 us (level); the launches traced: 533 us -> 527 us
  waiting for transfers between devices: 374 us -> 365 us
    ppermute x2 -> x4, waiting for transfers between devices: 17 us -> 8.21 us  [halving_sum(): lax.ppermute(send, axis_name, [(j, j ^ bit) for j in range(size)])]
  transfers between devices with their start and end apart: 7 -> 9, of which waited for: 6 -> 6; matrix products, arithmetic and copies ran while one was open for 13% -> 15% of each run, Pallas kernels for 0% -> 0%
where the time goes in v9:
time: 535 us; the launch traced here: 527 us
  waiting for transfers between devices  365 us (68%)
  local copies, waits for them, and re-layouts  57.6 us (11%)
  matrix products  36.6 us (7%)
  other arithmetic  34.3 us (6%)
  starting transfers between devices  18.6 us (3%)
  between operations  14.5 us (3%)
    all_to_all x1, waiting for transfers between devices, body(): lax.all_to_all(kv_pool[pack_index], 'pool', split_axis=0, concat_axis=0,...  222 us
    all_gather x1, waiting for transfers between devices, body(): gathered = lax.all_gather(attention, 'pool', axis=0, tiled=True)  70.3 us
    all_to_all x1, waiting for transfers between devices, body(): lax.all_to_all(spread[hot_owner], 'pool', split_axis=0, concat_axis=0, ti...  38.4 us
    all_to_all x1, waiting for transfers between devices, body(): lax.all_to_all(kv_pool[extra_index].reshape(pool_size, piece_rows, kv_col...  25.7 us
    select_n x2, other arithmetic, body(): jnp.where((numbers < my_resident[local_user])[:, None, None], resident_pa...  14.1 us
    gather x2, local copies, waits for them, and re-layouts, body(): regular_pages = arrived[owner * capacity + jnp.minimum(rank, capacity - 1)]  12.6 us
    dot_general x1, matrix products, body(): jnp.dot(draft_states, w_qkv, preferred_element_type=jnp.float32)  10.9 us
  transfers between devices with their start and end apart: 9, of which 6 were waited for; matrix products, arithmetic and copies ran while one was open for 15% of the time, Pallas kernels for 0%

profile of v9, /device:TPU:0, one launch (start us, length us, event | category | flops | bytes accessed | tf_op | source)
XLA Modules:
  0.0 526.7 jit_solution(4654088642165571962)
XLA Ops:
  11.0 2.4 scatter_custom_fusion.1
  13.4 5.6 %gather_fusion.3 = bf16[8,128,512]{2,1,0:T(8,128)(2,1)} fusion(bf16[80,128,512]{2,1,0:T(8,128)(2,1)} %param.13, s32[1024]{0:T(1024)S(1)} %pad_clamp_fusion.5), kind=kCustom, calls=%fused_computation.3 | custom fusion | bytes 2097184 | tf_op jit(solution)/shard_map/gather | solution.py:169
  19.0 7.3 %all-to-all-start.1 = ((bf16[8,128,512]{2,1,0:T(8,128)(2,1)}), bf16[8,128,512]{2,1,0:T(8,128)(2,1)S(1)}, u32[]{:S(2)}, u32[]{:S(2)}) async-start(bf16[8,128,512]{2,1,0:T(8,128)(2,1)} %gather_fusion.3), calls=%async_computation.2 | async-start | bytes 2097152 | tf_op jit(solution)/shard_map/all_to_all | solution.py:168
  26.3 10.9 %fusion.136 = f32[1024,2560]{1,0:T(8,128)} fusion(bf16[1024,1024]{1,0:T(8,128)(2,1)} %param.10, bf16[1024,2560]{1,0:T(8,128)(2,1)} %param.11), kind=kOutput, calls=%fused_computation.260 | convolution fusion | flops 5368709120 | bytes 17825792 | tf_op jit(solution)/shard_map/dot_general | solution.py:122
  38.1 25.7 %all-to-all-done.1 = bf16[8,128,512]{2,1,0:T(8,128)(2,1)S(1)} async-done(((bf16[8,128,512]{2,1,0:T(8,128)(2,1)}), bf16[8,128,512]{2,1,0:T(8,128)(2,1)S(1)}, u32[]{:S(2)}, u32[]{:S(2)}) %all-to-all-start.1) | async-done | bytes 1048608 | tf_op jit(solution)/shard_map/all_to_all | solution.py:168
  65.4 3.6 all-to-all-start.2
  71.4 9.8 %gather_fusion.1 = bf16[64,128,512]{2,1,0:T(8,128)(2,1)} fusion(bf16[80,128,512]{2,1,0:T(8,128)(2,1)} %param.13, s32[1024]{0:T(1024)S(1)} %pad_clamp_fusion.7), kind=kCustom, calls=%fused_computation.1 | custom fusion | bytes 16777472 | tf_op jit(solution)/shard_map/gather | solution.py:166
  81.2 38.4 %all-to-all-done.2 = bf16[8,128,512]{2,1,0:T(8,128)(2,1)S(1)} async-done(((bf16[8,128,512]{2,1,0:T(8,128)(2,1)}), bf16[8,128,512]{2,1,0:T(8,128)(2,1)S(1)}, u32[]{:S(2)}, u32[]{:S(2)}) %all-to-all-start.2) | async-done | bytes 1048608 | tf_op jit(solution)/shard_map/all_to_all | solution.py:175
  119.6 5.1 all-to-all-start
  126.9 2.8 gather_fusion
  129.7 2.9 gather_fusion.6
  137.5 2.8 gather_fusion.5
  140.3 2.8 gather_fusion.8
  143.1 222.4 %all-to-all-done = bf16[64,128,512]{2,1,0:T(8,128)(2,1)} async-done(((bf16[64,128,512]{2,1,0:T(8,128)(2,1)}), bf16[64,128,512]{2,1,0:T(8,128)(2,1)}, u32[]{:S(2)}, u32[]{:S(2)}) %all-to-all-start) | async-done | bytes 8388640 | tf_op jit(solution)/shard_map/all_to_all | solution.py:165
  365.5 6.3 %gather_fusion.2 = bf16[32,128,512]{2,1,0:T(8,128)(2,1)} fusion(bf16[64,128,512]{2,1,0:T(8,128)(2,1)} %all-to-all-done, s32[1024]{0:T(1024)S(1)} %pad_clamp_fusion.6), kind=kCustom, calls=%fused_computation.2 | custom fusion | bytes 8388736 | tf_op jit(solution)/shard_map/gather | solution.py:191
  371.8 6.3 %gather_fusion.7 = bf16[32,128,512]{2,1,0:T(8,128)(2,1)} fusion(bf16[64,128,512]{2,1,0:T(8,128)(2,1)} %all-to-all-done, s32[1024]{0:T(1024)S(1)} %pad_clamp_fusion.1), kind=kCustom, calls=%fused_computation.7 | custom fusion | bytes 8388736 | tf_op jit(solution)/shard_map/gather | solution.py:191
  378.1 9.6 %fusion.9 = bf16[4096,512]{1,0:T(8,128)(2,1)} fusion(bf16[32,128,512]{2,1,0:T(8,128)(2,1)} %gather_fusion.5, bf16[32,128,512]{2,1,0:T(8,128)(2,1)} %gather_fusion.2, bf16[32,128,512]{2,1,0:T(8,128)(2,1)} %gather_fusion, pred[4096]{0:T(1024)(128)(4,1)S(1)} %get-tuple-element.70, pred[4096]{0:T(1024)(128)(4,1)S(1)} %broadcast_bitcast_fusion.5), kind=kLoop, calls=%fused_computation.30 | loop fusion | flops 4194304 | bytes 16785408 | tf_op jit(solution)/shard_map/jit(_where)/select_n | solution.py:193
  387.8 4.4 fusion.8
  397.6 3.3 fusion
  408.8 3.3 fusion.4
  419.9 70.3 %all-gather.2.cloned.1.call-done = bf16[1024,2048]{1,0:T(8,128)(2,1)} async-done(((bf16[128,2048]{1,0:T(8,128)(2,1)}), bf16[1024,2048]{1,0:T(8,128)(2,1)}) %all-gather.2.cloned.1.call-update) | async-done | bytes 4194320 | tf_op jit(solution)/shard_map/all_gather | solution.py:208
  490.2 5.3 %fusion.24 = f32[1024,512]{1,0:T(8,128)S(1)} fusion(bf16[1024,2048]{1,0:T(8,128)(2,1)} %all-gather.2.cloned.1.call-done, bf16[2048,1024]{1,0:T(8,128)(2,1)} %param.12), kind=kOutput, calls=%fused_computation.41 | convolution fusion | flops 2147483648 | bytes 8388608 | tf_op jit(solution)/shard_map/dot_general | solution.py:212
  508.1 4.1 collective-permute-done.1
  513.2 4.1 collective-permute-done.3
  (153 shorter events, 52.8 us)
Async XLA Ops:
  6.5 120.4 %copy-start = (bf16[2,8,128,512]{3,2,1,0:T(8,128)(2,1)S(1)}, bf16[2,8,128,512]{3,2,1,0:T(8,128)(2,1)}, u32[]{:S(2)}) copy-start(bf16[2,8,128,512]{3,2,1,0:T(8,128)(2,1)} %param.14) | copy-start | bytes 6291460
  19.0 44.8 %all-to-all-start.1 = ((bf16[8,128,512]{2,1,0:T(8,128)(2,1)}), bf16[8,128,512]{2,1,0:T(8,128)(2,1)S(1)}, u32[]{:S(2)}, u32[]{:S(2)}) async-start(bf16[8,128,512]{2,1,0:T(8,128)(2,1)} %gather_fusion.3), calls=%async_computation.2 | async-start | bytes 2097152 | tf_op jit(solution)/shard_map/all_to_all | solution.py:168
  26.3 365.9 %reduce-scatter.2.cloned.1.call-start = ((), (), s32[]{:S(2)}) async-start(), calls=%async_computation.4 | async-start | bytes 11796480 | tf_op jit(solution)/shard_map/reduce_scatter | solution.py:121
  65.4 54.1 %all-to-all-start.2 = ((bf16[8,128,512]{2,1,0:T(8,128)(2,1)}), bf16[8,128,512]{2,1,0:T(8,128)(2,1)S(1)}, u32[]{:S(2)}, u32[]{:S(2)}) async-start(bf16[8,128,512]{2,1,0:T(8,128)(2,1)} %gather_fusion.4), calls=%async_computation.3 | async-start | bytes 2097152 | tf_op jit(solution)/shard_map/all_to_all | solution.py:175
  81.2 45.5 %copy-start.14 = (s32[16]{0:T(128)S(1)}, s32[16]{0:T(128)}, u32[]{:S(2)}) copy-start(s32[16]{0:T(128)} %param.18) | copy-start | bytes 196
  119.6 246.0 %all-to-all-start = ((bf16[64,128,512]{2,1,0:T(8,128)(2,1)}), bf16[64,128,512]{2,1,0:T(8,128)(2,1)}, u32[]{:S(2)}, u32[]{:S(2)}) async-start(bf16[64,128,512]{2,1,0:T(8,128)(2,1)} %gather_fusion.1), calls=%async_computation.1 | async-start | bytes 16777216 | tf_op jit(solution)/shard_map/all_to_all | solution.py:165
  124.6 365.5 %all-gather.2.cloned.1.call-start = ((), (), s32[]{:S(2)}) async-start(), calls=%async_computation.5 | async-start | bytes 4718592 | tf_op jit(solution)/shard_map/all_gather | solution.py:208
  129.7 5.2 copy-start.11
  378.1 9.7 %copy-start.2 = (bf16[32,128,512]{2,1,0:T(8,128)(2,1)S(1)}, bf16[32,128,512]{2,1,0:T(8,128)(2,1)}, u32[]{:S(2)}) copy-start(bf16[32,128,512]{2,1,0:T(8,128)(2,1)} %gather_fusion.6) | copy-start | bytes 12582916
  378.1 9.7 %copy-start.3 = (bf16[32,128,512]{2,1,0:T(8,128)(2,1)S(1)}, bf16[32,128,512]{2,1,0:T(8,128)(2,1)}, u32[]{:S(2)}) copy-start(bf16[32,128,512]{2,1,0:T(8,128)(2,1)} %gather_fusion.8) | copy-start | bytes 12582916
  378.1 9.7 %copy-start.4 = (bf16[32,128,512]{2,1,0:T(8,128)(2,1)S(1)}, bf16[32,128,512]{2,1,0:T(8,128)(2,1)}, u32[]{:S(2)}) copy-start(bf16[32,128,512]{2,1,0:T(8,128)(2,1)} %gather_fusion.7) | copy-start | bytes 12582916
  393.7 2.2 copy-start.6
  404.9 2.2 copy-start.5
  490.2 6.7 %copy-start.12 = (bf16[2048,1024]{1,0:T(8,128)(2,1)S(1)}, bf16[2048,1024]{1,0:T(8,128)(2,1)}, u32[]{:S(2)}) copy-start(bf16[2048,1024]{1,0:T(8,128)(2,1)} %param.12) | copy-start | bytes 12582916
  490.2 6.7 %copy-start.13 = (bf16[1024,2048]{1,0:T(8,128)(2,1)S(1)}, bf16[1024,2048]{1,0:T(8,128)(2,1)}, u32[]{:S(2)}) copy-start(bf16[1024,2048]{1,0:T(8,128)(2,1)} %all-gather.2.cloned.1.call-done) | copy-start | bytes 12582916
  495.5 1.3 copy-start.10
  496.8 4.0 collective-permute-start
  499.2 1.7 copy-start.8
  500.3 4.0 collective-permute-start.2
  500.9 3.5 copy-start.9
  500.9 18.5 %copy-start.1 = (bf16[2,8,128,512]{3,2,1,0:T(8,128)(2,1)S(1)}, bf16[2,8,128,512]{3,2,1,0:T(8,128)(2,1)}, u32[]{:S(2)}) copy-start(bf16[2,8,128,512]{3,2,1,0:T(8,128)(2,1)} %param.14) | copy-start | bytes 6291460
  502.8 9.3 %collective-permute-start.1 = (bf16[1,256,512]{2,1,0:T(8,128)(2,1)S(1)}, bf16[1,256,512]{2,1,0:T(8,128)(2,1)}, u32[]{:S(2)}, u32[]{:S(2)}) collective-permute-start(bf16[1,256,512]{2,1,0:T(8,128)(2,1)S(1)} %dynamic-slice_convert_fusion.1), channel_id=1, source_target_pairs={{0,2},{1,3},{2,0},{3,1},{4,6},{5,7},{6,4},{7,5},{8,10},{9,11},{10,... | collective-permute-start | bytes 786440 | tf_op jit(solution)/shard_map/ppermute | solution.py:239
  505.8 1.0 copy-start.7
  507.5 9.8 %collective-permute-start.3 = (bf16[1,256,512]{2,1,0:T(8,128)(2,1)}, bf16[1,256,512]{2,1,0:T(8,128)(2,1)}, u32[]{:S(2)}, u32[]{:S(2)}) collective-permute-start(bf16[1,256,512]{2,1,0:T(8,128)(2,1)} %dynamic-slice_convert_fusion), channel_id=1, source_target_pairs={{0,2},{1,3},{2,0},{3,1},{4,6},{5,7},{6,4},{7,5},{8,10},{9,11},{10,... | collective-permute-start | bytes 786440 | tf_op jit(solution)/shard_map/ppermute | solution.py:239
Sparse Core Ops, SparseCore 0:
  37.4 346.5 reduce-scatter.1
  420.0 70.1 all-gather.1

commit v10 on v7

--- a/solution.py
+++ b/solution.py
@@ -1,3 +1,4 @@
+import functools
 import math
 
 import jax
@@ -112,6 +113,7 @@
     hist_len,
     res_count,
     parents,
+    ring,
 ):
     pool_size = lax.axis_size("pool")
     my_index = lax.axis_index("pool")
@@ -205,12 +207,53 @@
         )
         outputs.append(finish(result, DRAFT))
     attention = jnp.concatenate(outputs, 0)
-    partial_out = jnp.dot(
-        lax.all_gather(attention, "pool", axis=0, tiled=True),
-        w_out,
-        preferred_element_type=jnp.float32,
-    )
-    return halving_sum(partial_out, "tp").astype(jnp.bfloat16)
+    return halving_sum(ring_product(attention, w_out, "pool", ring), "tp").astype(jnp.bfloat16)
+
+
+def ring_product(block, weights, axis_name, ring):
+    count = len(ring)
+    me = lax.axis_index(axis_name)
+    ring_order = jnp.array(ring, jnp.int32)
+    position = jnp.array([ring.index(index) for index in range(count)], jnp.int32)[me]
+    forward = [(ring[k], ring[(k + 1) % count]) for k in range(count)]
+    backward = [(ring[k], ring[(k - 1) % count]) for k in range(count)]
+    product = jnp.zeros((count, block.shape[0], weights.shape[1]), jnp.float32)
+
+    def place(product, rows, owner):
+        return lax.dynamic_update_index_in_dim(
+            product, jnp.dot(rows, weights, preferred_element_type=jnp.float32), owner, 0
+        )
+
+    product = place(product, block, me)
+    ahead = block
+    behind = block
+    for step in range(1, count // 2 + 1):
+        ahead = lax.ppermute(ahead, axis_name, forward)
+        product = place(product, ahead, ring_order[(position - step) % count])
+        if step < count - step:
+            behind = lax.ppermute(behind, axis_name, backward)
+            product = place(product, behind, ring_order[(position + step) % count])
+    return product.reshape(count * block.shape[0], weights.shape[1])
+
+
+def grid_ring(mesh):
+    count = mesh.shape["pool"]
+    try:
+        places = {}
+        for index in range(count):
+            device = mesh.devices[index, 0]
+            places[(device.coords[2], device.coords[0])] = index
+        rows = sorted({z for z, x in places})
+        cols = sorted({x for z, x in places})
+        if len(rows) % 2 or len(rows) * len(cols) != count or len(cols) < 2:
+            return list(range(count))
+        cycle = [places[(z, cols[0])] for z in rows]
+        for k, z in enumerate(reversed(rows)):
+            line = cols[1:] if k % 2 == 0 else cols[:0:-1]
+            cycle += [places[(z, x)] for x in line]
+        return cycle
+    except (AttributeError, IndexError, KeyError, TypeError):
+        return list(range(count))
 
 
 def halving_sum(partial, axis_name):
@@ -248,4 +291,4 @@
         P(),
     )
     out_specs = P("tp", "pool")
-    return jax.shard_map(body, mesh=mesh, in_specs=in_specs, out_specs=out_specs, check_vma=False)
+    return jax.shard_map(functools.partial(body, ring=grid_ring(mesh)), mesh=mesh, in_specs=in_specs, out_specs=out_specs, check_vma=False)

time: 533 us -> 520 us (0.976); the launches traced: 533 us -> 513 us
  waiting for transfers between devices: 374 us -> 327 us
  between operations: 14 us -> 32.2 us
  starting transfers between devices: 17.5 us -> 24.6 us
    all_gather x1 -> x0, waiting for transfers between devices: 70.3 us -> none  [body(): lax.all_gather(attention, 'pool', axis=0, tiled=True)]
    ppermute x0 -> x7, waiting for transfers between devices: none -> 26.7 us  [the longest x4 26.7 us: ring_product(): ahead = lax.ppermute(ahead, axis_name, forward)]
    ppermute x0 -> x7, starting transfers between devices: none -> 6.77 us  [the longest x3 5.84 us: ring_product(): behind = lax.ppermute(behind, axis_name, backward)]
  transfers between devices with their start and end apart: 7 -> 13, of which waited for: 6 -> 8; matrix products, arithmetic and copies ran while one was open for 13% -> 15% of each run, Pallas kernels for 0% -> 0%
where the time goes in v10:
time: 520 us; the launch traced here: 513 us
  waiting for transfers between devices  327 us (63%)
  local copies, waits for them, and re-layouts  62.2 us (12%)
  matrix products  34.9 us (7%)
  between operations  32.2 us (6%)
  other arithmetic  31.4 us (6%)
  starting transfers between devices  24.6 us (5%)
    all_to_all x1, waiting for transfers between devices, body(): lax.all_to_all(kv_pool[pack_index], 'pool', split_axis=0, concat_axis=0,...  219 us
    all_to_all x1, waiting for transfers between devices, body(): lax.all_to_all(spread[hot_owner], 'pool', split_axis=0, concat_axis=0, ti...  38.4 us
    ppermute x4, waiting for transfers between devices, ring_product(): ahead = lax.ppermute(ahead, axis_name, forward)  26.7 us
    all_to_all x1, waiting for transfers between devices, body(): lax.all_to_all(kv_pool[extra_index].reshape(pool_size, piece_rows, kv_col...  25.7 us
    ppermute x2, waiting for transfers between devices, halving_sum(): lax.ppermute(send, axis_name, [(j, j ^ bit) for j in range(size)])  17.2 us
    select_n x2, other arithmetic, body(): jnp.where((numbers < my_resident[local_user])[:, None, None], resident_pa...  13.9 us
    gather x2, local copies, waits for them, and re-layouts, body(): regular_pages = arrived[owner * capacity + jnp.minimum(rank, capacity - 1)]  12.5 us
    dot_general x1, matrix products, body(): jnp.dot(draft_states, w_qkv, preferred_element_type=jnp.float32)  10.9 us
  transfers between devices with their start and end apart: 13, of which 8 were waited for; matrix products, arithmetic and copies ran while one was open for 15% of the time, Pallas kernels for 0%

profile of v10, /device:TPU:0, one launch (start us, length us, event | category | flops | bytes accessed | tf_op | source)
XLA Modules:
  0.0 512.8 jit_solution(4168506810387053948)
XLA Ops:
  13.4 5.6 %gather_fusion.3 = bf16[8,128,512]{2,1,0:T(8,128)(2,1)} fusion(bf16[80,128,512]{2,1,0:T(8,128)(2,1)} %param.15, s32[1024]{0:T(1024)S(1)} %pad_clamp_fusion.5), kind=kCustom, calls=%fused_computation.3 | custom fusion | bytes 2097184 | tf_op jit(solution)/shard_map/gather | solution.py:171
  19.0 7.3 %all-to-all-start.1 = ((bf16[8,128,512]{2,1,0:T(8,128)(2,1)}), bf16[8,128,512]{2,1,0:T(8,128)(2,1)S(1)}, u32[]{:S(2)}, u32[]{:S(2)}) async-start(bf16[8,128,512]{2,1,0:T(8,128)(2,1)} %gather_fusion.3), calls=%async_computation.2 | async-start | bytes 2097152 | tf_op jit(solution)/shard_map/all_to_all | solution.py:170
  26.3 10.9 %fusion.140 = f32[1024,2560]{1,0:T(8,128)} fusion(bf16[1024,1024]{1,0:T(8,128)(2,1)} %param.12, bf16[1024,2560]{1,0:T(8,128)(2,1)} %param.13), kind=kOutput, calls=%fused_computation.266 | convolution fusion | flops 5368709120 | bytes 17825792 | tf_op jit(solution)/shard_map/dot_general | solution.py:124
  38.1 25.7 %all-to-all-done.1 = bf16[8,128,512]{2,1,0:T(8,128)(2,1)S(1)} async-done(((bf16[8,128,512]{2,1,0:T(8,128)(2,1)}), bf16[8,128,512]{2,1,0:T(8,128)(2,1)S(1)}, u32[]{:S(2)}, u32[]{:S(2)}) %all-to-all-start.1) | async-done | bytes 1048608 | tf_op jit(solution)/shard_map/all_to_all | solution.py:170
  65.4 3.6 all-to-all-start.2
  71.4 9.7 %gather_fusion.1 = bf16[64,128,512]{2,1,0:T(8,128)(2,1)} fusion(bf16[80,128,512]{2,1,0:T(8,128)(2,1)} %param.15, s32[1024]{0:T(1024)S(1)} %pad_clamp_fusion.7), kind=kCustom, calls=%fused_computation.1 | custom fusion | bytes 16777472 | tf_op jit(solution)/shard_map/gather | solution.py:168
  81.2 38.4 %all-to-all-done.2 = bf16[8,128,512]{2,1,0:T(8,128)(2,1)S(1)} async-done(((bf16[8,128,512]{2,1,0:T(8,128)(2,1)}), bf16[8,128,512]{2,1,0:T(8,128)(2,1)S(1)}, u32[]{:S(2)}, u32[]{:S(2)}) %all-to-all-start.2) | async-done | bytes 1048608 | tf_op jit(solution)/shard_map/all_to_all | solution.py:177
  119.6 5.6 %all-to-all-start = ((bf16[64,128,512]{2,1,0:T(8,128)(2,1)}), bf16[64,128,512]{2,1,0:T(8,128)(2,1)}, u32[]{:S(2)}, u32[]{:S(2)}) async-start(bf16[64,128,512]{2,1,0:T(8,128)(2,1)} %gather_fusion.1), calls=%async_computation.1 | async-start | bytes 16777216 | tf_op jit(solution)/shard_map/all_to_all | solution.py:167
  127.4 2.8 gather_fusion.6
  130.2 2.9 gather_fusion
  138.0 2.8 gather_fusion.8
  140.8 2.8 gather_fusion.5
  143.5 219.4 %all-to-all-done = bf16[64,128,512]{2,1,0:T(8,128)(2,1)} async-done(((bf16[64,128,512]{2,1,0:T(8,128)(2,1)}), bf16[64,128,512]{2,1,0:T(8,128)(2,1)}, u32[]{:S(2)}, u32[]{:S(2)}) %all-to-all-start) | async-done | bytes 8388640 | tf_op jit(solution)/shard_map/all_to_all | solution.py:167
  363.0 6.3 %gather_fusion.7 = bf16[32,128,512]{2,1,0:T(8,128)(2,1)} fusion(bf16[64,128,512]{2,1,0:T(8,128)(2,1)} %all-to-all-done, s32[1024]{0:T(1024)S(1)} %pad_clamp_fusion.1), kind=kCustom, calls=%fused_computation.7 | custom fusion | bytes 8388736 | tf_op jit(solution)/shard_map/gather | solution.py:193
  369.2 6.3 %gather_fusion.2 = bf16[32,128,512]{2,1,0:T(8,128)(2,1)} fusion(bf16[64,128,512]{2,1,0:T(8,128)(2,1)} %all-to-all-done, s32[1024]{0:T(1024)S(1)} %pad_clamp_fusion.6), kind=kCustom, calls=%fused_computation.2 | custom fusion | bytes 8388736 | tf_op jit(solution)/shard_map/gather | solution.py:193
  375.5 9.5 %fusion.8 = bf16[4096,512]{1,0:T(8,128)(2,1)} fusion(bf16[32,128,512]{2,1,0:T(8,128)(2,1)} %gather_fusion.8, bf16[32,128,512]{2,1,0:T(8,128)(2,1)} %gather_fusion.7, bf16[32,128,512]{2,1,0:T(8,128)(2,1)} %gather_fusion.6, pred[4096]{0:T(1024)(128)(4,1)S(1)} %get-tuple-element.78, pred[4096]{0:T(1024)(128)(4,1)S(1)} %broadcast_bitcast_fusion.3), kind=kLoop, calls=%fused_computation.28 | loop fusion | flops 4194304 | bytes 16785408 | tf_op jit(solution)/shard_map/jit(_where)/select_n | solution.py:195
  385.5 4.4 fusion.9
  395.4 3.3 fusion.4
  406.7 3.3 fusion
  444.6 9.1 %collective-permute-done.2 = bf16[128,2048]{1,0:T(8,128)(2,1)S(1)} collective-permute-done((bf16[128,2048]{1,0:T(8,128)(2,1)S(1)}, bf16[128,2048]{1,0:T(8,128)(2,1)S(1)}, u32[]{:S(2)}, u32[]{:S(2)}) %collective-permute-start.2) | collective-permute-done | bytes 524320 | tf_op jit(solution)/shard_map/ppermute | solution.py:231
  457.3 8.6 %collective-permute-done.4 = bf16[128,2048]{1,0:T(8,128)(2,1)S(1)} collective-permute-done((bf16[128,2048]{1,0:T(8,128)(2,1)S(1)}, bf16[128,2048]{1,0:T(8,128)(2,1)S(1)}, u32[]{:S(2)}, u32[]{:S(2)}) %collective-permute-start.4) | collective-permute-done | bytes 524320 | tf_op jit(solution)/shard_map/ppermute | solution.py:231
  467.7 9.1 %collective-permute-done.6 = bf16[128,2048]{1,0:T(8,128)(2,1)S(1)} collective-permute-done((bf16[128,2048]{1,0:T(8,128)(2,1)S(1)}, bf16[128,2048]{1,0:T(8,128)(2,1)S(1)}, u32[]{:S(2)}, u32[]{:S(2)}) %collective-permute-start.6) | collective-permute-done | bytes 524320 | tf_op jit(solution)/shard_map/ppermute | solution.py:231
  480.9 4.5 collective-permute-done.7
  490.8 12.7 %collective-permute-done.8 = bf16[1,256,1024]{2,1,0:T(8,128)(2,1)S(1)} collective-permute-done((bf16[1,256,1024]{2,1,0:T(8,128)(2,1)S(1)}, bf16[1,256,1024]{2,1,0:T(8,128)(2,1)S(1)}, u32[]{:S(2)}, u32[]{:S(2)}) %collective-permute-start.8) | collective-permute-done | bytes 524320 | tf_op jit(solution)/shard_map/ppermute | solution.py:274
  (160 shorter events, 66.2 us)
Async XLA Ops:
  6.5 120.9 %copy-start = (bf16[2,8,128,512]{3,2,1,0:T(8,128)(2,1)S(1)}, bf16[2,8,128,512]{3,2,1,0:T(8,128)(2,1)}, u32[]{:S(2)}) copy-start(bf16[2,8,128,512]{3,2,1,0:T(8,128)(2,1)} %param.16) | copy-start | bytes 6291460
  19.0 44.8 %all-to-all-start.1 = ((bf16[8,128,512]{2,1,0:T(8,128)(2,1)}), bf16[8,128,512]{2,1,0:T(8,128)(2,1)S(1)}, u32[]{:S(2)}, u32[]{:S(2)}) async-start(bf16[8,128,512]{2,1,0:T(8,128)(2,1)} %gather_fusion.3), calls=%async_computation.2 | async-start | bytes 2097152 | tf_op jit(solution)/shard_map/all_to_all | solution.py:170
  26.3 363.6 %reduce-scatter.2.cloned.1.call-start = ((), (), s32[]{:S(2)}) async-start(), calls=%async_computation.4 | async-start | bytes 11796480 | tf_op jit(solution)/shard_map/reduce_scatter | solution.py:123
  65.4 54.1 %all-to-all-start.2 = ((bf16[8,128,512]{2,1,0:T(8,128)(2,1)}), bf16[8,128,512]{2,1,0:T(8,128)(2,1)S(1)}, u32[]{:S(2)}, u32[]{:S(2)}) async-start(bf16[8,128,512]{2,1,0:T(8,128)(2,1)} %gather_fusion.4), calls=%async_computation.3 | async-start | bytes 2097152 | tf_op jit(solution)/shard_map/all_to_all | solution.py:177
  81.2 46.0 %copy-start.12 = (s32[16]{0:T(128)S(1)}, s32[16]{0:T(128)}, u32[]{:S(2)}) copy-start(s32[16]{0:T(128)} %param.20) | copy-start | bytes 196
  119.6 243.4 %all-to-all-start = ((bf16[64,128,512]{2,1,0:T(8,128)(2,1)}), bf16[64,128,512]{2,1,0:T(8,128)(2,1)}, u32[]{:S(2)}, u32[]{:S(2)}) async-start(bf16[64,128,512]{2,1,0:T(8,128)(2,1)} %gather_fusion.1), calls=%async_computation.1 | async-start | bytes 16777216 | tf_op jit(solution)/shard_map/all_to_all | solution.py:167
  130.2 5.2 %copy-start.11 = (s32[16]{0:T(128)S(1)}, s32[16]{0:T(128)}, u32[]{:S(2)}) copy-start(s32[16]{0:T(128)} %param.19) | copy-start | bytes 196
  375.5 9.6 %copy-start.4 = (bf16[32,128,512]{2,1,0:T(8,128)(2,1)S(1)}, bf16[32,128,512]{2,1,0:T(8,128)(2,1)}, u32[]{:S(2)}) copy-start(bf16[32,128,512]{2,1,0:T(8,128)(2,1)} %gather_fusion) | copy-start | bytes 12582916
  375.5 9.6 %copy-start.5 = (bf16[32,128,512]{2,1,0:T(8,128)(2,1)S(1)}, bf16[32,128,512]{2,1,0:T(8,128)(2,1)}, u32[]{:S(2)}) copy-start(bf16[32,128,512]{2,1,0:T(8,128)(2,1)} %gather_fusion.5) | copy-start | bytes 12582916
  375.5 10.0 %copy-start.6 = (bf16[32,128,512]{2,1,0:T(8,128)(2,1)S(1)}, bf16[32,128,512]{2,1,0:T(8,128)(2,1)}, u32[]{:S(2)}) copy-start(bf16[32,128,512]{2,1,0:T(8,128)(2,1)} %gather_fusion.2) | copy-start | bytes 12582916
  391.6 2.2 copy-start.8
  415.1 3.9 copy-start.13
  415.1 9.1 %copy-start.10 = (s32[8]{0:T(128)S(1)}, s32[8]{0:T(128)}, u32[]{:S(2)}) copy-start(s32[8]{0:T(128)} %constant.198.clone) | copy-start | bytes 100
  416.7 24.4 %collective-permute-start = (bf16[128,2048]{1,0:T(8,128)(2,1)S(1)}, bf16[128,2048]{1,0:T(8,128)(2,1)S(1)}, u32[]{:S(2)}, u32[]{:S(2)}) collective-permute-start(bf16[128,2048]{1,0:T(8,128)(2,1)S(1)} %bitcast_dynamic-update-slice_fusion), channel_id=1, source_target_pairs={{0,8},{8,16},{16,24},{24,28},{28,20},{20,12},{12,4},{4,0},{1,9},{9... | collective-permute-start | bytes 1572872 | tf_op jit(solution)/shard_map/ppermute | solution.py:231
  416.7 24.5 %collective-permute-start.1 = (bf16[128,2048]{1,0:T(8,128)(2,1)S(1)}, bf16[128,2048]{1,0:T(8,128)(2,1)S(1)}, u32[]{:S(2)}, u32[]{:S(2)}) collective-permute-start(bf16[128,2048]{1,0:T(8,128)(2,1)S(1)} %bitcast_dynamic-update-slice_fusion), channel_id=1, source_target_pairs={{0,4},{8,0},{16,8},{24,16},{28,24},{20,28},{12,20},{4,12},{1,5},{9... | collective-permute-start | bytes 1572872 | tf_op jit(solution)/shard_map/ppermute | solution.py:234
  438.1 2.2 copy-start.2
  441.0 12.7 %collective-permute-start.2 = (bf16[128,2048]{1,0:T(8,128)(2,1)S(1)}, bf16[128,2048]{1,0:T(8,128)(2,1)S(1)}, u32[]{:S(2)}, u32[]{:S(2)}) collective-permute-start(bf16[128,2048]{1,0:T(8,128)(2,1)S(1)} %collective-permute-done), channel_id=1, source_target_pairs={{0,8},{8,16},{16,24},{24,28},{28,20},{20,12},{12,4},{4,0},{1,9},{9... | collective-permute-start | bytes 1572872 | tf_op jit(solution)/shard_map/ppermute | solution.py:231
  441.2 12.9 %collective-permute-start.3 = (bf16[128,2048]{1,0:T(8,128)(2,1)S(1)}, bf16[128,2048]{1,0:T(8,128)(2,1)S(1)}, u32[]{:S(2)}, u32[]{:S(2)}) collective-permute-start(bf16[128,2048]{1,0:T(8,128)(2,1)S(1)} %collective-permute-done.1), channel_id=1, source_target_pairs={{0,4},{8,0},{16,8},{24,16},{28,24},{20,28},{12,20},{4,12},{1,5},{9... | collective-permute-start | bytes 1572872 | tf_op jit(solution)/shard_map/ppermute | solution.py:234
  453.7 12.1 %collective-permute-start.4 = (bf16[128,2048]{1,0:T(8,128)(2,1)S(1)}, bf16[128,2048]{1,0:T(8,128)(2,1)S(1)}, u32[]{:S(2)}, u32[]{:S(2)}) collective-permute-start(bf16[128,2048]{1,0:T(8,128)(2,1)S(1)} %collective-permute-done.2), channel_id=1, source_target_pairs={{0,8},{8,16},{16,24},{24,28},{28,20},{20,12},{12,4},{4,0},{1,9},{9... | collective-permute-start | bytes 1572872 | tf_op jit(solution)/shard_map/ppermute | solution.py:231
  454.1 12.8 %collective-permute-start.5 = (bf16[128,2048]{1,0:T(8,128)(2,1)S(1)}, bf16[128,2048]{1,0:T(8,128)(2,1)S(1)}, u32[]{:S(2)}, u32[]{:S(2)}) collective-permute-start(bf16[128,2048]{1,0:T(8,128)(2,1)S(1)} %collective-permute-done.3), channel_id=1, source_target_pairs={{0,4},{8,0},{16,8},{24,16},{28,24},{20,28},{12,20},{4,12},{1,5},{9... | collective-permute-start | bytes 1572872 | tf_op jit(solution)/shard_map/ppermute | solution.py:234
  465.8 10.9 %collective-permute-start.6 = (bf16[128,2048]{1,0:T(8,128)(2,1)S(1)}, bf16[128,2048]{1,0:T(8,128)(2,1)S(1)}, u32[]{:S(2)}, u32[]{:S(2)}) collective-permute-start(bf16[128,2048]{1,0:T(8,128)(2,1)S(1)} %collective-permute-done.4), channel_id=1, source_target_pairs={{0,8},{8,16},{16,24},{24,28},{28,20},{20,12},{12,4},{4,0},{1,9},{9... | collective-permute-start | bytes 1572872 | tf_op jit(solution)/shard_map/ppermute | solution.py:231
  480.9 4.5 collective-permute-start.7
  480.9 24.7 %copy-start.1 = (bf16[2,8,128,512]{3,2,1,0:T(8,128)(2,1)S(1)}, bf16[2,8,128,512]{3,2,1,0:T(8,128)(2,1)}, u32[]{:S(2)}) copy-start(bf16[2,8,128,512]{3,2,1,0:T(8,128)(2,1)} %param.16) | copy-start | bytes 6291460
  489.5 14.0 %collective-permute-start.8 = (bf16[1,256,1024]{2,1,0:T(8,128)(2,1)S(1)}, bf16[1,256,1024]{2,1,0:T(8,128)(2,1)S(1)}, u32[]{:S(2)}, u32[]{:S(2)}) collective-permute-start(bf16[1,256,1024]{2,1,0:T(8,128)(2,1)S(1)} %dynamic-slice_convert_fusion), channel_id=1, source_target_pairs={{0,2},{1,3},{2,0},{3,1},{4,6},{5,7},{6,4},{7,5},{8,10},{9,11},{10,... | collective-permute-start | bytes 1572872 | tf_op jit(solution)/shard_map/ppermute | solution.py:274
  (3 other events, 5.5 us)
Sparse Core Ops, SparseCore 0:
  37.4 346.6 reduce-scatter.1

commit v11 on v10

--- a/solution.py
+++ b/solution.py
@@ -227,12 +227,19 @@
     product = place(product, block, me)
     ahead = block
     behind = block
+    half = block.shape[0] // 2
     for step in range(1, count // 2 + 1):
-        ahead = lax.ppermute(ahead, axis_name, forward)
-        product = place(product, ahead, ring_order[(position - step) % count])
         if step < count - step:
+            ahead = lax.ppermute(ahead, axis_name, forward)
+            product = place(product, ahead, ring_order[(position - step) % count])
             behind = lax.ppermute(behind, axis_name, backward)
             product = place(product, behind, ring_order[(position + step) % count])
+        else:
+            first = lax.ppermute(ahead[:half], axis_name, forward)
+            second = lax.ppermute(behind[half:], axis_name, backward)
+            product = place(
+                product, jnp.concatenate([first, second], 0), ring_order[(position - step) % count]
+            )
     return product.reshape(count * block.shape[0], weights.shape[1])
 
 

time: 520 us -> 516 us (level)
  waiting for transfers between devices: 327 us -> 321 us
    ppermute x4 -> x3, waiting for transfers between devices: 26.7 us -> 17.6 us  [ring_product(): ahead = lax.ppermute(ahead, axis_name, forward)]
  transfers between devices with their start and end apart: 13 -> 14, of which waited for: 8 -> 9; matrix products, arithmetic and copies ran while one was open for 15% -> 15% of each run, Pallas kernels for 0% -> 0%
where the time goes in v11:
time: 516 us; the launch traced here: 509 us
  waiting for transfers between devices  321 us (62%)
  local copies, waits for them, and re-layouts  62.2 us (12%)
  matrix products  34.9 us (7%)
  between operations  32.2 us (6%)
  other arithmetic  31.4 us (6%)
  starting transfers between devices  26.5 us (5%)
    all_to_all x1, waiting for transfers between devices, body(): lax.all_to_all(kv_pool[pack_index], 'pool', split_axis=0, concat_axis=0,...  219 us
    all_to_all x1, waiting for transfers between devices, body(): lax.all_to_all(spread[hot_owner], 'pool', split_axis=0, concat_axis=0, ti...  38.4 us
    all_to_all x1, waiting for transfers between devices, body(): lax.all_to_all(kv_pool[extra_index].reshape(pool_size, piece_rows, kv_col...  25.7 us
    ppermute x3, waiting for transfers between devices, ring_product(): ahead = lax.ppermute(ahead, axis_name, forward)  17.6 us
    ppermute x2, waiting for transfers between devices, halving_sum(): lax.ppermute(send, axis_name, [(j, j ^ bit) for j in range(size)])  17 us
    select_n x2, other arithmetic, body(): jnp.where((numbers < my_resident[local_user])[:, None, None], resident_pa...  13.9 us
    gather x2, local copies, waits for them, and re-layouts, body(): regular_pages = arrived[owner * capacity + jnp.minimum(rank, capacity - 1)]  12.5 us
    dot_general x1, matrix products, body(): jnp.dot(draft_states, w_qkv, preferred_element_type=jnp.float32)  10.9 us
  transfers between devices with their start and end apart: 14, of which 9 were waited for; matrix products, arithmetic and copies ran while one was open for 15% of the time, Pallas kernels for 0%

profile of v11, /device:TPU:0, one launch (start us, length us, event | category | flops | bytes accessed | tf_op | source)
XLA Modules:
  0.0 508.7 jit_solution(16085465511799100091)
XLA Ops:
  13.4 5.6 %gather_fusion.3 = bf16[8,128,512]{2,1,0:T(8,128)(2,1)} fusion(bf16[80,128,512]{2,1,0:T(8,128)(2,1)} %param.15, s32[1024]{0:T(1024)S(1)} %pad_clamp_fusion.5), kind=kCustom, calls=%fused_computation.3 | custom fusion | bytes 2097184 | tf_op jit(solution)/shard_map/gather | solution.py:171
  19.0 7.3 %all-to-all-start.1 = ((bf16[8,128,512]{2,1,0:T(8,128)(2,1)}), bf16[8,128,512]{2,1,0:T(8,128)(2,1)S(1)}, u32[]{:S(2)}, u32[]{:S(2)}) async-start(bf16[8,128,512]{2,1,0:T(8,128)(2,1)} %gather_fusion.3), calls=%async_computation.2 | async-start | bytes 2097152 | tf_op jit(solution)/shard_map/all_to_all | solution.py:170
  26.3 10.9 %fusion.144 = f32[1024,2560]{1,0:T(8,128)} fusion(bf16[1024,1024]{1,0:T(8,128)(2,1)} %param.12, bf16[1024,2560]{1,0:T(8,128)(2,1)} %param.13), kind=kOutput, calls=%fused_computation.270 | convolution fusion | flops 5368709120 | bytes 17825792 | tf_op jit(solution)/shard_map/dot_general | solution.py:124
  38.1 25.7 %all-to-all-done.1 = bf16[8,128,512]{2,1,0:T(8,128)(2,1)S(1)} async-done(((bf16[8,128,512]{2,1,0:T(8,128)(2,1)}), bf16[8,128,512]{2,1,0:T(8,128)(2,1)S(1)}, u32[]{:S(2)}, u32[]{:S(2)}) %all-to-all-start.1) | async-done | bytes 1048608 | tf_op jit(solution)/shard_map/all_to_all | solution.py:170
  65.4 3.6 all-to-all-start.2
  71.4 9.7 %gather_fusion.1 = bf16[64,128,512]{2,1,0:T(8,128)(2,1)} fusion(bf16[80,128,512]{2,1,0:T(8,128)(2,1)} %param.15, s32[1024]{0:T(1024)S(1)} %pad_clamp_fusion.7), kind=kCustom, calls=%fused_computation.1 | custom fusion | bytes 16777472 | tf_op jit(solution)/shard_map/gather | solution.py:168
  81.2 38.4 %all-to-all-done.2 = bf16[8,128,512]{2,1,0:T(8,128)(2,1)S(1)} async-done(((bf16[8,128,512]{2,1,0:T(8,128)(2,1)}), bf16[8,128,512]{2,1,0:T(8,128)(2,1)S(1)}, u32[]{:S(2)}, u32[]{:S(2)}) %all-to-all-start.2) | async-done | bytes 1048608 | tf_op jit(solution)/shard_map/all_to_all | solution.py:177
  119.6 5.6 %all-to-all-start = ((bf16[64,128,512]{2,1,0:T(8,128)(2,1)}), bf16[64,128,512]{2,1,0:T(8,128)(2,1)}, u32[]{:S(2)}, u32[]{:S(2)}) async-start(bf16[64,128,512]{2,1,0:T(8,128)(2,1)} %gather_fusion.1), calls=%async_computation.1 | async-start | bytes 16777216 | tf_op jit(solution)/shard_map/all_to_all | solution.py:167
  127.4 2.8 gather_fusion.6
  130.2 2.9 gather_fusion
  138.0 2.8 gather_fusion.8
  140.8 2.8 gather_fusion.5
  143.5 219.4 %all-to-all-done = bf16[64,128,512]{2,1,0:T(8,128)(2,1)} async-done(((bf16[64,128,512]{2,1,0:T(8,128)(2,1)}), bf16[64,128,512]{2,1,0:T(8,128)(2,1)}, u32[]{:S(2)}, u32[]{:S(2)}) %all-to-all-start) | async-done | bytes 8388640 | tf_op jit(solution)/shard_map/all_to_all | solution.py:167
  363.0 6.3 %gather_fusion.7 = bf16[32,128,512]{2,1,0:T(8,128)(2,1)} fusion(bf16[64,128,512]{2,1,0:T(8,128)(2,1)} %all-to-all-done, s32[1024]{0:T(1024)S(1)} %pad_clamp_fusion.1), kind=kCustom, calls=%fused_computation.7 | custom fusion | bytes 8388736 | tf_op jit(solution)/shard_map/gather | solution.py:193
  369.2 6.3 %gather_fusion.2 = bf16[32,128,512]{2,1,0:T(8,128)(2,1)} fusion(bf16[64,128,512]{2,1,0:T(8,128)(2,1)} %all-to-all-done, s32[1024]{0:T(1024)S(1)} %pad_clamp_fusion.6), kind=kCustom, calls=%fused_computation.2 | custom fusion | bytes 8388736 | tf_op jit(solution)/shard_map/gather | solution.py:193
  375.5 9.5 %fusion.8 = bf16[4096,512]{1,0:T(8,128)(2,1)} fusion(bf16[32,128,512]{2,1,0:T(8,128)(2,1)} %gather_fusion.8, bf16[32,128,512]{2,1,0:T(8,128)(2,1)} %gather_fusion.7, bf16[32,128,512]{2,1,0:T(8,128)(2,1)} %gather_fusion.6, pred[4096]{0:T(1024)(128)(4,1)S(1)} %get-tuple-element.78, pred[4096]{0:T(1024)(128)(4,1)S(1)} %broadcast_bitcast_fusion.3), kind=kLoop, calls=%fused_computation.28 | loop fusion | flops 4194304 | bytes 16785408 | tf_op jit(solution)/shard_map/jit(_where)/select_n | solution.py:195
  385.5 4.4 fusion.9
  395.4 3.3 fusion.4
  406.7 3.3 fusion
  444.6 9.1 %collective-permute-done.2 = bf16[128,2048]{1,0:T(8,128)(2,1)S(1)} collective-permute-done((bf16[128,2048]{1,0:T(8,128)(2,1)S(1)}, bf16[128,2048]{1,0:T(8,128)(2,1)S(1)}, u32[]{:S(2)}, u32[]{:S(2)}) %collective-permute-start.2) | collective-permute-done | bytes 524320 | tf_op jit(solution)/shard_map/ppermute | solution.py:233
  457.3 8.5 %collective-permute-done.4 = bf16[128,2048]{1,0:T(8,128)(2,1)S(1)} collective-permute-done((bf16[128,2048]{1,0:T(8,128)(2,1)S(1)}, bf16[128,2048]{1,0:T(8,128)(2,1)S(1)}, u32[]{:S(2)}, u32[]{:S(2)}) %collective-permute-start.4) | collective-permute-done | bytes 524320 | tf_op jit(solution)/shard_map/ppermute | solution.py:233
  469.4 2.8 collective-permute-done.6
  476.8 4.5 collective-permute-done.8
  486.9 12.5 %collective-permute-done.9 = bf16[1,256,1024]{2,1,0:T(8,128)(2,1)S(1)} collective-permute-done((bf16[1,256,1024]{2,1,0:T(8,128)(2,1)S(1)}, bf16[1,256,1024]{2,1,0:T(8,128)(2,1)S(1)}, u32[]{:S(2)}, u32[]{:S(2)}) %collective-permute-start.9) | collective-permute-done | bytes 524320 | tf_op jit(solution)/shard_map/ppermute | solution.py:281
  (164 shorter events, 68.6 us)
Async XLA Ops:
  6.5 120.9 %copy-start = (bf16[2,8,128,512]{3,2,1,0:T(8,128)(2,1)S(1)}, bf16[2,8,128,512]{3,2,1,0:T(8,128)(2,1)}, u32[]{:S(2)}) copy-start(bf16[2,8,128,512]{3,2,1,0:T(8,128)(2,1)} %param.16) | copy-start | bytes 6291460
  19.0 44.8 %all-to-all-start.1 = ((bf16[8,128,512]{2,1,0:T(8,128)(2,1)}), bf16[8,128,512]{2,1,0:T(8,128)(2,1)S(1)}, u32[]{:S(2)}, u32[]{:S(2)}) async-start(bf16[8,128,512]{2,1,0:T(8,128)(2,1)} %gather_fusion.3), calls=%async_computation.2 | async-start | bytes 2097152 | tf_op jit(solution)/shard_map/all_to_all | solution.py:170
  26.3 363.6 %reduce-scatter.2.cloned.1.call-start = ((), (), s32[]{:S(2)}) async-start(), calls=%async_computation.4 | async-start | bytes 11796480 | tf_op jit(solution)/shard_map/reduce_scatter | solution.py:123
  65.4 54.1 %all-to-all-start.2 = ((bf16[8,128,512]{2,1,0:T(8,128)(2,1)}), bf16[8,128,512]{2,1,0:T(8,128)(2,1)S(1)}, u32[]{:S(2)}, u32[]{:S(2)}) async-start(bf16[8,128,512]{2,1,0:T(8,128)(2,1)} %gather_fusion.4), calls=%async_computation.3 | async-start | bytes 2097152 | tf_op jit(solution)/shard_map/all_to_all | solution.py:177
  81.2 46.0 %copy-start.12 = (s32[16]{0:T(128)S(1)}, s32[16]{0:T(128)}, u32[]{:S(2)}) copy-start(s32[16]{0:T(128)} %param.20) | copy-start | bytes 196
  119.6 243.4 %all-to-all-start = ((bf16[64,128,512]{2,1,0:T(8,128)(2,1)}), bf16[64,128,512]{2,1,0:T(8,128)(2,1)}, u32[]{:S(2)}, u32[]{:S(2)}) async-start(bf16[64,128,512]{2,1,0:T(8,128)(2,1)} %gather_fusion.1), calls=%async_computation.1 | async-start | bytes 16777216 | tf_op jit(solution)/shard_map/all_to_all | solution.py:167
  130.2 5.2 %copy-start.11 = (s32[16]{0:T(128)S(1)}, s32[16]{0:T(128)}, u32[]{:S(2)}) copy-start(s32[16]{0:T(128)} %param.19) | copy-start | bytes 196
  375.5 9.6 %copy-start.4 = (bf16[32,128,512]{2,1,0:T(8,128)(2,1)S(1)}, bf16[32,128,512]{2,1,0:T(8,128)(2,1)}, u32[]{:S(2)}) copy-start(bf16[32,128,512]{2,1,0:T(8,128)(2,1)} %gather_fusion) | copy-start | bytes 12582916
  375.5 9.6 %copy-start.5 = (bf16[32,128,512]{2,1,0:T(8,128)(2,1)S(1)}, bf16[32,128,512]{2,1,0:T(8,128)(2,1)}, u32[]{:S(2)}) copy-start(bf16[32,128,512]{2,1,0:T(8,128)(2,1)} %gather_fusion.5) | copy-start | bytes 12582916
  375.5 10.0 %copy-start.6 = (bf16[32,128,512]{2,1,0:T(8,128)(2,1)S(1)}, bf16[32,128,512]{2,1,0:T(8,128)(2,1)}, u32[]{:S(2)}) copy-start(bf16[32,128,512]{2,1,0:T(8,128)(2,1)} %gather_fusion.2) | copy-start | bytes 12582916
  415.1 3.9 copy-start.13
  415.1 9.1 %copy-start.10 = (s32[8]{0:T(128)S(1)}, s32[8]{0:T(128)}, u32[]{:S(2)}) copy-start(s32[8]{0:T(128)} %constant.198.clone) | copy-start | bytes 100
  416.7 24.4 %collective-permute-start = (bf16[128,2048]{1,0:T(8,128)(2,1)S(1)}, bf16[128,2048]{1,0:T(8,128)(2,1)S(1)}, u32[]{:S(2)}, u32[]{:S(2)}) collective-permute-start(bf16[128,2048]{1,0:T(8,128)(2,1)S(1)} %bitcast_dynamic-update-slice_fusion), channel_id=1, source_target_pairs={{0,8},{8,16},{16,24},{24,28},{28,20},{20,12},{12,4},{4,0},{1,9},{9... | collective-permute-start | bytes 1572872 | tf_op jit(solution)/shard_map/ppermute | solution.py:233
  416.7 24.5 %collective-permute-start.1 = (bf16[128,2048]{1,0:T(8,128)(2,1)S(1)}, bf16[128,2048]{1,0:T(8,128)(2,1)S(1)}, u32[]{:S(2)}, u32[]{:S(2)}) collective-permute-start(bf16[128,2048]{1,0:T(8,128)(2,1)S(1)} %bitcast_dynamic-update-slice_fusion), channel_id=1, source_target_pairs={{0,4},{8,0},{16,8},{24,16},{28,24},{20,28},{12,20},{4,12},{1,5},{9... | collective-permute-start | bytes 1572872 | tf_op jit(solution)/shard_map/ppermute | solution.py:235
  438.1 2.2 copy-start.2
  441.0 12.7 %collective-permute-start.2 = (bf16[128,2048]{1,0:T(8,128)(2,1)S(1)}, bf16[128,2048]{1,0:T(8,128)(2,1)S(1)}, u32[]{:S(2)}, u32[]{:S(2)}) collective-permute-start(bf16[128,2048]{1,0:T(8,128)(2,1)S(1)} %collective-permute-done), channel_id=1, source_target_pairs={{0,8},{8,16},{16,24},{24,28},{28,20},{20,12},{12,4},{4,0},{1,9},{9... | collective-permute-start | bytes 1572872 | tf_op jit(solution)/shard_map/ppermute | solution.py:233
  441.2 12.9 %collective-permute-start.3 = (bf16[128,2048]{1,0:T(8,128)(2,1)S(1)}, bf16[128,2048]{1,0:T(8,128)(2,1)S(1)}, u32[]{:S(2)}, u32[]{:S(2)}) collective-permute-start(bf16[128,2048]{1,0:T(8,128)(2,1)S(1)} %collective-permute-done.1), channel_id=1, source_target_pairs={{0,4},{8,0},{16,8},{24,16},{28,24},{20,28},{12,20},{4,12},{1,5},{9... | collective-permute-start | bytes 1572872 | tf_op jit(solution)/shard_map/ppermute | solution.py:235
  453.7 12.0 %collective-permute-start.4 = (bf16[128,2048]{1,0:T(8,128)(2,1)S(1)}, bf16[128,2048]{1,0:T(8,128)(2,1)S(1)}, u32[]{:S(2)}, u32[]{:S(2)}) collective-permute-start(bf16[128,2048]{1,0:T(8,128)(2,1)S(1)} %collective-permute-done.2), channel_id=1, source_target_pairs={{0,8},{8,16},{16,24},{24,28},{28,20},{20,12},{12,4},{4,0},{1,9},{9... | collective-permute-start | bytes 1572872 | tf_op jit(solution)/shard_map/ppermute | solution.py:233
  454.1 12.1 %collective-permute-start.5 = (bf16[128,2048]{1,0:T(8,128)(2,1)S(1)}, bf16[128,2048]{1,0:T(8,128)(2,1)S(1)}, u32[]{:S(2)}, u32[]{:S(2)}) collective-permute-start(bf16[128,2048]{1,0:T(8,128)(2,1)S(1)} %collective-permute-done.3), channel_id=1, source_target_pairs={{0,4},{8,0},{16,8},{24,16},{28,24},{20,28},{12,20},{4,12},{1,5},{9... | collective-permute-start | bytes 1572872 | tf_op jit(solution)/shard_map/ppermute | solution.py:235
  465.8 6.4 %collective-permute-start.6 = (bf16[64,2048]{1,0:T(8,128)(2,1)S(1)}, bf16[64,2048]{1,0:T(8,128)(2,1)S(1)}, u32[]{:S(2)}, u32[]{:S(2)}) collective-permute-start(bf16[64,2048]{1,0:T(8,128)(2,1)S(1)} %slice.252), channel_id=1, source_target_pairs={{0,8},{8,16},{16,24},{24,28},{28,20},{20,12},{12,4},{4,0},{1,9},{9... | collective-permute-start | bytes 786440 | tf_op jit(solution)/shard_map/ppermute | solution.py:238
  466.3 6.4 %collective-permute-start.7 = (bf16[64,2048]{1,0:T(8,128)(2,1)S(1)}, bf16[64,2048]{1,0:T(8,128)(2,1)S(1)}, u32[]{:S(2)}, u32[]{:S(2)}) collective-permute-start(bf16[64,2048]{1,0:T(8,128)(2,1)S(1)} %slice.253), channel_id=1, source_target_pairs={{0,4},{8,0},{16,8},{24,16},{28,24},{20,28},{12,20},{4,12},{1,5},{9... | collective-permute-start | bytes 786440 | tf_op jit(solution)/shard_map/ppermute | solution.py:239
  476.8 4.5 collective-permute-start.8
  476.8 24.7 %copy-start.1 = (bf16[2,8,128,512]{3,2,1,0:T(8,128)(2,1)S(1)}, bf16[2,8,128,512]{3,2,1,0:T(8,128)(2,1)}, u32[]{:S(2)}) copy-start(bf16[2,8,128,512]{3,2,1,0:T(8,128)(2,1)} %param.16) | copy-start | bytes 6291460
  485.4 14.0 %collective-permute-start.9 = (bf16[1,256,1024]{2,1,0:T(8,128)(2,1)S(1)}, bf16[1,256,1024]{2,1,0:T(8,128)(2,1)S(1)}, u32[]{:S(2)}, u32[]{:S(2)}) collective-permute-start(bf16[1,256,1024]{2,1,0:T(8,128)(2,1)S(1)} %dynamic-slice_convert_fusion), channel_id=1, source_target_pairs={{0,2},{1,3},{2,0},{3,1},{4,6},{5,7},{6,4},{7,5},{8,10},{9,11},{10,... | collective-permute-start | bytes 1572872 | tf_op jit(solution)/shard_map/ppermute | solution.py:281
  (4 other events, 7.7 us)
Sparse Core Ops, SparseCore 0:
  37.4 346.6 reduce-scatter.1

commit v12 on v11

--- a/solution.py
+++ b/solution.py
@@ -207,40 +207,48 @@
         )
         outputs.append(finish(result, DRAFT))
     attention = jnp.concatenate(outputs, 0)
-    return halving_sum(ring_product(attention, w_out, "pool", ring), "tp").astype(jnp.bfloat16)
+    return halving_sum(ring_product(attention, w_out, "pool", ring), "tp", 2).astype(jnp.bfloat16)
 
 
 def ring_product(block, weights, axis_name, ring):
     count = len(ring)
     me = lax.axis_index(axis_name)
+    tp_size = lax.axis_size("tp")
+    tp_bit = lax.axis_index("tp") % 2
     ring_order = jnp.array(ring, jnp.int32)
     position = jnp.array([ring.index(index) for index in range(count)], jnp.int32)[me]
     forward = [(ring[k], ring[(k + 1) % count]) for k in range(count)]
     backward = [(ring[k], ring[(k - 1) % count]) for k in range(count)]
-    product = jnp.zeros((count, block.shape[0], weights.shape[1]), jnp.float32)
-
-    def place(product, rows, owner):
-        return lax.dynamic_update_index_in_dim(
-            product, jnp.dot(rows, weights, preferred_element_type=jnp.float32), owner, 0
-        )
-
-    product = place(product, block, me)
+    block_rows = block.shape[0]
+    cols = weights.shape[1]
+    per_tp = count * block_rows // tp_size // block_rows
+    slots = jnp.zeros((tp_size // 2 + 1, per_tp, block_rows, cols), jnp.float32)
+    pairs = [(j, j ^ 1) for j in range(tp_size)]
+
+    def place(slots, rows, owner):
+        product = jnp.dot(rows, weights, preferred_element_type=jnp.float32)
+        total = product + lax.ppermute(product, "tp", pairs)
+        target = owner // per_tp
+        slot = jnp.where(target % 2 == tp_bit, target // 2, tp_size // 2)
+        return lax.dynamic_update_slice(slots, total[None, None], (slot, owner % per_tp, 0, 0))
+
+    slots = place(slots, block, me)
     ahead = block
     behind = block
-    half = block.shape[0] // 2
+    half = block_rows // 2
     for step in range(1, count // 2 + 1):
         if step < count - step:
             ahead = lax.ppermute(ahead, axis_name, forward)
-            product = place(product, ahead, ring_order[(position - step) % count])
+            slots = place(slots, ahead, ring_order[(position - step) % count])
             behind = lax.ppermute(behind, axis_name, backward)
-            product = place(product, behind, ring_order[(position + step) % count])
+            slots = place(slots, behind, ring_order[(position + step) % count])
         else:
             first = lax.ppermute(ahead[:half], axis_name, forward)
             second = lax.ppermute(behind[half:], axis_name, backward)
-            product = place(
-                product, jnp.concatenate([first, second], 0), ring_order[(position - step) % count]
+            slots = place(
+                slots, jnp.concatenate([first, second], 0), ring_order[(position - step) % count]
             )
-    return product.reshape(count * block.shape[0], weights.shape[1])
+    return slots[: tp_size // 2].reshape(tp_size // 2 * per_tp * block_rows, cols)
 
 
 def grid_ring(mesh):
@@ -263,13 +271,12 @@
         return list(range(count))
 
 
-def halving_sum(partial, axis_name):
+def halving_sum(partial, axis_name, bit):
     size = lax.axis_size(axis_name)
     me = lax.axis_index(axis_name)
-    rows = partial.shape[0] // size
+    rows = partial.shape[0] * bit // size
     cols = partial.shape[1]
     held = partial
-    bit = 1
     while bit < size:
         blocks = held.shape[0] // rows
         grouped = held.reshape(blocks // 2, 2, rows, cols)

time: 516 us -> 528 us (1.023)
  waiting for transfers between devices: 321 us -> 332 us
  between operations: 32.2 us -> 37.5 us
    ppermute x3, waiting for transfers between devices: 0.01 us -> 14.2 us  [ring_product(): behind = lax.ppermute(behind, axis_name, backward)]
    ppermute x2 -> x1, waiting for transfers between devices: 17 us -> 12.5 us  [halving_sum(): lax.ppermute(send, axis_name, [(j, j ^ bit) for j in range(size)])]
  transfers between devices with their start and end apart: 14 -> 21, of which waited for: 9 -> 11; matrix products, arithmetic and copies ran while one was open for 15% -> 15% of each run, Pallas kernels for 0% -> 0%
where the time goes in v12:
time: 528 us; the launch traced here: 521 us
  waiting for transfers between devices  332 us (63%)
  local copies, waits for them, and re-layouts  57.2 us (11%)
  between operations  37.5 us (7%)
  matrix products  36.9 us (7%)
  other arithmetic  29.4 us (6%)
  starting transfers between devices  27.9 us (5%)
    all_to_all x1, waiting for transfers between devices, body(): lax.all_to_all(kv_pool[pack_index], 'pool', split_axis=0, concat_axis=0,...  219 us
    all_to_all x1, waiting for transfers between devices, body(): lax.all_to_all(spread[hot_owner], 'pool', split_axis=0, concat_axis=0, ti...  38.4 us
    all_to_all x1, waiting for transfers between devices, body(): lax.all_to_all(kv_pool[extra_index].reshape(pool_size, piece_rows, kv_col...  25.7 us
    ppermute x3, waiting for transfers between devices, ring_product(): ahead = lax.ppermute(ahead, axis_name, forward)  16 us
    ppermute x3, waiting for transfers between devices, ring_product(): behind = lax.ppermute(behind, axis_name, backward)  14.2 us
    select_n x2, other arithmetic, body(): jnp.where((numbers < my_resident[local_user])[:, None, None], resident_pa...  13.9 us
    gather x2, local copies, waits for them, and re-layouts, body(): regular_pages = arrived[owner * capacity + jnp.minimum(rank, capacity - 1)]  12.5 us
    ppermute x1, waiting for transfers between devices, halving_sum(): lax.ppermute(send, axis_name, [(j, j ^ bit) for j in range(size)])  12.5 us
  transfers between devices with their start and end apart: 21, of which 11 were waited for; matrix products, arithmetic and copies ran while one was open for 15% of the time, Pallas kernels for 0%

profile of v12, /device:TPU:0, one launch (start us, length us, event | category | flops | bytes accessed | tf_op | source)
XLA Modules:
  0.0 520.6 jit_solution(16313500483984771252)
XLA Ops:
  13.4 5.6 %gather_fusion.3 = bf16[8,128,512]{2,1,0:T(8,128)(2,1)} fusion(bf16[80,128,512]{2,1,0:T(8,128)(2,1)} %param.15, s32[1024]{0:T(1024)S(1)} %pad_clamp_fusion.5), kind=kCustom, calls=%fused_computation.3 | custom fusion | bytes 2097184 | tf_op jit(solution)/shard_map/gather | solution.py:171
  19.0 7.3 %all-to-all-start.1 = ((bf16[8,128,512]{2,1,0:T(8,128)(2,1)}), bf16[8,128,512]{2,1,0:T(8,128)(2,1)S(1)}, u32[]{:S(2)}, u32[]{:S(2)}) async-start(bf16[8,128,512]{2,1,0:T(8,128)(2,1)} %gather_fusion.3), calls=%async_computation.2 | async-start | bytes 2097152 | tf_op jit(solution)/shard_map/all_to_all | solution.py:170
  26.3 10.9 %fusion.139 = f32[1024,2560]{1,0:T(8,128)} fusion(bf16[1024,1024]{1,0:T(8,128)(2,1)} %param.12, bf16[1024,2560]{1,0:T(8,128)(2,1)} %param.13), kind=kOutput, calls=%fused_computation.263 | convolution fusion | flops 5368709120 | bytes 17825792 | tf_op jit(solution)/shard_map/dot_general | solution.py:124
  38.1 25.7 %all-to-all-done.1 = bf16[8,128,512]{2,1,0:T(8,128)(2,1)S(1)} async-done(((bf16[8,128,512]{2,1,0:T(8,128)(2,1)}), bf16[8,128,512]{2,1,0:T(8,128)(2,1)S(1)}, u32[]{:S(2)}, u32[]{:S(2)}) %all-to-all-start.1) | async-done | bytes 1048608 | tf_op jit(solution)/shard_map/all_to_all | solution.py:170
  65.4 3.6 all-to-all-start.2
  71.4 9.7 %gather_fusion.1 = bf16[64,128,512]{2,1,0:T(8,128)(2,1)} fusion(bf16[80,128,512]{2,1,0:T(8,128)(2,1)} %param.15, s32[1024]{0:T(1024)S(1)} %pad_clamp_fusion.7), kind=kCustom, calls=%fused_computation.1 | custom fusion | bytes 16777472 | tf_op jit(solution)/shard_map/gather | solution.py:168
  81.2 38.4 %all-to-all-done.2 = bf16[8,128,512]{2,1,0:T(8,128)(2,1)S(1)} async-done(((bf16[8,128,512]{2,1,0:T(8,128)(2,1)}), bf16[8,128,512]{2,1,0:T(8,128)(2,1)S(1)}, u32[]{:S(2)}, u32[]{:S(2)}) %all-to-all-start.2) | async-done | bytes 1048608 | tf_op jit(solution)/shard_map/all_to_all | solution.py:177
  119.6 5.6 %all-to-all-start = ((bf16[64,128,512]{2,1,0:T(8,128)(2,1)}), bf16[64,128,512]{2,1,0:T(8,128)(2,1)}, u32[]{:S(2)}, u32[]{:S(2)}) async-start(bf16[64,128,512]{2,1,0:T(8,128)(2,1)} %gather_fusion.1), calls=%async_computation.1 | async-start | bytes 16777216 | tf_op jit(solution)/shard_map/all_to_all | solution.py:167
  130.2 2.9 gather_fusion
  138.0 2.8 gather_fusion.8
  143.5 219.4 %all-to-all-done = bf16[64,128,512]{2,1,0:T(8,128)(2,1)} async-done(((bf16[64,128,512]{2,1,0:T(8,128)(2,1)}), bf16[64,128,512]{2,1,0:T(8,128)(2,1)}, u32[]{:S(2)}, u32[]{:S(2)}) %all-to-all-start) | async-done | bytes 8388640 | tf_op jit(solution)/shard_map/all_to_all | solution.py:167
  363.0 6.3 %gather_fusion.7 = bf16[32,128,512]{2,1,0:T(8,128)(2,1)} fusion(bf16[64,128,512]{2,1,0:T(8,128)(2,1)} %all-to-all-done, s32[1024]{0:T(1024)S(1)} %pad_clamp_fusion.1), kind=kCustom, calls=%fused_computation.7 | custom fusion | bytes 8388736 | tf_op jit(solution)/shard_map/gather | solution.py:193
  369.2 6.3 %gather_fusion.2 = bf16[32,128,512]{2,1,0:T(8,128)(2,1)} fusion(bf16[64,128,512]{2,1,0:T(8,128)(2,1)} %all-to-all-done, s32[1024]{0:T(1024)S(1)} %pad_clamp_fusion.6), kind=kCustom, calls=%fused_computation.2 | custom fusion | bytes 8388736 | tf_op jit(solution)/shard_map/gather | solution.py:193
  375.5 9.5 %fusion.8 = bf16[4096,512]{1,0:T(8,128)(2,1)} fusion(bf16[32,128,512]{2,1,0:T(8,128)(2,1)} %gather_fusion.8, bf16[32,128,512]{2,1,0:T(8,128)(2,1)} %gather_fusion.7, bf16[32,128,512]{2,1,0:T(8,128)(2,1)} %gather_fusion.6, pred[4096]{0:T(1024)(128)(4,1)S(1)} %get-tuple-element.78, pred[4096]{0:T(1024)(128)(4,1)S(1)} %broadcast_bitcast_fusion.3), kind=kLoop, calls=%fused_computation.28 | loop fusion | flops 4194304 | bytes 16785408 | tf_op jit(solution)/shard_map/jit(_where)/select_n | solution.py:195
  385.5 4.4 fusion.9
  395.4 3.3 fusion.4
  406.7 3.3 fusion
  443.1 2.9 fusion.140
  447.4 6.9 %collective-permute-done.3 = bf16[128,2048]{1,0:T(8,128)(2,1)S(1)} collective-permute-done((bf16[128,2048]{1,0:T(8,128)(2,1)S(1)}, bf16[128,2048]{1,0:T(8,128)(2,1)S(1)}, u32[]{:S(2)}, u32[]{:S(2)}) %collective-permute-start.3) | collective-permute-done | bytes 524320 | tf_op jit(solution)/shard_map/ppermute | solution.py:243
  457.3 3.9 collective-permute-done.5
  462.1 7.3 %collective-permute-done.7 = bf16[128,2048]{1,0:T(8,128)(2,1)S(1)} collective-permute-done((bf16[128,2048]{1,0:T(8,128)(2,1)S(1)}, bf16[128,2048]{1,0:T(8,128)(2,1)S(1)}, u32[]{:S(2)}, u32[]{:S(2)}) %collective-permute-start.7) | collective-permute-done | bytes 524320 | tf_op jit(solution)/shard_map/ppermute | solution.py:243
  472.5 12.1 %collective-permute-done.9 = bf16[128,2048]{1,0:T(8,128)(2,1)S(1)} collective-permute-done((bf16[128,2048]{1,0:T(8,128)(2,1)S(1)}, bf16[128,2048]{1,0:T(8,128)(2,1)S(1)}, u32[]{:S(2)}, u32[]{:S(2)}) %collective-permute-start.9) | collective-permute-done | bytes 524320 | tf_op jit(solution)/shard_map/ppermute | solution.py:241
  489.0 3.4 collective-permute-done.13
  498.7 12.5 %collective-permute-done.16 = bf16[1,256,1024]{2,1,0:T(8,128)(2,1)S(1)} collective-permute-done((bf16[1,256,1024]{2,1,0:T(8,128)(2,1)S(1)}, bf16[1,256,1024]{2,1,0:T(8,128)(2,1)S(1)}, u32[]{:S(2)}, u32[]{:S(2)}) %collective-permute-start.16) | collective-permute-done | bytes 524320 | tf_op jit(solution)/shard_map/ppermute | solution.py:288
  (183 shorter events, 69.3 us)
Async XLA Ops:
  6.5 120.9 %copy-start = (bf16[2,8,128,512]{3,2,1,0:T(8,128)(2,1)S(1)}, bf16[2,8,128,512]{3,2,1,0:T(8,128)(2,1)}, u32[]{:S(2)}) copy-start(bf16[2,8,128,512]{3,2,1,0:T(8,128)(2,1)} %param.16) | copy-start | bytes 6291460
  19.0 44.8 %all-to-all-start.1 = ((bf16[8,128,512]{2,1,0:T(8,128)(2,1)}), bf16[8,128,512]{2,1,0:T(8,128)(2,1)S(1)}, u32[]{:S(2)}, u32[]{:S(2)}) async-start(bf16[8,128,512]{2,1,0:T(8,128)(2,1)} %gather_fusion.3), calls=%async_computation.2 | async-start | bytes 2097152 | tf_op jit(solution)/shard_map/all_to_all | solution.py:170
  26.3 363.6 %reduce-scatter.2.cloned.1.call-start = ((), (), s32[]{:S(2)}) async-start(), calls=%async_computation.4 | async-start | bytes 11796480 | tf_op jit(solution)/shard_map/reduce_scatter | solution.py:123
  65.4 54.1 %all-to-all-start.2 = ((bf16[8,128,512]{2,1,0:T(8,128)(2,1)}), bf16[8,128,512]{2,1,0:T(8,128)(2,1)S(1)}, u32[]{:S(2)}, u32[]{:S(2)}) async-start(bf16[8,128,512]{2,1,0:T(8,128)(2,1)} %gather_fusion.4), calls=%async_computation.3 | async-start | bytes 2097152 | tf_op jit(solution)/shard_map/all_to_all | solution.py:177
  81.2 46.0 %copy-start.11 = (s32[16]{0:T(128)S(1)}, s32[16]{0:T(128)}, u32[]{:S(2)}) copy-start(s32[16]{0:T(128)} %param.20) | copy-start | bytes 196
  119.6 243.4 %all-to-all-start = ((bf16[64,128,512]{2,1,0:T(8,128)(2,1)}), bf16[64,128,512]{2,1,0:T(8,128)(2,1)}, u32[]{:S(2)}, u32[]{:S(2)}) async-start(bf16[64,128,512]{2,1,0:T(8,128)(2,1)} %gather_fusion.1), calls=%async_computation.1 | async-start | bytes 16777216 | tf_op jit(solution)/shard_map/all_to_all | solution.py:167
  416.6 29.4 %collective-permute-start.1 = (bf16[128,2048]{1,0:T(8,128)(2,1)S(1)}, bf16[128,2048]{1,0:T(8,128)(2,1)S(1)}, u32[]{:S(2)}, u32[]{:S(2)}) collective-permute-start(bf16[128,2048]{1,0:T(8,128)(2,1)S(1)} %bitcast_dynamic-update-slice_fusion.8), channel_id=1, source_target_pairs={{0,8},{8,16},{16,24},{24,28},{28,20},{20,12},{12,4},{4,0},{1,9},{9... | collective-permute-start | bytes 1572872 | tf_op jit(solution)/shard_map/ppermute | solution.py:241
  441.0 13.3 %collective-permute-start.3 = (bf16[128,2048]{1,0:T(8,128)(2,1)S(1)}, bf16[128,2048]{1,0:T(8,128)(2,1)S(1)}, u32[]{:S(2)}, u32[]{:S(2)}) collective-permute-start(bf16[128,2048]{1,0:T(8,128)(2,1)S(1)} %bitcast_dynamic-update-slice_fusion.8), channel_id=1, source_target_pairs={{0,4},{8,0},{16,8},{24,16},{28,24},{20,28},{12,20},{4,12},{1,5},{9... | collective-permute-start | bytes 1572872 | tf_op jit(solution)/shard_map/ppermute | solution.py:243
  446.0 10.9 %collective-permute-start = (f32[128,1024]{1,0:T(8,128)S(1)}, f32[128,1024]{1,0:T(8,128)S(1)}, u32[]{:S(2)}, u32[]{:S(2)}) collective-permute-start(f32[128,1024]{1,0:T(8,128)S(1)} %fusion.140), channel_id=1, source_target_pairs={{0,1},{1,0},{2,3},{3,2},{4,5},{5,4},{6,7},{7,6},{8,9},{9,8},{10,11... | collective-permute-start | bytes 1572872 | tf_op jit(solution)/shard_map/ppermute | solution.py:230
  446.8 23.5 %collective-permute-start.2 = (f32[128,1024]{1,0:T(8,128)S(1)}, f32[128,1024]{1,0:T(8,128)S(1)}, u32[]{:S(2)}, u32[]{:S(2)}) collective-permute-start(f32[128,1024]{1,0:T(8,128)S(1)} %fusion.141), channel_id=1, source_target_pairs={{0,1},{1,0},{2,3},{3,2},{4,5},{5,4},{6,7},{7,6},{8,9},{9,8},{10,11... | collective-permute-start | bytes 1572872 | tf_op jit(solution)/shard_map/ppermute | solution.py:230
  447.4 13.9 %collective-permute-start.5 = (bf16[128,2048]{1,0:T(8,128)(2,1)S(1)}, bf16[128,2048]{1,0:T(8,128)(2,1)S(1)}, u32[]{:S(2)}, u32[]{:S(2)}) collective-permute-start(bf16[128,2048]{1,0:T(8,128)(2,1)S(1)} %collective-permute-done.1), channel_id=1, source_target_pairs={{0,8},{8,16},{16,24},{24,28},{28,20},{20,12},{12,4},{4,0},{1,9},{9... | collective-permute-start | bytes 1572872 | tf_op jit(solution)/shard_map/ppermute | solution.py:241
  455.0 17.4 %collective-permute-start.4 = (f32[128,1024]{1,0:T(8,128)S(1)}, f32[128,1024]{1,0:T(8,128)S(1)}, u32[]{:S(2)}, u32[]{:S(2)}) collective-permute-start(f32[128,1024]{1,0:T(8,128)S(1)} %fusion.142), channel_id=1, source_target_pairs={{0,1},{1,0},{2,3},{3,2},{4,5},{5,4},{6,7},{7,6},{8,9},{9,8},{10,11... | collective-permute-start | bytes 1572872 | tf_op jit(solution)/shard_map/ppermute | solution.py:230
  455.1 14.3 %collective-permute-start.7 = (bf16[128,2048]{1,0:T(8,128)(2,1)S(1)}, bf16[128,2048]{1,0:T(8,128)(2,1)S(1)}, u32[]{:S(2)}, u32[]{:S(2)}) collective-permute-start(bf16[128,2048]{1,0:T(8,128)(2,1)S(1)} %collective-permute-done.3), channel_id=1, source_target_pairs={{0,4},{8,0},{16,8},{24,16},{28,24},{20,28},{12,20},{4,12},{1,5},{9... | collective-permute-start | bytes 1572872 | tf_op jit(solution)/shard_map/ppermute | solution.py:243
  462.0 26.3 %collective-permute-start.6 = (f32[128,1024]{1,0:T(8,128)S(1)}, f32[128,1024]{1,0:T(8,128)S(1)}, u32[]{:S(2)}, u32[]{:S(2)}) collective-permute-start(f32[128,1024]{1,0:T(8,128)S(1)} %fusion.143), channel_id=1, source_target_pairs={{0,1},{1,0},{2,3},{3,2},{4,5},{5,4},{6,7},{7,6},{8,9},{9,8},{10,11... | collective-permute-start | bytes 1572872 | tf_op jit(solution)/shard_map/ppermute | solution.py:230
  470.2 18.8 %collective-permute-start.8 = (f32[128,1024]{1,0:T(8,128)S(1)}, f32[128,1024]{1,0:T(8,128)S(1)}, u32[]{:S(2)}, u32[]{:S(2)}) collective-permute-start(f32[128,1024]{1,0:T(8,128)S(1)} %fusion.144), channel_id=1, source_target_pairs={{0,1},{1,0},{2,3},{3,2},{4,5},{5,4},{6,7},{7,6},{8,9},{9,8},{10,11... | collective-permute-start | bytes 1572872 | tf_op jit(solution)/shard_map/ppermute | solution.py:230
  470.2 14.3 %collective-permute-start.9 = (bf16[128,2048]{1,0:T(8,128)(2,1)S(1)}, bf16[128,2048]{1,0:T(8,128)(2,1)S(1)}, u32[]{:S(2)}, u32[]{:S(2)}) collective-permute-start(bf16[128,2048]{1,0:T(8,128)(2,1)S(1)} %collective-permute-done.5), channel_id=1, source_target_pairs={{0,8},{8,16},{16,24},{24,28},{28,20},{20,12},{12,4},{4,0},{1,9},{9... | collective-permute-start | bytes 1572872 | tf_op jit(solution)/shard_map/ppermute | solution.py:241
  470.3 14.6 %collective-permute-start.11 = (bf16[128,2048]{1,0:T(8,128)(2,1)S(1)}, bf16[128,2048]{1,0:T(8,128)(2,1)S(1)}, u32[]{:S(2)}, u32[]{:S(2)}) collective-permute-start(bf16[128,2048]{1,0:T(8,128)(2,1)S(1)} %collective-permute-done.7), channel_id=1, source_target_pairs={{0,4},{8,0},{16,8},{24,16},{28,24},{20,28},{12,20},{4,12},{1,5},{9... | collective-permute-start | bytes 1572872 | tf_op jit(solution)/shard_map/ppermute | solution.py:243
  484.6 7.9 %collective-permute-start.13 = (bf16[64,2048]{1,0:T(8,128)(2,1)S(1)}, bf16[64,2048]{1,0:T(8,128)(2,1)S(1)}, u32[]{:S(2)}, u32[]{:S(2)}) collective-permute-start(bf16[64,2048]{1,0:T(8,128)(2,1)S(1)} %slice.256), channel_id=1, source_target_pairs={{0,8},{8,16},{16,24},{24,28},{28,20},{20,12},{12,4},{4,0},{1,9},{9... | collective-permute-start | bytes 786440 | tf_op jit(solution)/shard_map/ppermute | solution.py:246
  484.9 7.8 %collective-permute-start.14 = (bf16[64,2048]{1,0:T(8,128)(2,1)S(1)}, bf16[64,2048]{1,0:T(8,128)(2,1)S(1)}, u32[]{:S(2)}, u32[]{:S(2)}) collective-permute-start(bf16[64,2048]{1,0:T(8,128)(2,1)S(1)} %slice.257), channel_id=1, source_target_pairs={{0,4},{8,0},{16,8},{24,16},{28,24},{20,28},{12,20},{4,12},{1,5},{9... | collective-permute-start | bytes 786440 | tf_op jit(solution)/shard_map/ppermute | solution.py:247
  487.5 6.1 %collective-permute-start.10 = (f32[128,1024]{1,0:T(8,128)S(1)}, f32[128,1024]{1,0:T(8,128)S(1)}, u32[]{:S(2)}, u32[]{:S(2)}) collective-permute-start(f32[128,1024]{1,0:T(8,128)S(1)} %fusion.145), channel_id=1, source_target_pairs={{0,1},{1,0},{2,3},{3,2},{4,5},{5,4},{6,7},{7,6},{8,9},{9,8},{10,11... | collective-permute-start | bytes 1572872 | tf_op jit(solution)/shard_map/ppermute | solution.py:230
  488.3 5.4 %collective-permute-start.12 = (f32[128,1024]{1,0:T(8,128)S(1)}, f32[128,1024]{1,0:T(8,128)S(1)}, u32[]{:S(2)}, u32[]{:S(2)}) collective-permute-start(f32[128,1024]{1,0:T(8,128)S(1)} %fusion.146), channel_id=1, source_target_pairs={{0,1},{1,0},{2,3},{3,2},{4,5},{5,4},{6,7},{7,6},{8,9},{9,8},{10,11... | collective-permute-start | bytes 1572872 | tf_op jit(solution)/shard_map/ppermute | solution.py:230
  493.5 2.0 collective-permute-start.15
  493.7 19.7 %copy-start.1 = (bf16[2,8,128,512]{3,2,1,0:T(8,128)(2,1)S(1)}, bf16[2,8,128,512]{3,2,1,0:T(8,128)(2,1)}, u32[]{:S(2)}) copy-start(bf16[2,8,128,512]{3,2,1,0:T(8,128)(2,1)} %param.16) | copy-start | bytes 6291460
  497.1 14.0 %collective-permute-start.16 = (bf16[1,256,1024]{2,1,0:T(8,128)(2,1)S(1)}, bf16[1,256,1024]{2,1,0:T(8,128)(2,1)S(1)}, u32[]{:S(2)}, u32[]{:S(2)}) collective-permute-start(bf16[1,256,1024]{2,1,0:T(8,128)(2,1)S(1)} %fusion.53), channel_id=1, source_target_pairs={{0,2},{1,3},{2,0},{3,1},{4,6},{5,7},{6,4},{7,5},{8,10},{9,11},{10,... | collective-permute-start | bytes 1572872 | tf_op jit(solution)/shard_map/ppermute | solution.py:288
  (10 other events, 54.1 us)
Sparse Core Ops, SparseCore 0:
  37.4 346.6 reduce-scatter.1

commit v13 on v11

--- a/solution.py
+++ b/solution.py
@@ -276,9 +276,19 @@
         mine = (me // bit) % 2
         keep = lax.dynamic_index_in_dim(grouped, mine, 1, keepdims=False)
         send = lax.dynamic_index_in_dim(grouped, 1 - mine, 1, keepdims=False)
+        partners = [(j, j ^ bit) for j in range(size)]
         if bit > 1:
             send = send.astype(jnp.bfloat16)
-        received = lax.ppermute(send, axis_name, [(j, j ^ bit) for j in range(size)])
+            cut = send.shape[-1] // 2
+            received = jnp.concatenate(
+                [
+                    lax.ppermute(send[..., :cut], axis_name, partners),
+                    lax.ppermute(send[..., cut:], axis_name, partners),
+                ],
+                -1,
+            )
+        else:
+            received = lax.ppermute(send, axis_name, partners)
         held = (keep + received.astype(jnp.float32)).reshape(blocks // 2 * rows, cols)
         bit *= 2
     return held

time: 516 us -> 516 us (level)
    ppermute x2 -> x3, waiting for transfers between devices: 17 us -> 16.4 us  [the longest x1 7.15 us: halving_sum(): lax.ppermute(send[..., cut:], axis_name, partners)]
  transfers between devices with their start and end apart: 14 -> 15, of which waited for: 9 -> 10; matrix products, arithmetic and copies ran while one was open for 15% -> 15% of each run, Pallas kernels for 0% -> 0%
where the time goes in v13:
time: 516 us; the launch traced here: 509 us
  waiting for transfers between devices  321 us (62%)
  local copies, waits for them, and re-layouts  62.3 us (12%)
  matrix products  34.9 us (7%)
  between operations  32.2 us (6%)
  other arithmetic  31.4 us (6%)
  starting transfers between devices  27.1 us (5%)
    all_to_all x1, waiting for transfers between devices, body(): lax.all_to_all(kv_pool[pack_index], 'pool', split_axis=0, concat_axis=0,...  219 us
    all_to_all x1, waiting for transfers between devices, body(): lax.all_to_all(spread[hot_owner], 'pool', split_axis=0, concat_axis=0, ti...  38.4 us
    all_to_all x1, waiting for transfers between devices, body(): lax.all_to_all(kv_pool[extra_index].reshape(pool_size, piece_rows, kv_col...  25.7 us
    ppermute x3, waiting for transfers between devices, ring_product(): ahead = lax.ppermute(ahead, axis_name, forward)  17.6 us
    select_n x2, other arithmetic, body(): jnp.where((numbers < my_resident[local_user])[:, None, None], resident_pa...  13.9 us
    gather x2, local copies, waits for them, and re-layouts, body(): regular_pages = arrived[owner * capacity + jnp.minimum(rank, capacity - 1)]  12.5 us
    dot_general x1, matrix products, body(): jnp.dot(draft_states, w_qkv, preferred_element_type=jnp.float32)  10.9 us
  transfers between devices with their start and end apart: 15, of which 10 were waited for; matrix products, arithmetic and copies ran while one was open for 15% of the time, Pallas kernels for 0%

profile of v13, /device:TPU:0, one launch (start us, length us, event | category | flops | bytes accessed | tf_op | source)
XLA Modules:
  0.0 508.7 jit_solution(14241728625945616547)
XLA Ops:
  13.4 5.6 %gather_fusion.3 = bf16[8,128,512]{2,1,0:T(8,128)(2,1)} fusion(bf16[80,128,512]{2,1,0:T(8,128)(2,1)} %param.15, s32[1024]{0:T(1024)S(1)} %pad_clamp_fusion.5), kind=kCustom, calls=%fused_computation.3 | custom fusion | bytes 2097184 | tf_op jit(solution)/shard_map/gather | solution.py:171
  19.0 7.3 %all-to-all-start.1 = ((bf16[8,128,512]{2,1,0:T(8,128)(2,1)}), bf16[8,128,512]{2,1,0:T(8,128)(2,1)S(1)}, u32[]{:S(2)}, u32[]{:S(2)}) async-start(bf16[8,128,512]{2,1,0:T(8,128)(2,1)} %gather_fusion.3), calls=%async_computation.2 | async-start | bytes 2097152 | tf_op jit(solution)/shard_map/all_to_all | solution.py:170
  26.3 10.9 %fusion.145 = f32[1024,2560]{1,0:T(8,128)} fusion(bf16[1024,1024]{1,0:T(8,128)(2,1)} %param.12, bf16[1024,2560]{1,0:T(8,128)(2,1)} %param.13), kind=kOutput, calls=%fused_computation.271 | convolution fusion | flops 5368709120 | bytes 17825792 | tf_op jit(solution)/shard_map/dot_general | solution.py:124
  38.1 25.7 %all-to-all-done.1 = bf16[8,128,512]{2,1,0:T(8,128)(2,1)S(1)} async-done(((bf16[8,128,512]{2,1,0:T(8,128)(2,1)}), bf16[8,128,512]{2,1,0:T(8,128)(2,1)S(1)}, u32[]{:S(2)}, u32[]{:S(2)}) %all-to-all-start.1) | async-done | bytes 1048608 | tf_op jit(solution)/shard_map/all_to_all | solution.py:170
  65.4 3.6 all-to-all-start.2
  71.4 9.7 %gather_fusion.1 = bf16[64,128,512]{2,1,0:T(8,128)(2,1)} fusion(bf16[80,128,512]{2,1,0:T(8,128)(2,1)} %param.15, s32[1024]{0:T(1024)S(1)} %pad_clamp_fusion.7), kind=kCustom, calls=%fused_computation.1 | custom fusion | bytes 16777472 | tf_op jit(solution)/shard_map/gather | solution.py:168
  81.2 38.4 %all-to-all-done.2 = bf16[8,128,512]{2,1,0:T(8,128)(2,1)S(1)} async-done(((bf16[8,128,512]{2,1,0:T(8,128)(2,1)}), bf16[8,128,512]{2,1,0:T(8,128)(2,1)S(1)}, u32[]{:S(2)}, u32[]{:S(2)}) %all-to-all-start.2) | async-done | bytes 1048608 | tf_op jit(solution)/shard_map/all_to_all | solution.py:177
  119.6 5.6 %all-to-all-start = ((bf16[64,128,512]{2,1,0:T(8,128)(2,1)}), bf16[64,128,512]{2,1,0:T(8,128)(2,1)}, u32[]{:S(2)}, u32[]{:S(2)}) async-start(bf16[64,128,512]{2,1,0:T(8,128)(2,1)} %gather_fusion.1), calls=%async_computation.1 | async-start | bytes 16777216 | tf_op jit(solution)/shard_map/all_to_all | solution.py:167
  127.4 2.8 gather_fusion.6
  130.2 2.9 gather_fusion
  138.0 2.8 gather_fusion.8
  143.5 219.4 %all-to-all-done = bf16[64,128,512]{2,1,0:T(8,128)(2,1)} async-done(((bf16[64,128,512]{2,1,0:T(8,128)(2,1)}), bf16[64,128,512]{2,1,0:T(8,128)(2,1)}, u32[]{:S(2)}, u32[]{:S(2)}) %all-to-all-start) | async-done | bytes 8388640 | tf_op jit(solution)/shard_map/all_to_all | solution.py:167
  363.0 6.3 %gather_fusion.7 = bf16[32,128,512]{2,1,0:T(8,128)(2,1)} fusion(bf16[64,128,512]{2,1,0:T(8,128)(2,1)} %all-to-all-done, s32[1024]{0:T(1024)S(1)} %pad_clamp_fusion.1), kind=kCustom, calls=%fused_computation.7 | custom fusion | bytes 8388736 | tf_op jit(solution)/shard_map/gather | solution.py:193
  369.2 6.3 %gather_fusion.2 = bf16[32,128,512]{2,1,0:T(8,128)(2,1)} fusion(bf16[64,128,512]{2,1,0:T(8,128)(2,1)} %all-to-all-done, s32[1024]{0:T(1024)S(1)} %pad_clamp_fusion.6), kind=kCustom, calls=%fused_computation.2 | custom fusion | bytes 8388736 | tf_op jit(solution)/shard_map/gather | solution.py:193
  375.5 9.5 %fusion.8 = bf16[4096,512]{1,0:T(8,128)(2,1)} fusion(bf16[32,128,512]{2,1,0:T(8,128)(2,1)} %gather_fusion.8, bf16[32,128,512]{2,1,0:T(8,128)(2,1)} %gather_fusion.7, bf16[32,128,512]{2,1,0:T(8,128)(2,1)} %gather_fusion.6, pred[4096]{0:T(1024)(128)(4,1)S(1)} %get-tuple-element.80, pred[4096]{0:T(1024)(128)(4,1)S(1)} %broadcast_bitcast_fusion.3), kind=kLoop, calls=%fused_computation.28 | loop fusion | flops 4194304 | bytes 16785408 | tf_op jit(solution)/shard_map/jit(_where)/select_n | solution.py:195
  385.5 4.4 fusion.9
  395.4 3.3 fusion.4
  406.7 3.3 fusion
  444.6 9.1 %collective-permute-done.2 = bf16[128,2048]{1,0:T(8,128)(2,1)S(1)} collective-permute-done((bf16[128,2048]{1,0:T(8,128)(2,1)S(1)}, bf16[128,2048]{1,0:T(8,128)(2,1)S(1)}, u32[]{:S(2)}, u32[]{:S(2)}) %collective-permute-start.2) | collective-permute-done | bytes 524320 | tf_op jit(solution)/shard_map/ppermute | solution.py:233
  457.3 8.5 %collective-permute-done.4 = bf16[128,2048]{1,0:T(8,128)(2,1)S(1)} collective-permute-done((bf16[128,2048]{1,0:T(8,128)(2,1)S(1)}, bf16[128,2048]{1,0:T(8,128)(2,1)S(1)}, u32[]{:S(2)}, u32[]{:S(2)}) %collective-permute-start.4) | collective-permute-done | bytes 524320 | tf_op jit(solution)/shard_map/ppermute | solution.py:233
  469.4 2.8 collective-permute-done.6
  476.8 4.5 collective-permute-done.8
  487.5 7.1 %collective-permute-done.10 = bf16[1,256,512]{2,1,0:T(8,128)(2,1)S(1)} collective-permute-done((bf16[1,256,512]{2,1,0:T(8,128)(2,1)S(1)}, bf16[1,256,512]{2,1,0:T(8,128)(2,1)S(1)}, u32[]{:S(2)}, u32[]{:S(2)}) %collective-permute-start.10) | collective-permute-done | bytes 262176 | tf_op jit(solution)/shard_map/ppermute | solution.py:286
  494.7 4.8 collective-permute-done.9
  (167 shorter events, 72.0 us)
Async XLA Ops:
  6.5 120.9 %copy-start = (bf16[2,8,128,512]{3,2,1,0:T(8,128)(2,1)S(1)}, bf16[2,8,128,512]{3,2,1,0:T(8,128)(2,1)}, u32[]{:S(2)}) copy-start(bf16[2,8,128,512]{3,2,1,0:T(8,128)(2,1)} %param.16) | copy-start | bytes 6291460
  19.0 44.8 %all-to-all-start.1 = ((bf16[8,128,512]{2,1,0:T(8,128)(2,1)}), bf16[8,128,512]{2,1,0:T(8,128)(2,1)S(1)}, u32[]{:S(2)}, u32[]{:S(2)}) async-start(bf16[8,128,512]{2,1,0:T(8,128)(2,1)} %gather_fusion.3), calls=%async_computation.2 | async-start | bytes 2097152 | tf_op jit(solution)/shard_map/all_to_all | solution.py:170
  26.3 363.6 %reduce-scatter.2.cloned.1.call-start = ((), (), s32[]{:S(2)}) async-start(), calls=%async_computation.4 | async-start | bytes 11796480 | tf_op jit(solution)/shard_map/reduce_scatter | solution.py:123
  65.4 54.1 %all-to-all-start.2 = ((bf16[8,128,512]{2,1,0:T(8,128)(2,1)}), bf16[8,128,512]{2,1,0:T(8,128)(2,1)S(1)}, u32[]{:S(2)}, u32[]{:S(2)}) async-start(bf16[8,128,512]{2,1,0:T(8,128)(2,1)} %gather_fusion.4), calls=%async_computation.3 | async-start | bytes 2097152 | tf_op jit(solution)/shard_map/all_to_all | solution.py:177
  81.2 46.0 %copy-start.12 = (s32[16]{0:T(128)S(1)}, s32[16]{0:T(128)}, u32[]{:S(2)}) copy-start(s32[16]{0:T(128)} %param.20) | copy-start | bytes 196
  119.6 243.4 %all-to-all-start = ((bf16[64,128,512]{2,1,0:T(8,128)(2,1)}), bf16[64,128,512]{2,1,0:T(8,128)(2,1)}, u32[]{:S(2)}, u32[]{:S(2)}) async-start(bf16[64,128,512]{2,1,0:T(8,128)(2,1)} %gather_fusion.1), calls=%async_computation.1 | async-start | bytes 16777216 | tf_op jit(solution)/shard_map/all_to_all | solution.py:167
  130.2 5.2 %copy-start.11 = (s32[16]{0:T(128)S(1)}, s32[16]{0:T(128)}, u32[]{:S(2)}) copy-start(s32[16]{0:T(128)} %param.19) | copy-start | bytes 196
  375.5 9.6 %copy-start.4 = (bf16[32,128,512]{2,1,0:T(8,128)(2,1)S(1)}, bf16[32,128,512]{2,1,0:T(8,128)(2,1)}, u32[]{:S(2)}) copy-start(bf16[32,128,512]{2,1,0:T(8,128)(2,1)} %gather_fusion) | copy-start | bytes 12582916
  375.5 9.6 %copy-start.5 = (bf16[32,128,512]{2,1,0:T(8,128)(2,1)S(1)}, bf16[32,128,512]{2,1,0:T(8,128)(2,1)}, u32[]{:S(2)}) copy-start(bf16[32,128,512]{2,1,0:T(8,128)(2,1)} %gather_fusion.5) | copy-start | bytes 12582916
  375.5 10.0 %copy-start.6 = (bf16[32,128,512]{2,1,0:T(8,128)(2,1)S(1)}, bf16[32,128,512]{2,1,0:T(8,128)(2,1)}, u32[]{:S(2)}) copy-start(bf16[32,128,512]{2,1,0:T(8,128)(2,1)} %gather_fusion.2) | copy-start | bytes 12582916
  415.1 3.9 copy-start.13
  415.1 9.1 %copy-start.10 = (s32[8]{0:T(128)S(1)}, s32[8]{0:T(128)}, u32[]{:S(2)}) copy-start(s32[8]{0:T(128)} %constant.198.clone) | copy-start | bytes 100
  416.7 24.4 %collective-permute-start = (bf16[128,2048]{1,0:T(8,128)(2,1)S(1)}, bf16[128,2048]{1,0:T(8,128)(2,1)S(1)}, u32[]{:S(2)}, u32[]{:S(2)}) collective-permute-start(bf16[128,2048]{1,0:T(8,128)(2,1)S(1)} %bitcast_dynamic-update-slice_fusion), channel_id=1, source_target_pairs={{0,8},{8,16},{16,24},{24,28},{28,20},{20,12},{12,4},{4,0},{1,9},{9... | collective-permute-start | bytes 1572872 | tf_op jit(solution)/shard_map/ppermute | solution.py:233
  416.7 24.5 %collective-permute-start.1 = (bf16[128,2048]{1,0:T(8,128)(2,1)S(1)}, bf16[128,2048]{1,0:T(8,128)(2,1)S(1)}, u32[]{:S(2)}, u32[]{:S(2)}) collective-permute-start(bf16[128,2048]{1,0:T(8,128)(2,1)S(1)} %bitcast_dynamic-update-slice_fusion), channel_id=1, source_target_pairs={{0,4},{8,0},{16,8},{24,16},{28,24},{20,28},{12,20},{4,12},{1,5},{9... | collective-permute-start | bytes 1572872 | tf_op jit(solution)/shard_map/ppermute | solution.py:235
  441.0 12.7 %collective-permute-start.2 = (bf16[128,2048]{1,0:T(8,128)(2,1)S(1)}, bf16[128,2048]{1,0:T(8,128)(2,1)S(1)}, u32[]{:S(2)}, u32[]{:S(2)}) collective-permute-start(bf16[128,2048]{1,0:T(8,128)(2,1)S(1)} %collective-permute-done), channel_id=1, source_target_pairs={{0,8},{8,16},{16,24},{24,28},{28,20},{20,12},{12,4},{4,0},{1,9},{9... | collective-permute-start | bytes 1572872 | tf_op jit(solution)/shard_map/ppermute | solution.py:233
  441.2 12.9 %collective-permute-start.3 = (bf16[128,2048]{1,0:T(8,128)(2,1)S(1)}, bf16[128,2048]{1,0:T(8,128)(2,1)S(1)}, u32[]{:S(2)}, u32[]{:S(2)}) collective-permute-start(bf16[128,2048]{1,0:T(8,128)(2,1)S(1)} %collective-permute-done.1), channel_id=1, source_target_pairs={{0,4},{8,0},{16,8},{24,16},{28,24},{20,28},{12,20},{4,12},{1,5},{9... | collective-permute-start | bytes 1572872 | tf_op jit(solution)/shard_map/ppermute | solution.py:235
  453.7 12.0 %collective-permute-start.4 = (bf16[128,2048]{1,0:T(8,128)(2,1)S(1)}, bf16[128,2048]{1,0:T(8,128)(2,1)S(1)}, u32[]{:S(2)}, u32[]{:S(2)}) collective-permute-start(bf16[128,2048]{1,0:T(8,128)(2,1)S(1)} %collective-permute-done.2), channel_id=1, source_target_pairs={{0,8},{8,16},{16,24},{24,28},{28,20},{20,12},{12,4},{4,0},{1,9},{9... | collective-permute-start | bytes 1572872 | tf_op jit(solution)/shard_map/ppermute | solution.py:233
  454.1 12.1 %collective-permute-start.5 = (bf16[128,2048]{1,0:T(8,128)(2,1)S(1)}, bf16[128,2048]{1,0:T(8,128)(2,1)S(1)}, u32[]{:S(2)}, u32[]{:S(2)}) collective-permute-start(bf16[128,2048]{1,0:T(8,128)(2,1)S(1)} %collective-permute-done.3), channel_id=1, source_target_pairs={{0,4},{8,0},{16,8},{24,16},{28,24},{20,28},{12,20},{4,12},{1,5},{9... | collective-permute-start | bytes 1572872 | tf_op jit(solution)/shard_map/ppermute | solution.py:235
  465.8 6.4 %collective-permute-start.6 = (bf16[64,2048]{1,0:T(8,128)(2,1)S(1)}, bf16[64,2048]{1,0:T(8,128)(2,1)S(1)}, u32[]{:S(2)}, u32[]{:S(2)}) collective-permute-start(bf16[64,2048]{1,0:T(8,128)(2,1)S(1)} %slice.260), channel_id=1, source_target_pairs={{0,8},{8,16},{16,24},{24,28},{28,20},{20,12},{12,4},{4,0},{1,9},{9... | collective-permute-start | bytes 786440 | tf_op jit(solution)/shard_map/ppermute | solution.py:238
  466.3 6.4 %collective-permute-start.7 = (bf16[64,2048]{1,0:T(8,128)(2,1)S(1)}, bf16[64,2048]{1,0:T(8,128)(2,1)S(1)}, u32[]{:S(2)}, u32[]{:S(2)}) collective-permute-start(bf16[64,2048]{1,0:T(8,128)(2,1)S(1)} %slice.261), channel_id=1, source_target_pairs={{0,4},{8,0},{16,8},{24,16},{28,24},{20,28},{12,20},{4,12},{1,5},{9... | collective-permute-start | bytes 786440 | tf_op jit(solution)/shard_map/ppermute | solution.py:239
  476.8 4.5 collective-permute-start.8
  476.8 24.8 %copy-start.1 = (bf16[2,8,128,512]{3,2,1,0:T(8,128)(2,1)S(1)}, bf16[2,8,128,512]{3,2,1,0:T(8,128)(2,1)}, u32[]{:S(2)}) copy-start(bf16[2,8,128,512]{3,2,1,0:T(8,128)(2,1)} %param.16) | copy-start | bytes 6291460
  485.4 9.2 %collective-permute-start.10 = (bf16[1,256,512]{2,1,0:T(8,128)(2,1)S(1)}, bf16[1,256,512]{2,1,0:T(8,128)(2,1)S(1)}, u32[]{:S(2)}, u32[]{:S(2)}) collective-permute-start(bf16[1,256,512]{2,1,0:T(8,128)(2,1)S(1)} %get-tuple-element.32), channel_id=1, source_target_pairs={{0,2},{1,3},{2,0},{3,1},{4,6},{5,7},{6,4},{7,5},{8,10},{9,11},{10,... | collective-permute-start | bytes 786440 | tf_op jit(solution)/shard_map/ppermute | solution.py:286
  486.9 12.5 %collective-permute-start.9 = (bf16[1,256,512]{2,1,0:T(8,128)(2,1)S(1)}, bf16[1,256,512]{2,1,0:T(8,128)(2,1)S(1)}, u32[]{:S(2)}, u32[]{:S(2)}) collective-permute-start(bf16[1,256,512]{2,1,0:T(8,128)(2,1)S(1)} %get-tuple-element.31), channel_id=1, source_target_pairs={{0,2},{1,3},{2,0},{3,1},{4,6},{5,7},{6,4},{7,5},{8,10},{9,11},{10,... | collective-permute-start | bytes 786440 | tf_op jit(solution)/shard_map/ppermute | solution.py:285
  (5 other events, 9.8 us)
Sparse Core Ops, SparseCore 0:
  37.4 346.6 reduce-scatter.1

commit v14 on v11

--- a/solution.py
+++ b/solution.py
@@ -276,8 +276,7 @@
         mine = (me // bit) % 2
         keep = lax.dynamic_index_in_dim(grouped, mine, 1, keepdims=False)
         send = lax.dynamic_index_in_dim(grouped, 1 - mine, 1, keepdims=False)
-        if bit > 1:
-            send = send.astype(jnp.bfloat16)
+        send = send.astype(jnp.bfloat16)
         received = lax.ppermute(send, axis_name, [(j, j ^ bit) for j in range(size)])
         held = (keep + received.astype(jnp.float32)).reshape(blocks // 2 * rows, cols)
         bit *= 2

time: 516 us -> 513 us (level)
  no operation moved by 1% of the time
where the time goes in v14:
time: 513 us; the launch traced here: 505 us
  waiting for transfers between devices  320 us (62%)
  local copies, waits for them, and re-layouts  60.9 us (12%)
  matrix products  34.9 us (7%)
  between operations  32.3 us (6%)
  other arithmetic  31 us (6%)
  starting transfers between devices  26.6 us (5%)
    all_to_all x1, waiting for transfers between devices, body(): lax.all_to_all(kv_pool[pack_index], 'pool', split_axis=0, concat_axis=0,...  219 us
    all_to_all x1, waiting for transfers between devices, body(): lax.all_to_all(spread[hot_owner], 'pool', split_axis=0, concat_axis=0, ti...  38.4 us
    all_to_all x1, waiting for transfers between devices, body(): lax.all_to_all(kv_pool[extra_index].reshape(pool_size, piece_rows, kv_col...  25.7 us
    ppermute x3, waiting for transfers between devices, ring_product(): ahead = lax.ppermute(ahead, axis_name, forward)  17.6 us
    ppermute x2, waiting for transfers between devices, halving_sum(): lax.ppermute(send, axis_name, [(j, j ^ bit) for j in range(size)])  15.2 us
    select_n x2, other arithmetic, body(): jnp.where((numbers < my_resident[local_user])[:, None, None], resident_pa...  13.9 us
    gather x2, local copies, waits for them, and re-layouts, body(): regular_pages = arrived[owner * capacity + jnp.minimum(rank, capacity - 1)]  12.5 us
    dot_general x1, matrix products, body(): jnp.dot(draft_states, w_qkv, preferred_element_type=jnp.float32)  10.9 us
  transfers between devices with their start and end apart: 14, of which 9 were waited for; matrix products, arithmetic and copies ran while one was open for 15% of the time, Pallas kernels for 0%

profile of v14, /device:TPU:0, one launch (start us, length us, event | category | flops | bytes accessed | tf_op | source)
XLA Modules:
  0.0 505.3 jit_solution(18311686085081552417)
XLA Ops:
  13.4 5.6 %gather_fusion.3 = bf16[8,128,512]{2,1,0:T(8,128)(2,1)} fusion(bf16[80,128,512]{2,1,0:T(8,128)(2,1)} %param.15, s32[1024]{0:T(1024)S(1)} %pad_clamp_fusion.5), kind=kCustom, calls=%fused_computation.3 | custom fusion | bytes 2097184 | tf_op jit(solution)/shard_map/gather | solution.py:171
  19.0 7.3 %all-to-all-start.1 = ((bf16[8,128,512]{2,1,0:T(8,128)(2,1)}), bf16[8,128,512]{2,1,0:T(8,128)(2,1)S(1)}, u32[]{:S(2)}, u32[]{:S(2)}) async-start(bf16[8,128,512]{2,1,0:T(8,128)(2,1)} %gather_fusion.3), calls=%async_computation.2 | async-start | bytes 2097152 | tf_op jit(solution)/shard_map/all_to_all | solution.py:170
  26.3 10.9 %fusion.145 = f32[1024,2560]{1,0:T(8,128)} fusion(bf16[1024,1024]{1,0:T(8,128)(2,1)} %param.12, bf16[1024,2560]{1,0:T(8,128)(2,1)} %param.13), kind=kOutput, calls=%fused_computation.271 | convolution fusion | flops 5368709120 | bytes 17825792 | tf_op jit(solution)/shard_map/dot_general | solution.py:124
  38.1 25.7 %all-to-all-done.1 = bf16[8,128,512]{2,1,0:T(8,128)(2,1)S(1)} async-done(((bf16[8,128,512]{2,1,0:T(8,128)(2,1)}), bf16[8,128,512]{2,1,0:T(8,128)(2,1)S(1)}, u32[]{:S(2)}, u32[]{:S(2)}) %all-to-all-start.1) | async-done | bytes 1048608 | tf_op jit(solution)/shard_map/all_to_all | solution.py:170
  65.4 3.6 all-to-all-start.2
  71.4 9.7 %gather_fusion.1 = bf16[64,128,512]{2,1,0:T(8,128)(2,1)} fusion(bf16[80,128,512]{2,1,0:T(8,128)(2,1)} %param.15, s32[1024]{0:T(1024)S(1)} %pad_clamp_fusion.7), kind=kCustom, calls=%fused_computation.1 | custom fusion | bytes 16777472 | tf_op jit(solution)/shard_map/gather | solution.py:168
  81.2 38.4 %all-to-all-done.2 = bf16[8,128,512]{2,1,0:T(8,128)(2,1)S(1)} async-done(((bf16[8,128,512]{2,1,0:T(8,128)(2,1)}), bf16[8,128,512]{2,1,0:T(8,128)(2,1)S(1)}, u32[]{:S(2)}, u32[]{:S(2)}) %all-to-all-start.2) | async-done | bytes 1048608 | tf_op jit(solution)/shard_map/all_to_all | solution.py:177
  119.6 5.6 %all-to-all-start = ((bf16[64,128,512]{2,1,0:T(8,128)(2,1)}), bf16[64,128,512]{2,1,0:T(8,128)(2,1)}, u32[]{:S(2)}, u32[]{:S(2)}) async-start(bf16[64,128,512]{2,1,0:T(8,128)(2,1)} %gather_fusion.1), calls=%async_computation.1 | async-start | bytes 16777216 | tf_op jit(solution)/shard_map/all_to_all | solution.py:167
  127.4 2.8 gather_fusion.6
  130.2 2.9 gather_fusion
  138.0 2.8 gather_fusion.8
  140.8 2.8 gather_fusion.5
  143.5 219.4 %all-to-all-done = bf16[64,128,512]{2,1,0:T(8,128)(2,1)} async-done(((bf16[64,128,512]{2,1,0:T(8,128)(2,1)}), bf16[64,128,512]{2,1,0:T(8,128)(2,1)}, u32[]{:S(2)}, u32[]{:S(2)}) %all-to-all-start) | async-done | bytes 8388640 | tf_op jit(solution)/shard_map/all_to_all | solution.py:167
  363.0 6.3 %gather_fusion.7 = bf16[32,128,512]{2,1,0:T(8,128)(2,1)} fusion(bf16[64,128,512]{2,1,0:T(8,128)(2,1)} %all-to-all-done, s32[1024]{0:T(1024)S(1)} %pad_clamp_fusion.1), kind=kCustom, calls=%fused_computation.7 | custom fusion | bytes 8388736 | tf_op jit(solution)/shard_map/gather | solution.py:193
  369.2 6.3 %gather_fusion.2 = bf16[32,128,512]{2,1,0:T(8,128)(2,1)} fusion(bf16[64,128,512]{2,1,0:T(8,128)(2,1)} %all-to-all-done, s32[1024]{0:T(1024)S(1)} %pad_clamp_fusion.6), kind=kCustom, calls=%fused_computation.2 | custom fusion | bytes 8388736 | tf_op jit(solution)/shard_map/gather | solution.py:193
  375.5 9.5 %fusion.8 = bf16[4096,512]{1,0:T(8,128)(2,1)} fusion(bf16[32,128,512]{2,1,0:T(8,128)(2,1)} %gather_fusion.8, bf16[32,128,512]{2,1,0:T(8,128)(2,1)} %gather_fusion.7, bf16[32,128,512]{2,1,0:T(8,128)(2,1)} %gather_fusion.6, pred[4096]{0:T(1024)(128)(4,1)S(1)} %get-tuple-element.78, pred[4096]{0:T(1024)(128)(4,1)S(1)} %broadcast_bitcast_fusion.3), kind=kLoop, calls=%fused_computation.28 | loop fusion | flops 4194304 | bytes 16785408 | tf_op jit(solution)/shard_map/jit(_where)/select_n | solution.py:195
  385.5 4.4 fusion.9
  395.4 3.3 fusion.4
  406.7 3.3 fusion
  444.6 9.1 %collective-permute-done.2 = bf16[128,2048]{1,0:T(8,128)(2,1)S(1)} collective-permute-done((bf16[128,2048]{1,0:T(8,128)(2,1)S(1)}, bf16[128,2048]{1,0:T(8,128)(2,1)S(1)}, u32[]{:S(2)}, u32[]{:S(2)}) %collective-permute-start.2) | collective-permute-done | bytes 524320 | tf_op jit(solution)/shard_map/ppermute | solution.py:233
  457.3 8.5 %collective-permute-done.4 = bf16[128,2048]{1,0:T(8,128)(2,1)S(1)} collective-permute-done((bf16[128,2048]{1,0:T(8,128)(2,1)S(1)}, bf16[128,2048]{1,0:T(8,128)(2,1)S(1)}, u32[]{:S(2)}, u32[]{:S(2)}) %collective-permute-start.4) | collective-permute-done | bytes 524320 | tf_op jit(solution)/shard_map/ppermute | solution.py:233
  469.4 2.8 collective-permute-done.6
  475.7 2.7 collective-permute-done.8
  483.5 12.5 %collective-permute-done.9 = bf16[1,256,1024]{2,1,0:T(8,128)(2,1)S(1)} collective-permute-done((bf16[1,256,1024]{2,1,0:T(8,128)(2,1)S(1)}, bf16[1,256,1024]{2,1,0:T(8,128)(2,1)S(1)}, u32[]{:S(2)}, u32[]{:S(2)}) %collective-permute-start.9) | collective-permute-done | bytes 524320 | tf_op jit(solution)/shard_map/ppermute | solution.py:280
  (164 shorter events, 67.0 us)
Async XLA Ops:
  6.5 120.9 %copy-start = (bf16[2,8,128,512]{3,2,1,0:T(8,128)(2,1)S(1)}, bf16[2,8,128,512]{3,2,1,0:T(8,128)(2,1)}, u32[]{:S(2)}) copy-start(bf16[2,8,128,512]{3,2,1,0:T(8,128)(2,1)} %param.16) | copy-start | bytes 6291460
  19.0 44.8 %all-to-all-start.1 = ((bf16[8,128,512]{2,1,0:T(8,128)(2,1)}), bf16[8,128,512]{2,1,0:T(8,128)(2,1)S(1)}, u32[]{:S(2)}, u32[]{:S(2)}) async-start(bf16[8,128,512]{2,1,0:T(8,128)(2,1)} %gather_fusion.3), calls=%async_computation.2 | async-start | bytes 2097152 | tf_op jit(solution)/shard_map/all_to_all | solution.py:170
  26.3 363.6 %reduce-scatter.2.cloned.1.call-start = ((), (), s32[]{:S(2)}) async-start(), calls=%async_computation.4 | async-start | bytes 11796480 | tf_op jit(solution)/shard_map/reduce_scatter | solution.py:123
  65.4 54.1 %all-to-all-start.2 = ((bf16[8,128,512]{2,1,0:T(8,128)(2,1)}), bf16[8,128,512]{2,1,0:T(8,128)(2,1)S(1)}, u32[]{:S(2)}, u32[]{:S(2)}) async-start(bf16[8,128,512]{2,1,0:T(8,128)(2,1)} %gather_fusion.4), calls=%async_computation.3 | async-start | bytes 2097152 | tf_op jit(solution)/shard_map/all_to_all | solution.py:177
  81.2 46.0 %copy-start.12 = (s32[16]{0:T(128)S(1)}, s32[16]{0:T(128)}, u32[]{:S(2)}) copy-start(s32[16]{0:T(128)} %param.20) | copy-start | bytes 196
  119.6 243.4 %all-to-all-start = ((bf16[64,128,512]{2,1,0:T(8,128)(2,1)}), bf16[64,128,512]{2,1,0:T(8,128)(2,1)}, u32[]{:S(2)}, u32[]{:S(2)}) async-start(bf16[64,128,512]{2,1,0:T(8,128)(2,1)} %gather_fusion.1), calls=%async_computation.1 | async-start | bytes 16777216 | tf_op jit(solution)/shard_map/all_to_all | solution.py:167
  130.2 5.2 %copy-start.11 = (s32[16]{0:T(128)S(1)}, s32[16]{0:T(128)}, u32[]{:S(2)}) copy-start(s32[16]{0:T(128)} %param.19) | copy-start | bytes 196
  375.5 9.6 %copy-start.3 = (bf16[32,128,512]{2,1,0:T(8,128)(2,1)S(1)}, bf16[32,128,512]{2,1,0:T(8,128)(2,1)}, u32[]{:S(2)}) copy-start(bf16[32,128,512]{2,1,0:T(8,128)(2,1)} %gather_fusion) | copy-start | bytes 12582916
  375.5 9.6 %copy-start.4 = (bf16[32,128,512]{2,1,0:T(8,128)(2,1)S(1)}, bf16[32,128,512]{2,1,0:T(8,128)(2,1)}, u32[]{:S(2)}) copy-start(bf16[32,128,512]{2,1,0:T(8,128)(2,1)} %gather_fusion.5) | copy-start | bytes 12582916
  375.5 10.0 %copy-start.5 = (bf16[32,128,512]{2,1,0:T(8,128)(2,1)S(1)}, bf16[32,128,512]{2,1,0:T(8,128)(2,1)}, u32[]{:S(2)}) copy-start(bf16[32,128,512]{2,1,0:T(8,128)(2,1)} %gather_fusion.2) | copy-start | bytes 12582916
  415.1 3.9 copy-start.13
  415.1 9.1 %copy-start.10 = (s32[8]{0:T(128)S(1)}, s32[8]{0:T(128)}, u32[]{:S(2)}) copy-start(s32[8]{0:T(128)} %constant.198.clone) | copy-start | bytes 100
  416.7 24.4 %collective-permute-start = (bf16[128,2048]{1,0:T(8,128)(2,1)S(1)}, bf16[128,2048]{1,0:T(8,128)(2,1)S(1)}, u32[]{:S(2)}, u32[]{:S(2)}) collective-permute-start(bf16[128,2048]{1,0:T(8,128)(2,1)S(1)} %bitcast_dynamic-update-slice_fusion), channel_id=1, source_target_pairs={{0,8},{8,16},{16,24},{24,28},{28,20},{20,12},{12,4},{4,0},{1,9},{9... | collective-permute-start | bytes 1572872 | tf_op jit(solution)/shard_map/ppermute | solution.py:233
  416.7 24.5 %collective-permute-start.1 = (bf16[128,2048]{1,0:T(8,128)(2,1)S(1)}, bf16[128,2048]{1,0:T(8,128)(2,1)S(1)}, u32[]{:S(2)}, u32[]{:S(2)}) collective-permute-start(bf16[128,2048]{1,0:T(8,128)(2,1)S(1)} %bitcast_dynamic-update-slice_fusion), channel_id=1, source_target_pairs={{0,4},{8,0},{16,8},{24,16},{28,24},{20,28},{12,20},{4,12},{1,5},{9... | collective-permute-start | bytes 1572872 | tf_op jit(solution)/shard_map/ppermute | solution.py:235
  438.1 2.2 copy-start.2
  441.0 12.7 %collective-permute-start.2 = (bf16[128,2048]{1,0:T(8,128)(2,1)S(1)}, bf16[128,2048]{1,0:T(8,128)(2,1)S(1)}, u32[]{:S(2)}, u32[]{:S(2)}) collective-permute-start(bf16[128,2048]{1,0:T(8,128)(2,1)S(1)} %collective-permute-done), channel_id=1, source_target_pairs={{0,8},{8,16},{16,24},{24,28},{28,20},{20,12},{12,4},{4,0},{1,9},{9... | collective-permute-start | bytes 1572872 | tf_op jit(solution)/shard_map/ppermute | solution.py:233
  441.2 12.9 %collective-permute-start.3 = (bf16[128,2048]{1,0:T(8,128)(2,1)S(1)}, bf16[128,2048]{1,0:T(8,128)(2,1)S(1)}, u32[]{:S(2)}, u32[]{:S(2)}) collective-permute-start(bf16[128,2048]{1,0:T(8,128)(2,1)S(1)} %collective-permute-done.1), channel_id=1, source_target_pairs={{0,4},{8,0},{16,8},{24,16},{28,24},{20,28},{12,20},{4,12},{1,5},{9... | collective-permute-start | bytes 1572872 | tf_op jit(solution)/shard_map/ppermute | solution.py:235
  453.7 12.0 %collective-permute-start.4 = (bf16[128,2048]{1,0:T(8,128)(2,1)S(1)}, bf16[128,2048]{1,0:T(8,128)(2,1)S(1)}, u32[]{:S(2)}, u32[]{:S(2)}) collective-permute-start(bf16[128,2048]{1,0:T(8,128)(2,1)S(1)} %collective-permute-done.2), channel_id=1, source_target_pairs={{0,8},{8,16},{16,24},{24,28},{28,20},{20,12},{12,4},{4,0},{1,9},{9... | collective-permute-start | bytes 1572872 | tf_op jit(solution)/shard_map/ppermute | solution.py:233
  454.1 12.1 %collective-permute-start.5 = (bf16[128,2048]{1,0:T(8,128)(2,1)S(1)}, bf16[128,2048]{1,0:T(8,128)(2,1)S(1)}, u32[]{:S(2)}, u32[]{:S(2)}) collective-permute-start(bf16[128,2048]{1,0:T(8,128)(2,1)S(1)} %collective-permute-done.3), channel_id=1, source_target_pairs={{0,4},{8,0},{16,8},{24,16},{28,24},{20,28},{12,20},{4,12},{1,5},{9... | collective-permute-start | bytes 1572872 | tf_op jit(solution)/shard_map/ppermute | solution.py:235
  465.8 6.4 %collective-permute-start.6 = (bf16[64,2048]{1,0:T(8,128)(2,1)S(1)}, bf16[64,2048]{1,0:T(8,128)(2,1)S(1)}, u32[]{:S(2)}, u32[]{:S(2)}) collective-permute-start(bf16[64,2048]{1,0:T(8,128)(2,1)S(1)} %slice.252), channel_id=1, source_target_pairs={{0,8},{8,16},{16,24},{24,28},{28,20},{20,12},{12,4},{4,0},{1,9},{9... | collective-permute-start | bytes 786440 | tf_op jit(solution)/shard_map/ppermute | solution.py:238
  466.3 6.4 %collective-permute-start.7 = (bf16[64,2048]{1,0:T(8,128)(2,1)S(1)}, bf16[64,2048]{1,0:T(8,128)(2,1)S(1)}, u32[]{:S(2)}, u32[]{:S(2)}) collective-permute-start(bf16[64,2048]{1,0:T(8,128)(2,1)S(1)} %slice.253), channel_id=1, source_target_pairs={{0,4},{8,0},{16,8},{24,16},{28,24},{20,28},{12,20},{4,12},{1,5},{9... | collective-permute-start | bytes 786440 | tf_op jit(solution)/shard_map/ppermute | solution.py:239
  475.5 2.9 collective-permute-start.8
  475.6 22.6 %copy-start.1 = (bf16[2,8,128,512]{3,2,1,0:T(8,128)(2,1)S(1)}, bf16[2,8,128,512]{3,2,1,0:T(8,128)(2,1)}, u32[]{:S(2)}) copy-start(bf16[2,8,128,512]{3,2,1,0:T(8,128)(2,1)} %param.16) | copy-start | bytes 6291460
  482.0 14.0 %collective-permute-start.9 = (bf16[1,256,1024]{2,1,0:T(8,128)(2,1)S(1)}, bf16[1,256,1024]{2,1,0:T(8,128)(2,1)S(1)}, u32[]{:S(2)}, u32[]{:S(2)}) collective-permute-start(bf16[1,256,1024]{2,1,0:T(8,128)(2,1)S(1)} %dynamic-slice_convert_fusion.1), channel_id=1, source_target_pairs={{0,2},{1,3},{2,0},{3,1},{4,6},{5,7},{6,4},{7,5},{8,10},{9,11},{10,... | collective-permute-start | bytes 1572872 | tf_op jit(solution)/shard_map/ppermute | solution.py:280
  (4 other events, 7.7 us)
Sparse Core Ops, SparseCore 0:
  37.4 346.6 reduce-scatter.1
